TPU v7x, 32 devices: a whole 2x2x4 slice. The times are simulated.
32 devices in a mesh: clique: 8 (over z, core), shard: 4 (over y, x).
Axes of the slice: x: 2, y: 2, z: 4, core: 2. Of those that a mesh axis runs over, the one named last changes fastest.
Arguments:
- tables: float32 [3, 8, 4096, 128], P(None, 'clique', 'shard'), may hold values from 0.1 to 10
- up_map: int32 [2, 8, 4096], P(None, 'clique', 'shard'), may hold values from 0 to 4095, as said below
- down_map: int32 [2, 8, 4096], P(None, 'clique', 'shard'), may hold values from 0 to 4095, as said below
- parents: int32 [2, 8], replicated, may hold values from 0 to 7
Outputs:
- calibrated: float32 [3, 8, 4096, 128], P(None, 'clique', 'shard')
Inputs may be any that keep to these rules, and one draw needn't show every extreme that they name: For every edge and clique, of the 1024 blocks of one device exactly 256 name blocks in each range [k * 1024, (k + 1) * 1024). Every list of up_map and down_map names the same set of separator blocks; a named separator block is named by the same number of blocks of a clique in every list, a multiple of 1. For every edge and clique, of the 1024 blocks of one device exactly 256 name blocks in each range [k * 1024, (k + 1) * 1024). Every list of up_map and down_map names the same set of separator blocks; a named separator block is named by the same number of blocks of a clique in every list, a multiple of 1.
All inputs are finite; a program needn't handle non-finite values.
Results may differ from a plain program's by a relative error of at most 0.0003.
Values sent between devices are 32-bit elements; how exact they have to be, the bound alone decides.
No kernel may reach another device: no remote copies, remote signals or barrier semaphores. Data moves between devices by JAX's collectives and lax.ppermute only.
A program may use at most 64 MiB of HBM per device.

v0:
```python
import jax
import jax.numpy as jnp
from jax import lax
from jax.sharding import PartitionSpec as P

SEPB = 4096


def shards(tables, up_map, down_map, parents):
    shard_count = lax.axis_size("shard")
    clique_count = lax.axis_size("clique")
    block_count = tables.shape[2]
    lane_count = tables.shape[3]
    per_owner = SEPB // shard_count
    per_peer = block_count // shard_count
    sep_states = float(SEPB * lane_count)
    slot_ids = jnp.arange(per_owner, dtype=jnp.int32)

    def to_owners(potential, index_list):
        ordering = jnp.argsort(index_list // per_owner, stable=True)
        sent_rows = potential[ordering].reshape(shard_count, per_peer, lane_count)
        sent_slots = (index_list % per_owner)[ordering].reshape(shard_count, per_peer)
        arrived_rows, arrived_slots = (
            lax.all_to_all(sent_rows, "shard", split_axis=0, concat_axis=0, tiled=True),
            lax.all_to_all(sent_slots, "shard", split_axis=0, concat_axis=0, tiled=True),
        )
        one_hot = (arrived_slots.reshape(block_count)[:, None] == slot_ids[None, :]).astype(
            jnp.float32
        )
        message = jnp.dot(
            one_hot.T,
            arrived_rows.reshape(block_count, lane_count),
            precision=lax.Precision.HIGHEST,
            preferred_element_type=jnp.float32,
        )
        partial_sum = jnp.sum(message)
        total = lax.psum(partial_sum, "shard")
        return message * (sep_states / total)

    def fetch(owned_rows, index_list):
        gathered = lax.all_gather(owned_rows, "shard", axis=0, tiled=True)
        result = gathered[index_list]
        return result

    def route(owned_rows, mixing):
        pieces = owned_rows.reshape(clique_count, per_owner // clique_count, lane_count)
        combined = jnp.einsum(
            "oi,ixl->oxl",
            mixing,
            lax.all_to_all(pieces, "clique", split_axis=0, concat_axis=0, tiled=True),
            precision=lax.Precision.HIGHEST,
        )
        moved = lax.all_to_all(combined, "clique", split_axis=0, concat_axis=0, tiled=True)
        return moved.reshape(per_owner, lane_count)

    clique_ids = jnp.arange(clique_count, dtype=jnp.int32)
    current = [tables[0, 0], tables[1, 0], tables[2, 0]]
    previous = [tables[0, 0], tables[0, 0]]
    for edge in (1, 0):
        selector = (parents[edge][:, None] == clique_ids[None, :]).astype(jnp.float32)
        scaled = to_owners(current[edge + 1], up_map[edge, 0])
        previous[edge] = scaled
        incoming = jnp.exp(route(jnp.log(scaled), selector.T))
        current[edge] = current[edge] * fetch(incoming, down_map[edge, 0])
    for edge in (0, 1):
        selector = (parents[edge][:, None] == clique_ids[None, :]).astype(jnp.float32)
        fresh = to_owners(current[edge], down_map[edge, 0])
        from_parent = route(fresh, selector)
        update = from_parent / previous[edge]
        current[edge + 1] = current[edge + 1] * fetch(update, up_map[edge, 0])
    return jnp.stack(current)[:, None]


def solution(mesh):
    return jax.shard_map(
        shards,
        mesh=mesh,
        in_specs=(
            P(None, "clique", "shard", None),
            P(None, "clique", "shard"),
            P(None, "clique", "shard"),
            P(),
        ),
        out_specs=P(None, "clique", "shard", None),
        check_vma=False,
    )
```

profile of v0, /device:TPU:0, one launch (start us, length us, event | category | flops | bytes accessed | tf_op | source)
XLA Modules:
  0.0 467.1 jit_solution(16538825504890834248)
XLA Ops:
  7.3 4.4 sort.60
  11.6 8.8 %gather_fusion.1 = s32[1024]{0:T(1024)} fusion(s32[1024]{0:T(1024)S(1)} %get-tuple-element.30, s32[1024]{0:T(1024)S(1)} %fusion.17), kind=kCustom, calls=%fused_computation.1 | custom fusion | bytes 12288 | tf_op jit(solution)/shard_map/gather | solution.py:22
  20.5 5.2 %all-to-all-start.1 = ((s32[4,1,256]{2,1,0:T(1,128)}), s32[4,1,256]{2,1,0:T(1,128)S(1)}, u32[]{:S(2)}, u32[]{:S(2)}) async-start(s32[4,1,256]{2,1,0:T(1,128)} %bitcast.10), calls=%async_computation.1 | async-start | bytes 8192 | tf_op jit(solution)/shard_map/all_to_all | solution.py:25
  25.7 2.8 gather_fusion.2
  28.5 1.8 all-to-all-done.1
  30.3 10.1 %all_to_all.96 = f32[4,256,128]{2,1,0:T(8,128)S(1)} all-to-all(f32[4,256,128]{2,1,0:T(8,128)S(1)} %bitcast.91), channel_id=1, replica_groups=mesh['clique'=8,'shard'=4] {'shard'}, dimensions={0} | all-to-all | bytes 1048576 | tf_op jit(solution)/shard_map/all_to_all | solution.py:24
  40.5 4.2 fusion.40
  44.7 9.0 %psum.28 = f32[]{:T(128)} all-reduce(f32[]{:T(128)} %get-tuple-element.34), channel_id=1, replica_groups=mesh['clique'=8,'shard'=4] {'shard'}, use_global_device_ids=true, to_apply=%region_3.4 | all-reduce | flops 1 | bytes 8 | tf_op jit(solution)/shard_map/psum | solution.py:37
  55.2 4.9 %all-to-all-start.3 = ((f32[8,128,128]{2,1,0:T(8,128)}), f32[8,128,128]{2,1,0:T(8,128)S(1)}, u32[]{:S(2)}, u32[]{:S(2)}) async-start(f32[8,128,128]{2,1,0:T(8,128)} %bitcast.15), calls=%async_computation.3 | async-start | bytes 1048576 | tf_op jit(solution)/shard_map/all_to_all | solution.py:50
  60.2 15.3 %all-to-all-done.3 = f32[8,128,128]{2,1,0:T(8,128)S(1)} async-done(((f32[8,128,128]{2,1,0:T(8,128)}), f32[8,128,128]{2,1,0:T(8,128)S(1)}, u32[]{:S(2)}, u32[]{:S(2)}) %all-to-all-start.3) | async-done | bytes 524320 | tf_op jit(solution)/shard_map/all_to_all | solution.py:50
  76.3 17.7 %all_to_all.97 = f32[8,128,128]{2,1,0:T(8,128)S(1)} all-to-all(f32[8,128,128]{2,1,0:T(8,128)S(1)} %copy.27), channel_id=1, replica_groups=mesh['clique'=8,'shard'=4] {'clique'}, dimensions={0} | all-to-all | bytes 1048576 | tf_op jit(solution)/shard_map/all_to_all | solution.py:53
  95.0 4.4 sort.59
  99.3 8.8 %gather_fusion = s32[1024]{0:T(1024)} fusion(s32[1024]{0:T(1024)S(1)} %get-tuple-element.28, s32[1024]{0:T(1024)S(1)} %fusion.16), kind=kCustom, calls=%fused_computation | custom fusion | bytes 12288 | tf_op jit(solution)/shard_map/gather | solution.py:22
  108.1 3.2 all-to-all-start
  111.4 17.2 %all-gather.5.cloned.1.call-done = f32[4096,128]{1,0:T(8,128)} async-done(((f32[1024,128]{1,0:T(8,128)}), f32[4096,128]{1,0:T(8,128)}) %all-gather.5.cloned.1.call-update) | async-done | bytes 2097168 | tf_op jit(solution)/shard_map/all_gather | solution.py:41
  128.6 4.4 gather_fusion.3
  133.1 2.8 gather_fusion.4
  135.9 11.0 %all_to_all.98 = f32[4,256,128]{2,1,0:T(8,128)S(1)} all-to-all(f32[4,256,128]{2,1,0:T(8,128)S(1)} %bitcast.94), channel_id=1, replica_groups=mesh['clique'=8,'shard'=4] {'shard'}, dimensions={0} | all-to-all | bytes 1048576 | tf_op jit(solution)/shard_map/all_to_all | solution.py:24
  147.0 4.2 fusion.41
  151.2 9.0 %psum.29 = f32[]{:T(128)} all-reduce(f32[]{:T(128)} %get-tuple-element.36), channel_id=1, replica_groups=mesh['clique'=8,'shard'=4] {'shard'}, use_global_device_ids=true, to_apply=%region_5.6 | all-reduce | flops 1 | bytes 8 | tf_op jit(solution)/shard_map/psum | solution.py:37
  161.0 19.7 %all_to_all.99 = f32[8,128,128]{2,1,0:T(8,128)S(1)} all-to-all(f32[8,128,128]{2,1,0:T(8,128)S(1)} %bitcast.90), channel_id=1, replica_groups=mesh['clique'=8,'shard'=4] {'clique'}, dimensions={0} | all-to-all | bytes 1048576 | tf_op jit(solution)/shard_map/all_to_all | solution.py:50
  181.5 17.7 %all_to_all.100 = f32[8,128,128]{2,1,0:T(8,128)S(1)} all-to-all(f32[8,128,128]{2,1,0:T(8,128)S(1)} %copy.30), channel_id=1, replica_groups=mesh['clique'=8,'shard'=4] {'clique'}, dimensions={0} | all-to-all | bytes 1048576 | tf_op jit(solution)/shard_map/all_to_all | solution.py:53
  200.2 4.4 sort.61
  204.6 8.8 %gather_fusion.6 = s32[1024]{0:T(1024)} fusion(s32[1024]{0:T(1024)S(1)} %get-tuple-element.26, s32[1024]{0:T(1024)S(1)} %fusion.18), kind=kCustom, calls=%fused_computation.6 | custom fusion | bytes 12288 | tf_op jit(solution)/shard_map/gather | solution.py:22
  213.4 3.2 all-to-all-start.8
  216.7 17.2 %all-gather.7.cloned.1.call-done = f32[4096,128]{1,0:T(8,128)} async-done(((f32[1024,128]{1,0:T(8,128)}), f32[4096,128]{1,0:T(8,128)}) %all-gather.7.cloned.1.call-update) | async-done | bytes 2097168 | tf_op jit(solution)/shard_map/all_gather | solution.py:41
  233.9 5.6 %gather_fusion.5 = f32[1024,128]{1,0:T(8,128)} fusion(f32[4096,128]{1,0:T(8,128)} %all-gather.7.cloned.1.call-done, s32[1024]{0:T(1024)S(1)} %broadcast_clamp_fusion.2), kind=kCustom, calls=%fused_computation.5 | custom fusion | bytes 1052672 | tf_op jit(solution)/shard_map/gather | solution.py:42
  240.6 4.0 gather_fusion.7
  244.6 12.1 %all_to_all.101 = f32[4,256,128]{2,1,0:T(8,128)S(1)} all-to-all(f32[4,256,128]{2,1,0:T(8,128)} %bitcast.92), channel_id=1, replica_groups=mesh['clique'=8,'shard'=4] {'shard'}, dimensions={0} | all-to-all | bytes 1048576 | tf_op jit(solution)/shard_map/all_to_all | solution.py:24
  256.7 5.1 %fusion.42 = (f32[]{:T(128)}, f32[1024,128]{1,0:T(8,128)}) fusion(f32[1024,128]{1,0:T(8,128)S(1)} %bitcast.97, s32[1024]{0:T(1024)S(1)} %bitcast.109), kind=kOutput, calls=%fused_computation.108 | convolution fusion | flops 1611792384 | bytes 1052676 | tf_op jit(solution)/shard_map/dot_general | solution.py:30
  261.8 9.0 %psum.30 = f32[]{:T(128)} all-reduce(f32[]{:T(128)} %get-tuple-element.38), channel_id=1, replica_groups=mesh['clique'=8,'shard'=4] {'shard'}, use_global_device_ids=true, to_apply=%region_8.9 | all-reduce | flops 1 | bytes 8 | tf_op jit(solution)/shard_map/psum | solution.py:37
  272.5 19.9 %all_to_all.102 = f32[8,128,128]{2,1,0:T(8,128)S(1)} all-to-all(f32[8,128,128]{2,1,0:T(8,128)S(1)} %bitcast.88), channel_id=1, replica_groups=mesh['clique'=8,'shard'=4] {'clique'}, dimensions={0} | all-to-all | bytes 1048576 | tf_op jit(solution)/shard_map/all_to_all | solution.py:50
  293.1 17.7 %all_to_all.103 = f32[8,128,128]{2,1,0:T(8,128)S(1)} all-to-all(f32[8,128,128]{2,1,0:T(8,128)S(1)} %copy.32), channel_id=1, replica_groups=mesh['clique'=8,'shard'=4] {'clique'}, dimensions={0} | all-to-all | bytes 1048576 | tf_op jit(solution)/shard_map/all_to_all | solution.py:53
  311.8 4.4 sort.62
  316.2 8.8 %gather_fusion.9 = s32[1024]{0:T(1024)} fusion(s32[1024]{0:T(1024)S(1)} %get-tuple-element.24, s32[1024]{0:T(1024)S(1)} %fusion.19), kind=kCustom, calls=%fused_computation.9 | custom fusion | bytes 12288 | tf_op jit(solution)/shard_map/gather | solution.py:22
  325.0 3.2 all-to-all-start.12
  328.3 17.1 %all-gather.9.cloned.1.call-done = f32[4096,128]{1,0:T(8,128)} async-done(((f32[1024,128]{1,0:T(8,128)}), f32[4096,128]{1,0:T(8,128)}) %all-gather.9.cloned.1.call-update) | async-done | bytes 2097168 | tf_op jit(solution)/shard_map/all_gather | solution.py:41
  345.5 5.6 %gather_fusion.8 = f32[1024,128]{1,0:T(8,128)} fusion(f32[4096,128]{1,0:T(8,128)} %all-gather.9.cloned.1.call-done, s32[1024]{0:T(1024)S(1)} %broadcast_clamp_fusion.1), kind=kCustom, calls=%fused_computation.8 | custom fusion | bytes 1052672 | tf_op jit(solution)/shard_map/gather | solution.py:42
  352.1 2.8 gather_fusion.10
  355.0 11.0 %all_to_all.104 = f32[4,256,128]{2,1,0:T(8,128)S(1)} all-to-all(f32[4,256,128]{2,1,0:T(8,128)S(1)} %bitcast.93), channel_id=1, replica_groups=mesh['clique'=8,'shard'=4] {'shard'}, dimensions={0} | all-to-all | bytes 1048576 | tf_op jit(solution)/shard_map/all_to_all | solution.py:24
  366.0 4.3 fusion.43
  370.3 9.0 %psum.31 = f32[]{:T(128)} all-reduce(f32[]{:T(128)} %get-tuple-element.40), channel_id=1, replica_groups=mesh['clique'=8,'shard'=4] {'shard'}, use_global_device_ids=true, to_apply=%region_11.12 | all-reduce | flops 1 | bytes 8 | tf_op jit(solution)/shard_map/psum | solution.py:37
  380.0 19.9 %all_to_all.105 = f32[8,128,128]{2,1,0:T(8,128)S(1)} all-to-all(f32[8,128,128]{2,1,0:T(8,128)S(1)} %bitcast.89), channel_id=1, replica_groups=mesh['clique'=8,'shard'=4] {'clique'}, dimensions={0} | all-to-all | bytes 1048576 | tf_op jit(solution)/shard_map/all_to_all | solution.py:50
  400.6 17.7 %all_to_all.106 = f32[8,128,128]{2,1,0:T(8,128)S(1)} all-to-all(f32[8,128,128]{2,1,0:T(8,128)S(1)} %copy.34), channel_id=1, replica_groups=mesh['clique'=8,'shard'=4] {'clique'}, dimensions={0} | all-to-all | bytes 1048576 | tf_op jit(solution)/shard_map/all_to_all | solution.py:53
  419.3 33.2 %all-gather.11.cloned.1.call-done = f32[4096,128]{1,0:T(8,128)} async-done(((f32[1024,128]{1,0:T(8,128)}), f32[4096,128]{1,0:T(8,128)}) %all-gather.11.cloned.1.call-update) | async-done | bytes 2097168 | tf_op jit(solution)/shard_map/all_gather | solution.py:41
  452.5 5.6 %gather_fusion.11 = f32[1024,128]{1,0:T(8,128)} fusion(f32[4096,128]{1,0:T(8,128)} %all-gather.11.cloned.1.call-done, s32[1024]{0:T(1024)S(1)} %broadcast_clamp_fusion), kind=kCustom, calls=%fused_computation.11 | custom fusion | bytes 1052672 | tf_op jit(solution)/shard_map/gather | solution.py:42
  458.1 1.2 bitcast_multiply_fusion.4
  459.3 1.2 maximum_bitcast_fusion
  (72 shorter events, 12.1 us)
Async XLA Ops:
  11.6 14.0 %copy-start = (f32[3,1,1024,128]{3,2,1,0:T(8,128)S(1)}, f32[3,1,1024,128]{3,2,1,0:T(8,128)}, u32[]{:S(2)}) copy-start(f32[3,1,1024,128]{3,2,1,0:T(8,128)} %param.4) | copy-start | bytes 4718596
  20.5 9.9 %all-to-all-start.1 = ((s32[4,1,256]{2,1,0:T(1,128)}), s32[4,1,256]{2,1,0:T(1,128)S(1)}, u32[]{:S(2)}, u32[]{:S(2)}) async-start(s32[4,1,256]{2,1,0:T(1,128)} %bitcast.10), calls=%async_computation.1 | async-start | bytes 8192 | tf_op jit(solution)/shard_map/all_to_all | solution.py:25
  40.5 19.7 %copy-start.9 = (s32[2,8]{1,0:T(2,128)S(1)}, s32[2,8]{1,0:T(2,128)}, u32[]{:S(2)}) copy-start(s32[2,8]{1,0:T(2,128)} %param.7) | copy-start | bytes 196
  44.7 31.6 %copy-start.3 = (f32[1024,128]{1,0:T(8,128)}, f32[1024,128]{1,0:T(8,128)S(1)}, u32[]{:S(2)}) copy-start(f32[1024,128]{1,0:T(8,128)S(1)} %get-tuple-element.35) | copy-start | bytes 1572868
  55.2 20.2 %all-to-all-start.3 = ((f32[8,128,128]{2,1,0:T(8,128)}), f32[8,128,128]{2,1,0:T(8,128)S(1)}, u32[]{:S(2)}, u32[]{:S(2)}) async-start(f32[8,128,128]{2,1,0:T(8,128)} %bitcast.15), calls=%async_computation.3 | async-start | bytes 1048576 | tf_op jit(solution)/shard_map/all_to_all | solution.py:50
  60.1 68.5 %all-gather.5.cloned.1.call-start = ((), (), s32[]{:S(2)}) async-start(), calls=%async_computation.16 | async-start | bytes 2621440 | tf_op jit(solution)/shard_map/all_gather | solution.py:41
  99.3 12.1 %copy-start.7 = (s32[2,1,1024]{2,1,0:T(1,128)S(1)}, s32[2,1,1024]{2,1,0:T(1,128)}, u32[]{:S(2)}) copy-start(s32[2,1,1024]{2,1,0:T(1,128)} %param.6) | copy-start | bytes 24580
  108.1 27.8 %all-to-all-start = ((s32[4,1,256]{2,1,0:T(1,128)}), s32[4,1,256]{2,1,0:T(1,128)S(1)}, u32[]{:S(2)}, u32[]{:S(2)}) async-start(s32[4,1,256]{2,1,0:T(1,128)} %bitcast.4), calls=%async_computation | async-start | bytes 8192 | tf_op jit(solution)/shard_map/all_to_all | solution.py:25
  111.3 122.6 %all-gather.7.cloned.1.call-start = ((), (), s32[]{:S(2)}) async-start(), calls=%async_computation.17 | async-start | bytes 2621440 | tf_op jit(solution)/shard_map/all_gather | solution.py:41
  151.2 30.4 %copy-start.5 = (f32[1024,128]{1,0:T(8,128)}, f32[1024,128]{1,0:T(8,128)S(1)}, u32[]{:S(2)}) copy-start(f32[1024,128]{1,0:T(8,128)S(1)} %get-tuple-element.37) | copy-start | bytes 1572868
  213.4 31.2 %all-to-all-start.8 = ((s32[4,1,256]{2,1,0:T(1,128)}), s32[4,1,256]{2,1,0:T(1,128)S(1)}, u32[]{:S(2)}, u32[]{:S(2)}) async-start(s32[4,1,256]{2,1,0:T(1,128)} %bitcast.30), calls=%async_computation.8 | async-start | bytes 8192 | tf_op jit(solution)/shard_map/all_to_all | solution.py:25
  216.7 128.8 %all-gather.9.cloned.1.call-start = ((), (), s32[]{:S(2)}) async-start(), calls=%async_computation.18 | async-start | bytes 2621440 | tf_op jit(solution)/shard_map/all_gather | solution.py:41
  272.4 38.4 %copy-start.6 = (f32[1024,128]{1,0:T(8,128)S(1)}, f32[1024,128]{1,0:T(8,128)}, u32[]{:S(2)}) copy-start(f32[1024,128]{1,0:T(8,128)} %copy-done.5) | copy-start | bytes 1572868
  316.2 12.1 %copy-start.8 = (s32[2,1,1024]{2,1,0:T(1,128)S(1)}, s32[2,1,1024]{2,1,0:T(1,128)}, u32[]{:S(2)}) copy-start(s32[2,1,1024]{2,1,0:T(1,128)} %param.5) | copy-start | bytes 24580
  325.0 29.9 %all-to-all-start.12 = ((s32[4,1,256]{2,1,0:T(1,128)}), s32[4,1,256]{2,1,0:T(1,128)S(1)}, u32[]{:S(2)}, u32[]{:S(2)}) async-start(s32[4,1,256]{2,1,0:T(1,128)} %bitcast.43), calls=%async_computation.12 | async-start | bytes 8192 | tf_op jit(solution)/shard_map/all_to_all | solution.py:25
  328.2 124.2 %all-gather.11.cloned.1.call-start = ((), (), s32[]{:S(2)}) async-start(), calls=%async_computation.19 | async-start | bytes 2621440 | tf_op jit(solution)/shard_map/all_gather | solution.py:41
  379.9 38.4 %copy-start.4 = (f32[1024,128]{1,0:T(8,128)S(1)}, f32[1024,128]{1,0:T(8,128)}, u32[]{:S(2)}) copy-start(f32[1024,128]{1,0:T(8,128)} %copy-done.3) | copy-start | bytes 1572868
  419.3 38.8 %copy-start.1 = (f32[1024,128]{1,0:T(8,128)S(1)}, f32[1024,128]{1,0:T(8,128)}, u32[]{:S(2)}) copy-start(f32[1024,128]{1,0:T(8,128)} %gather_fusion.5) | copy-start | bytes 1572868
  419.3 38.8 %copy-start.2 = (f32[1024,128]{1,0:T(8,128)S(1)}, f32[1024,128]{1,0:T(8,128)}, u32[]{:S(2)}) copy-start(f32[1024,128]{1,0:T(8,128)} %gather_fusion.8) | copy-start | bytes 1572868
Sparse Core Ops, SparseCore 0:
  95.1 33.5 all-gather.4
  200.3 33.5 all-gather.6
  311.9 33.5 all-gather.8
  419.4 33.0 all-gather.10
where the time goes:
time: 468 us; the launch traced here: 467 us
  blocking collectives  211 us (45%)
  waiting for transfers between devices  102 us (22%)
  local copies, waits for them, and re-layouts  71.8 us (15%)
  other arithmetic  26.1 us (6%)
  matrix products  20.5 us (4%)
  starting transfers between devices  19.9 us (4%)
  between operations  16.1 us (3%)
    all_gather x4, waiting for transfers between devices, fetch(): gathered = lax.all_gather(owned_rows, 'shard', axis=0, tiled=True)  84.7 us
    all_to_all x4, blocking collectives, route(): lax.all_to_all(combined, 'clique', split_axis=0, concat_axis=0, tiled=True)  70.9 us
    all_to_all x3, blocking collectives, route(): lax.all_to_all(pieces, 'clique', split_axis=0, concat_axis=0, tiled=True)  59.5 us
    all_to_all x4, blocking collectives, to_owners(): lax.all_to_all(sent_rows, 'shard', split_axis=0, concat_axis=0, tiled=True)  44.3 us
    psum x4, blocking collectives, to_owners(): total = lax.psum(partial_sum, 'shard')  36 us
    gather x4, local copies, waits for them, and re-layouts, to_owners(): (index_list % per_owner)[ordering].reshape(shard_count, per_peer)  35.3 us
    gather x4, local copies, waits for them, and re-layouts, fetch(): result = gathered[index_list]  21.2 us
    dot_general x4, matrix products, to_owners(): jnp.dot(one_hot.T, arrived_rows.reshape(block_count, lane_count), precisi...  17.8 us
  transfers between devices with their start and end apart: 9, of which 6 were waited for; matrix products, arithmetic and copies ran while one was open for 15% of the time, Pallas kernels for 0%

commit v1 on v0

v1 whole, which is shorter than its diff:
```python
import jax
import jax.numpy as jnp
from jax import lax
from jax.sharding import PartitionSpec as P

SEPB = 4096
PAD = 8


def split_dot(one_hot, x):
    lanes = x.shape[-1]
    hi = lax.reduce_precision(x, exponent_bits=8, mantissa_bits=7)
    rest = x - hi
    mid = lax.reduce_precision(rest, exponent_bits=8, mantissa_bits=7)
    lo = rest - mid
    parts = jnp.concatenate([hi, mid, lo], axis=1).astype(jnp.bfloat16)
    y = jnp.dot(
        one_hot,
        parts,
        preferred_element_type=jnp.float32,
    )
    return (y[:, :lanes] + y[:, lanes : 2 * lanes]) + y[:, 2 * lanes :]


def gather_rows(x, index):
    one_hot = (index[:, None] == jnp.arange(x.shape[0], dtype=jnp.int32)[None, :]).astype(
        jnp.bfloat16
    )
    return split_dot(one_hot, x)


def segment_rows(x, segment, count):
    one_hot = (jnp.arange(count, dtype=jnp.int32)[:, None] == segment[None, :]).astype(
        jnp.bfloat16
    )
    return split_dot(one_hot, x)


def shards(tables, up_map, down_map, parents):
    shard_count = lax.axis_size("shard")
    clique_count = lax.axis_size("clique")
    block_count = tables.shape[2]
    lane_count = tables.shape[3]
    per_owner = SEPB // shard_count
    per_peer = block_count // shard_count
    sep_states = float(SEPB * lane_count)

    lists = jnp.stack([up_map[1, 0], up_map[0, 0], down_map[0, 0], down_map[1, 0]])
    owner = lists // per_owner
    slot = lists % per_owner
    order = jnp.argsort(owner, axis=1, stable=True)
    sent_slots = jnp.take_along_axis(slot, order, axis=1).reshape(4, shard_count, per_peer)
    arrived = lax.all_to_all(sent_slots, "shard", 1, 1, tiled=True).reshape(4, block_count)
    is_owner = owner[:, :, None] == jnp.arange(shard_count, dtype=jnp.int32)[None, None, :]
    rank = jnp.sum(jnp.where(is_owner, jnp.cumsum(is_owner.astype(jnp.int32), axis=1), 0), axis=2)
    position = owner * per_peer + rank - 1

    def send(sorted_rows, which):
        partial_sum = jnp.sum(sorted_rows)
        payload = jnp.concatenate(
            [
                sorted_rows.reshape(shard_count, per_peer, lane_count),
                jnp.broadcast_to(partial_sum, (shard_count, PAD, lane_count)),
            ],
            axis=1,
        )
        arrived_rows = lax.all_to_all(payload, "shard", 0, 0, tiled=True)
        total = jnp.sum(arrived_rows[:, per_peer, 0])
        rows = arrived_rows[:, :per_peer].reshape(block_count, lane_count)
        message = segment_rows(rows, arrived[which], per_owner)
        return message * (sep_states / total)

    def fetch(owned_rows, which):
        owned_rows = jnp.where(jnp.isfinite(owned_rows), owned_rows, 0.0)
        picked = gather_rows(owned_rows, arrived[which])
        back = lax.all_to_all(
            picked.reshape(shard_count, per_peer, lane_count), "shard", 0, 0, tiled=True
        )
        return back.reshape(block_count, lane_count)

    def route(owned_rows, mixing):
        pieces = owned_rows.reshape(clique_count, per_owner // clique_count, lane_count)
        combined = jnp.einsum(
            "oi,ixl->oxl",
            mixing,
            lax.all_to_all(pieces, "clique", split_axis=0, concat_axis=0, tiled=True),
            precision=lax.Precision.HIGHEST,
        )
        moved = lax.all_to_all(combined, "clique", split_axis=0, concat_axis=0, tiled=True)
        return moved.reshape(per_owner, lane_count)

    clique_ids = jnp.arange(clique_count, dtype=jnp.int32)
    sel = [
        (parents[edge][:, None] == clique_ids[None, :]).astype(jnp.float32) for edge in (0, 1)
    ]
    t0, t1, t2 = tables[0, 0], tables[1, 0], tables[2, 0]

    t2_up1 = gather_rows(t2, order[0])
    scaled1 = send(t2_up1, 0)
    incoming1 = jnp.exp(route(jnp.log(scaled1), sel[1].T))
    t1_down1 = gather_rows(t1, order[3]) * fetch(incoming1, 3)
    t1_up0 = gather_rows(t1_down1, jnp.take(position[3], order[1]))
    scaled0 = send(t1_up0, 1)
    incoming0 = jnp.exp(route(jnp.log(scaled0), sel[0].T))
    t0_down0 = gather_rows(t0, order[2]) * fetch(incoming0, 2)
    out0 = gather_rows(t0_down0, position[2])
    fresh0 = send(t0_down0, 2)
    update0 = route(fresh0, sel[0]) / scaled0
    t1_up0 = t1_up0 * fetch(update0, 1)
    out1 = gather_rows(t1_up0, position[1])
    t1_down1 = gather_rows(t1_up0, jnp.take(position[1], order[3]))
    fresh1 = send(t1_down1, 3)
    update1 = route(fresh1, sel[1]) / scaled1
    t2_up1 = t2_up1 * fetch(update1, 0)
    out2 = gather_rows(t2_up1, position[0])
    return jnp.stack([out0, out1, out2])[:, None]


def solution(mesh):
    return jax.shard_map(
        shards,
        mesh=mesh,
        in_specs=(
            P(None, "clique", "shard", None),
            P(None, "clique", "shard"),
            P(None, "clique", "shard"),
            P(),
        ),
        out_specs=P(None, "clique", "shard", None),
        check_vma=False,
    )
```

time: 468 us -> 345 us (0.74)
  blocking collectives: 211 us -> 123 us
  waiting for transfers between devices: 102 us -> 63 us
  local copies, waits for them, and re-layouts: 71.8 us -> 55.2 us
  starting transfers between devices: 19.9 us -> 34.6 us
  matrix products: 20.5 us -> 25.5 us
    all_gather x4 -> x0, waiting for transfers between devices: 84.7 us -> none  [fetch(): gathered = lax.all_gather(owned_rows, 'shard', axis=0, tiled=True)]
    all_to_all x4 -> x8, waiting for transfers between devices: 1.83 us -> 53.4 us  [the longest x2 24.3 us: route(): lax.all_to_all(combined, 'clique', split_axis=0, concat_axis=0, tiled=True)]
    psum x4 -> x0, blocking collectives: 36 us -> none  [to_owners(): total = lax.psum(partial_sum, 'shard')]
    all_to_all x4 -> x2, blocking collectives: 70.9 us -> 35.5 us  [route(): lax.all_to_all(combined, 'clique', split_axis=0, concat_axis=0, tiled=True)]
    gather x12 -> x4, local copies, waits for them, and re-layouts: 68.9 us -> 44.1 us  [the longest x2 35 us: shards(): jnp.take_along_axis(slot, order, axis=1).reshape(4, shard_count, per_peer)]
    sort x4 -> x0, other arithmetic: 17.5 us -> none  [to_owners(): ordering = jnp.argsort(index_list // per_owner, stable=True)]
    all_to_all x4 -> x8, starting transfers between devices: 14.9 us -> 29.8 us  [the longest x4 14.1 us: fetch(): lax.all_to_all(picked.reshape(shard_count, per_peer, lane_count), 'shard'...]
    another operation x0 -> x21, other arithmetic: none -> 13.1 us
  transfers between devices with their start and end apart: 9 -> 9, of which waited for: 6 -> 9; matrix products, arithmetic and copies ran while one was open for 15% -> 8% of each run, Pallas kernels for 0% -> 0%
where the time goes in v1:
time: 345 us; the launch traced here: 343 us
  blocking collectives  123 us (36%)
  waiting for transfers between devices  63 us (18%)
  local copies, waits for them, and re-layouts  55.2 us (16%)
  starting transfers between devices  34.6 us (10%)
  matrix products  25.5 us (7%)
  other arithmetic  25 us (7%)
  between operations  16.8 us (5%)
    all_to_all x3, blocking collectives, route(): lax.all_to_all(pieces, 'clique', split_axis=0, concat_axis=0, tiled=True)  56.3 us
    all_to_all x2, blocking collectives, route(): lax.all_to_all(combined, 'clique', split_axis=0, concat_axis=0, tiled=True)  35.5 us
    gather x2, local copies, waits for them, and re-layouts, shards(): jnp.take_along_axis(slot, order, axis=1).reshape(4, shard_count, per_peer)  35 us
    all_to_all x3, blocking collectives, send(): arrived_rows = lax.all_to_all(payload, 'shard', 0, 0, tiled=True)  31.5 us
    all_to_all x2, waiting for transfers between devices, route(): lax.all_to_all(combined, 'clique', split_axis=0, concat_axis=0, tiled=True)  24.3 us
    dot_general x16, matrix products, split_dot(): y = jnp.dot(one_hot, parts, preferred_element_type=jnp.float32)  22.7 us
    all_to_all x4, waiting for transfers between devices, fetch(): lax.all_to_all(picked.reshape(shard_count, per_peer, lane_count), 'shard'...  20.8 us
    all_to_all x4, starting transfers between devices, fetch(): lax.all_to_all(picked.reshape(shard_count, per_peer, lane_count), 'shard'...  14.1 us
  transfers between devices with their start and end apart: 9, of which 9 were waited for; matrix products, arithmetic and copies ran while one was open for 8% of the time, Pallas kernels for 0%

profile of v1, /device:TPU:0, one launch (start us, length us, event | category | flops | bytes accessed | tf_op | source)
XLA Modules:
  0.0 343.4 jit_solution(11454941010618489584)
XLA Ops:
  8.6 2.7 reduce-precision_convert_fusion.29
  11.3 1.5 sort.19.cloned.1.call-done
  14.5 35.0 %gather_fusion = s32[4096]{0:T(1024)S(1)} fusion(s32[4,1024]{1,0:T(4,128)S(1)} %get-tuple-element.78, s32[4096]{0:T(1024)S(1)} %bitcast.187), kind=kCustom, calls=%fused_computation.2 | custom fusion | bytes 65536 | tf_op jit(solution)/shard_map/jit(take_along_axis)/gather | solution.py:52
  50.1 5.2 %all-to-all-start = ((s32[4,4,256]{2,0,1:T(4,128)}), s32[4,4,256]{2,0,1:T(4,128)S(1)}, u32[]{:S(2)}, u32[]{:S(2)}) async-start(s32[4,4,256]{2,0,1:T(4,128)} %bitcast.13), calls=%async_computation | async-start | bytes 32768 | tf_op jit(solution)/shard_map/all_to_all | solution.py:53
  55.3 1.3 fusion.8
  57.4 1.5 concatenate.93
  60.0 3.5 %all-to-all-start.1 = ((f32[4,264,128]{2,1,0:T(8,128)}), f32[4,264,128]{2,1,0:T(8,128)S(1)}, u32[]{:S(2)}, u32[]{:S(2)}) async-start(f32[4,264,128]{2,1,0:T(8,128)} %concatenate.93), calls=%async_computation.1 | async-start | bytes 1081344 | tf_op jit(solution)/shard_map/all_to_all | solution.py:67
  63.5 7.2 %all-to-all-done.1 = f32[4,264,128]{2,1,0:T(8,128)S(1)} async-done(((f32[4,264,128]{2,1,0:T(8,128)}), f32[4,264,128]{2,1,0:T(8,128)S(1)}, u32[]{:S(2)}, u32[]{:S(2)}) %all-to-all-start.1) | async-done | bytes 540704 | tf_op jit(solution)/shard_map/all_to_all | solution.py:67
  72.2 1.3 fusion.7
  74.4 4.9 %all-to-all-start.2 = ((f32[8,128,128]{2,1,0:T(8,128)}), f32[8,128,128]{2,1,0:T(8,128)S(1)}, u32[]{:S(2)}, u32[]{:S(2)}) async-start(f32[8,128,128]{2,1,0:T(8,128)} %bitcast.30), calls=%async_computation.2 | async-start | bytes 1048576 | tf_op jit(solution)/shard_map/all_to_all | solution.py:86
  79.3 4.5 %reduce-window.6 = s32[4,4,8,128]{3,2,1,0:T(8,128)S(1)} reduce-window(s32[4,4,8,128]{3,2,1,0:T(8,128)S(1)} %fusion.135, s32[]{:T(128)} %constant.54.clone.1), window={size=1x1x1x128 pad=0_0x0_0x0_0x127_0}, to_apply=%region_0.1 | reduce-window | flops 2080768 | bytes 131076 | tf_op jit(solution)/shard_map/reduce-window
  84.9 9.6 %all-to-all-done.2 = f32[8,128,128]{2,1,0:T(8,128)S(1)} async-done(((f32[8,128,128]{2,1,0:T(8,128)}), f32[8,128,128]{2,1,0:T(8,128)S(1)}, u32[]{:S(2)}, u32[]{:S(2)}) %all-to-all-start.2) | async-done | bytes 524320 | tf_op jit(solution)/shard_map/all_to_all | solution.py:86
  96.2 3.5 %all-to-all-start.3 = ((f32[8,128,128]{2,1,0:T(8,128)}), f32[8,128,128]{2,1,0:T(8,128)S(1)}, u32[]{:S(2)}, u32[]{:S(2)}) async-start(f32[8,128,128]{2,1,0:T(8,128)} %copy.32), calls=%async_computation.3 | async-start | bytes 1048576 | tf_op jit(solution)/shard_map/all_to_all | solution.py:89
  99.9 4.5 %gather_fusion.1 = s32[1024]{0:T(1024)S(1)} fusion(s32[1024]{0:T(1024)S(1)} %bitcast.186, s32[1024]{0:T(1024)S(1)} %fusion.146), kind=kCustom, calls=%fused_computation.clone | custom fusion | bytes 12288 | tf_op jit(solution)/shard_map/jit(_take)/gather | solution.py:102
  104.5 10.5 %all-to-all-done.3 = f32[8,128,128]{2,1,0:T(8,128)S(1)} async-done(((f32[8,128,128]{2,1,0:T(8,128)}), f32[8,128,128]{2,1,0:T(8,128)S(1)}, u32[]{:S(2)}, u32[]{:S(2)}) %all-to-all-start.3) | async-done | bytes 524320 | tf_op jit(solution)/shard_map/all_to_all | solution.py:89
  115.2 1.3 fusion.6
  117.6 3.5 %all-to-all-start.4 = ((f32[4,256,128]{1,2,0:T(8,128)}), f32[4,256,128]{1,2,0:T(8,128)S(1)}, u32[]{:S(2)}, u32[]{:S(2)}) async-start(f32[4,256,128]{1,2,0:T(8,128)} %copy.33), calls=%async_computation.4 | async-start | bytes 1048576 | tf_op jit(solution)/shard_map/all_to_all | solution.py:76
  121.0 2.3 fusion.5
  123.4 5.6 %all-to-all-done.4 = f32[4,256,128]{1,2,0:T(8,128)S(1)} async-done(((f32[4,256,128]{1,2,0:T(8,128)}), f32[4,256,128]{1,2,0:T(8,128)S(1)}, u32[]{:S(2)}, u32[]{:S(2)}) %all-to-all-start.4) | async-done | bytes 524320 | tf_op jit(solution)/shard_map/all_to_all | solution.py:76
  129.4 1.3 fusion.4
  132.1 10.5 %all_to_all.85 = f32[4,264,128]{2,1,0:T(8,128)S(1)} all-to-all(f32[4,264,128]{2,1,0:T(8,128)S(1)} %concatenate.97), channel_id=1, replica_groups=mesh['clique'=8,'shard'=4] {'shard'}, dimensions={0} | all-to-all | bytes 1081344 | tf_op jit(solution)/shard_map/all_to_all | solution.py:67
  145.5 18.7 %all_to_all.86 = f32[8,128,128]{2,1,0:T(8,128)S(1)} all-to-all(f32[8,128,128]{2,1,0:T(8,128)S(1)} %bitcast.196), channel_id=1, replica_groups=mesh['clique'=8,'shard'=4] {'clique'}, dimensions={0} | all-to-all | bytes 1048576 | tf_op jit(solution)/shard_map/all_to_all | solution.py:86
  165.0 17.7 %all_to_all.87 = f32[8,128,128]{2,1,0:T(8,128)S(1)} all-to-all(f32[8,128,128]{2,1,0:T(8,128)S(1)} %copy.37), channel_id=1, replica_groups=mesh['clique'=8,'shard'=4] {'clique'}, dimensions={0} | all-to-all | bytes 1048576 | tf_op jit(solution)/shard_map/all_to_all | solution.py:89
  183.0 1.3 fusion.2
  185.2 3.5 %all-to-all-start.8 = ((f32[4,256,128]{2,1,0:T(8,128)}), f32[4,256,128]{2,1,0:T(8,128)S(1)}, u32[]{:S(2)}, u32[]{:S(2)}) async-start(f32[4,256,128]{2,1,0:T(8,128)} %bitcast.37), calls=%async_computation.8 | async-start | bytes 1048576 | tf_op jit(solution)/shard_map/all_to_all | solution.py:76
  188.7 2.4 fusion.1
  191.1 5.4 %all-to-all-done.8 = f32[4,256,128]{2,1,0:T(8,128)S(1)} async-done(((f32[4,256,128]{2,1,0:T(8,128)}), f32[4,256,128]{2,1,0:T(8,128)S(1)}, u32[]{:S(2)}, u32[]{:S(2)}) %all-to-all-start.8) | async-done | bytes 524320 | tf_op jit(solution)/shard_map/all_to_all | solution.py:76
  196.5 2.2 reduce-precision_convert_fusion.13
  200.2 10.5 %all_to_all.88 = f32[4,264,128]{2,1,0:T(8,128)S(1)} all-to-all(f32[4,264,128]{2,1,0:T(8,128)S(1)} %concatenate.101), channel_id=1, replica_groups=mesh['clique'=8,'shard'=4] {'shard'}, dimensions={0} | all-to-all | bytes 1081344 | tf_op jit(solution)/shard_map/all_to_all | solution.py:67
  212.1 1.3 fusion.11
  213.5 18.8 %all_to_all.89 = f32[8,128,128]{2,1,0:T(8,128)S(1)} all-to-all(f32[8,128,128]{2,1,0:T(8,128)S(1)} %bitcast.191), channel_id=1, replica_groups=mesh['clique'=8,'shard'=4] {'clique'}, dimensions={0} | all-to-all | bytes 1048576 | tf_op jit(solution)/shard_map/all_to_all | solution.py:86
  233.1 17.7 %all_to_all.90 = f32[8,128,128]{2,1,0:T(8,128)S(1)} all-to-all(f32[8,128,128]{2,1,0:T(8,128)S(1)} %copy.39), channel_id=1, replica_groups=mesh['clique'=8,'shard'=4] {'clique'}, dimensions={0} | all-to-all | bytes 1048576 | tf_op jit(solution)/shard_map/all_to_all | solution.py:89
  251.0 1.3 fusion.10
  253.2 3.7 %all-to-all-start.12 = ((f32[4,256,128]{2,1,0:T(8,128)}), f32[4,256,128]{2,1,0:T(8,128)S(1)}, u32[]{:S(2)}, u32[]{:S(2)}) async-start(f32[4,256,128]{2,1,0:T(8,128)} %bitcast.46), calls=%async_computation.12 | async-start | bytes 1048576 | tf_op jit(solution)/shard_map/all_to_all | solution.py:76
  256.9 4.5 %gather_fusion.2 = s32[1024]{0:T(1024)S(1)} fusion(s32[1024]{0:T(1024)S(1)} %bitcast.184, s32[1024]{0:T(1024)S(1)} %fusion.147), kind=kCustom, calls=%fused_computation.1.clone | custom fusion | bytes 12288 | tf_op jit(solution)/shard_map/jit(_take)/gather | solution.py:111
  261.4 3.1 all-to-all-done.12
  264.7 1.3 fusion.15
  267.4 10.5 %all_to_all.91 = f32[4,264,128]{2,1,0:T(8,128)S(1)} all-to-all(f32[4,264,128]{2,1,0:T(8,128)S(1)} %concatenate.105), channel_id=1, replica_groups=mesh['clique'=8,'shard'=4] {'shard'}, dimensions={0} | all-to-all | bytes 1081344 | tf_op jit(solution)/shard_map/all_to_all | solution.py:67
  279.4 1.3 fusion.14
  280.8 18.9 %all_to_all.92 = f32[8,128,128]{2,1,0:T(8,128)S(1)} all-to-all(f32[8,128,128]{2,1,0:T(8,128)S(1)} %bitcast.192), channel_id=1, replica_groups=mesh['clique'=8,'shard'=4] {'clique'}, dimensions={0} | all-to-all | bytes 1048576 | tf_op jit(solution)/shard_map/all_to_all | solution.py:86
  301.2 3.5 %all-to-all-start.15 = ((f32[8,128,128]{2,1,0:T(8,128)}), f32[8,128,128]{2,1,0:T(8,128)S(1)}, u32[]{:S(2)}, u32[]{:S(2)}) async-start(f32[8,128,128]{2,1,0:T(8,128)} %copy.41), calls=%async_computation.15 | async-start | bytes 1048576 | tf_op jit(solution)/shard_map/all_to_all | solution.py:89
  304.7 1.3 fusion
  306.1 13.9 %all-to-all-done.15 = f32[8,128,128]{2,1,0:T(8,128)S(1)} async-done(((f32[8,128,128]{2,1,0:T(8,128)}), f32[8,128,128]{2,1,0:T(8,128)S(1)}, u32[]{:S(2)}, u32[]{:S(2)}) %all-to-all-start.15) | async-done | bytes 524320 | tf_op jit(solution)/shard_map/all_to_all | solution.py:89
  320.2 1.3 fusion.13
  322.3 3.5 %all-to-all-start.16 = ((f32[4,256,128]{2,1,0:T(8,128)}), f32[4,256,128]{2,1,0:T(8,128)S(1)}, u32[]{:S(2)}, u32[]{:S(2)}) async-start(f32[4,256,128]{2,1,0:T(8,128)} %bitcast.55), calls=%async_computation.16 | async-start | bytes 1048576 | tf_op jit(solution)/shard_map/all_to_all | solution.py:76
  325.8 1.3 fusion.9
  327.2 6.6 %all-to-all-done.16 = f32[4,256,128]{2,1,0:T(8,128)S(1)} async-done(((f32[4,256,128]{2,1,0:T(8,128)}), f32[4,256,128]{2,1,0:T(8,128)S(1)}, u32[]{:S(2)}, u32[]{:S(2)}) %all-to-all-start.16) | async-done | bytes 524320 | tf_op jit(solution)/shard_map/all_to_all | solution.py:76
  333.9 1.3 fusion.12
  (90 shorter events, 28.8 us)
Async XLA Ops:
  6.5 6.3 %sort.19.cloned.1.call-start = ((), (), s32[]{:S(2)}) async-start(), calls=%async_computation.17 | async-start | bytes 98336 | tf_op jit(solution)/shard_map/jit(argsort)/sort | solution.py:51
  14.5 35.0 %copy-start.4 = (s32[4,1024]{1,0:T(4,128)S(1)}, s32[4,1024]{1,0:T(4,128)}, u32[]{:S(2)}) copy-start(s32[4,1024]{1,0:T(4,128)} %get-tuple-element.7) | copy-start | bytes 49156
  50.1 9.9 %all-to-all-start = ((s32[4,4,256]{2,0,1:T(4,128)}), s32[4,4,256]{2,0,1:T(4,128)S(1)}, u32[]{:S(2)}, u32[]{:S(2)}) async-start(s32[4,4,256]{2,0,1:T(4,128)} %bitcast.13), calls=%async_computation | async-start | bytes 32768 | tf_op jit(solution)/shard_map/all_to_all | solution.py:53
  60.0 10.7 %all-to-all-start.1 = ((f32[4,264,128]{2,1,0:T(8,128)}), f32[4,264,128]{2,1,0:T(8,128)S(1)}, u32[]{:S(2)}, u32[]{:S(2)}) async-start(f32[4,264,128]{2,1,0:T(8,128)} %concatenate.93), calls=%async_computation.1 | async-start | bytes 1081344 | tf_op jit(solution)/shard_map/all_to_all | solution.py:67
  73.5 11.5 %copy-start.5 = (s32[2,8]{1,0:T(2,128)S(1)}, s32[2,8]{1,0:T(2,128)}, u32[]{:S(2)}) copy-start(s32[2,8]{1,0:T(2,128)} %param.9) | copy-start | bytes 196
  74.4 20.2 %all-to-all-start.2 = ((f32[8,128,128]{2,1,0:T(8,128)}), f32[8,128,128]{2,1,0:T(8,128)S(1)}, u32[]{:S(2)}, u32[]{:S(2)}) async-start(f32[8,128,128]{2,1,0:T(8,128)} %bitcast.30), calls=%async_computation.2 | async-start | bytes 1048576 | tf_op jit(solution)/shard_map/all_to_all | solution.py:86
  94.6 5.2 %copy-start = (s32[4,1024]{1,0:T(4,128)S(1)}, s32[4,1024]{1,0:T(4,128)}, u32[]{:S(2)}) copy-start(s32[4,1024]{1,0:T(4,128)} %get-tuple-element.79) | copy-start | bytes 49156
  96.2 18.8 %all-to-all-start.3 = ((f32[8,128,128]{2,1,0:T(8,128)}), f32[8,128,128]{2,1,0:T(8,128)S(1)}, u32[]{:S(2)}, u32[]{:S(2)}) async-start(f32[8,128,128]{2,1,0:T(8,128)} %copy.32), calls=%async_computation.3 | async-start | bytes 1048576 | tf_op jit(solution)/shard_map/all_to_all | solution.py:89
  117.6 11.4 %all-to-all-start.4 = ((f32[4,256,128]{1,2,0:T(8,128)}), f32[4,256,128]{1,2,0:T(8,128)S(1)}, u32[]{:S(2)}, u32[]{:S(2)}) async-start(f32[4,256,128]{1,2,0:T(8,128)} %copy.33), calls=%async_computation.4 | async-start | bytes 1048576 | tf_op jit(solution)/shard_map/all_to_all | solution.py:76
  184.3 4.4 %copy-start.2 = (bf16[1024,128]{1,0:T(8,128)(2,1)S(1)}, bf16[1024,128]{1,0:T(8,128)(2,1)}, u32[]{:S(2)}) copy-start(bf16[1024,128]{1,0:T(8,128)(2,1)} %get-tuple-element.25) | copy-start | bytes 786436
  184.3 4.4 %copy-start.3 = (bf16[1024,128]{1,0:T(8,128)(2,1)S(1)}, bf16[1024,128]{1,0:T(8,128)(2,1)}, u32[]{:S(2)}) copy-start(bf16[1024,128]{1,0:T(8,128)(2,1)} %get-tuple-element.26) | copy-start | bytes 786436
  185.2 11.4 %all-to-all-start.8 = ((f32[4,256,128]{2,1,0:T(8,128)}), f32[4,256,128]{2,1,0:T(8,128)S(1)}, u32[]{:S(2)}, u32[]{:S(2)}) async-start(f32[4,256,128]{2,1,0:T(8,128)} %bitcast.37), calls=%async_computation.8 | async-start | bytes 1048576 | tf_op jit(solution)/shard_map/all_to_all | solution.py:76
  253.2 11.4 %all-to-all-start.12 = ((f32[4,256,128]{2,1,0:T(8,128)}), f32[4,256,128]{2,1,0:T(8,128)S(1)}, u32[]{:S(2)}, u32[]{:S(2)}) async-start(f32[4,256,128]{2,1,0:T(8,128)} %bitcast.46), calls=%async_computation.12 | async-start | bytes 1048576 | tf_op jit(solution)/shard_map/all_to_all | solution.py:76
  299.6 5.1 %copy-start.1 = (bf16[1024,128]{1,0:T(8,128)(2,1)S(1)}, bf16[1024,128]{1,0:T(8,128)(2,1)}, u32[]{:S(2)}) copy-start(bf16[1024,128]{1,0:T(8,128)(2,1)} %get-tuple-element.8) | copy-start | bytes 786436
  301.2 18.8 %all-to-all-start.15 = ((f32[8,128,128]{2,1,0:T(8,128)}), f32[8,128,128]{2,1,0:T(8,128)S(1)}, u32[]{:S(2)}, u32[]{:S(2)}) async-start(f32[8,128,128]{2,1,0:T(8,128)} %copy.41), calls=%async_computation.15 | async-start | bytes 1048576 | tf_op jit(solution)/shard_map/all_to_all | solution.py:89
  322.3 11.4 %all-to-all-start.16 = ((f32[4,256,128]{2,1,0:T(8,128)}), f32[4,256,128]{2,1,0:T(8,128)S(1)}, u32[]{:S(2)}, u32[]{:S(2)}) async-start(f32[4,256,128]{2,1,0:T(8,128)} %bitcast.55), calls=%async_computation.16 | async-start | bytes 1048576 | tf_op jit(solution)/shard_map/all_to_all | solution.py:76
Sparse Core Ops, SparseCore 0:
  9.8 2.7 sort.21.cloned.1.call-done
  (1 shorter events, 0.0 us)

commit v2 on v1

--- a/solution.py
+++ b/solution.py
@@ -48,12 +48,17 @@
     lists = jnp.stack([up_map[1, 0], up_map[0, 0], down_map[0, 0], down_map[1, 0]])
     owner = lists // per_owner
     slot = lists % per_owner
-    order = jnp.argsort(owner, axis=1, stable=True)
-    sent_slots = jnp.take_along_axis(slot, order, axis=1).reshape(4, shard_count, per_peer)
-    arrived = lax.all_to_all(sent_slots, "shard", 1, 1, tiled=True).reshape(4, block_count)
-    is_owner = owner[:, :, None] == jnp.arange(shard_count, dtype=jnp.int32)[None, None, :]
-    rank = jnp.sum(jnp.where(is_owner, jnp.cumsum(is_owner.astype(jnp.int32), axis=1), 0), axis=2)
-    position = owner * per_peer + rank - 1
+    blocks = jnp.broadcast_to(jnp.arange(block_count, dtype=jnp.int32), lists.shape)
+    _, sent_slots, order = lax.sort((owner, slot, blocks), dimension=1, num_keys=1, is_stable=True)
+    arrived = lax.all_to_all(
+        sent_slots.reshape(4, shard_count, per_peer), "shard", 1, 1, tiled=True
+    ).reshape(4, block_count)
+    position = lax.sort((order, blocks), dimension=1, num_keys=1)[1]
+    moves = lax.sort(
+        (jnp.stack([position[1], position[3]]), jnp.stack([position[3], position[1]])),
+        dimension=1,
+        num_keys=1,
+    )[1]
 
     def send(sorted_rows, which):
         partial_sum = jnp.sum(sorted_rows)
@@ -99,7 +104,7 @@
     scaled1 = send(t2_up1, 0)
     incoming1 = jnp.exp(route(jnp.log(scaled1), sel[1].T))
     t1_down1 = gather_rows(t1, order[3]) * fetch(incoming1, 3)
-    t1_up0 = gather_rows(t1_down1, jnp.take(position[3], order[1]))
+    t1_up0 = gather_rows(t1_down1, moves[0])
     scaled0 = send(t1_up0, 1)
     incoming0 = jnp.exp(route(jnp.log(scaled0), sel[0].T))
     t0_down0 = gather_rows(t0, order[2]) * fetch(incoming0, 2)
@@ -108,7 +113,7 @@
     update0 = route(fresh0, sel[0]) / scaled0
     t1_up0 = t1_up0 * fetch(update0, 1)
     out1 = gather_rows(t1_up0, position[1])
-    t1_down1 = gather_rows(t1_up0, jnp.take(position[1], order[3]))
+    t1_down1 = gather_rows(t1_up0, moves[1])
     fresh1 = send(t1_down1, 3)
     update1 = route(fresh1, sel[1]) / scaled1
     t2_up1 = t2_up1 * fetch(update1, 0)

time: 345 us -> 307 us (0.89)
  local copies, waits for them, and re-layouts: 55.2 us -> 20.5 us
  blocking collectives: 123 us -> 134 us
  other arithmetic: 25 us -> 18 us
  starting transfers between devices: 34.6 us -> 31 us
    gather x4 -> x0, local copies, waits for them, and re-layouts: 44.1 us -> none  [the longest x2 35 us: shards(): jnp.take_along_axis(slot, order, axis=1).reshape(4, shard_count, per_peer)]
    all_to_all x0 -> x1, blocking collectives: none -> 10.8 us  [fetch(): lax.all_to_all(picked.reshape(shard_count, per_peer, lane_count), 'shard'...]
    sort x2 -> x6, local copies, waits for them, and re-layouts: 1.53 us -> 9.02 us  [the longest x2 7.24 us: shards(): position = lax.sort((order, blocks), dimension=1, num_keys=1)[1]]
    all_to_all x1, waiting for transfers between devices: 9.62 us -> 15.3 us  [route(): lax.all_to_all(pieces, 'clique', split_axis=0, concat_axis=0, tiled=True)]
    all_to_all x2, waiting for transfers between devices: 24.3 us -> 19.6 us  [route(): lax.all_to_all(combined, 'clique', split_axis=0, concat_axis=0, tiled=True)]
    another operation x18 -> x16, other arithmetic: 12.9 us -> 8.16 us
    all_to_all x4 -> x3, waiting for transfers between devices: 20.8 us -> 16.9 us  [fetch(): lax.all_to_all(picked.reshape(shard_count, per_peer, lane_count), 'shard'...]
    all_to_all x4 -> x3, starting transfers between devices: 14.1 us -> 10.4 us  [fetch(): lax.all_to_all(picked.reshape(shard_count, per_peer, lane_count), 'shard'...]
  transfers between devices with their start and end apart: 9 -> 8, of which waited for: 9 -> 8; matrix products, arithmetic and copies ran while one was open for 8% -> 5% of each run, Pallas kernels for 0% -> 0%
where the time goes in v2:
time: 307 us; the launch traced here: 305 us
  blocking collectives  134 us (44%)
  waiting for transfers between devices  60.1 us (20%)
  starting transfers between devices  31 us (10%)
  matrix products  25.5 us (8%)
  local copies, waits for them, and re-layouts  20.5 us (7%)
  other arithmetic  18 us (6%)
  between operations  16.3 us (5%)
    all_to_all x3, blocking collectives, route(): lax.all_to_all(pieces, 'clique', split_axis=0, concat_axis=0, tiled=True)  56.5 us
    all_to_all x2, blocking collectives, route(): lax.all_to_all(combined, 'clique', split_axis=0, concat_axis=0, tiled=True)  35.5 us
    all_to_all x3, blocking collectives, send(): arrived_rows = lax.all_to_all(payload, 'shard', 0, 0, tiled=True)  31.1 us
    dot_general x16, matrix products, split_dot(): y = jnp.dot(one_hot, parts, preferred_element_type=jnp.float32)  22.7 us
    all_to_all x2, waiting for transfers between devices, route(): lax.all_to_all(combined, 'clique', split_axis=0, concat_axis=0, tiled=True)  19.6 us
    all_to_all x3, waiting for transfers between devices, fetch(): lax.all_to_all(picked.reshape(shard_count, per_peer, lane_count), 'shard'...  16.9 us
    all_to_all x1, waiting for transfers between devices, route(): lax.all_to_all(pieces, 'clique', split_axis=0, concat_axis=0, tiled=True)  15.3 us
    all_to_all x1, blocking collectives, fetch(): lax.all_to_all(picked.reshape(shard_count, per_peer, lane_count), 'shard'...  10.8 us
  transfers between devices with their start and end apart: 8, of which 8 were waited for; matrix products, arithmetic and copies ran while one was open for 5% of the time, Pallas kernels for 0%

profile of v2, /device:TPU:0, one launch (start us, length us, event | category | flops | bytes accessed | tf_op | source)
XLA Modules:
  0.0 305.3 jit_solution(1797807782991963589)
XLA Ops:
  8.6 2.7 reduce-precision_convert_fusion.29
  11.3 1.7 sort.55.cloned.1.call-done
  13.9 5.2 %all-to-all-start = ((s32[4,4,256]{2,0,1:T(4,128)}), s32[4,4,256]{2,0,1:T(4,128)S(1)}, u32[]{:S(2)}, u32[]{:S(2)}) async-start(s32[4,4,256]{2,0,1:T(4,128)} %bitcast.174), calls=%async_computation | async-start | bytes 32768 | tf_op jit(solution)/shard_map/all_to_all | solution.py:53
  19.1 1.3 fusion.8
  21.2 1.5 concatenate.76
  22.7 1.1 all-to-all-done
  23.8 3.5 %all-to-all-start.1 = ((f32[4,264,128]{2,1,0:T(8,128)}), f32[4,264,128]{2,1,0:T(8,128)S(1)}, u32[]{:S(2)}, u32[]{:S(2)}) async-start(f32[4,264,128]{2,1,0:T(8,128)} %concatenate.76), calls=%async_computation.1 | async-start | bytes 1081344 | tf_op jit(solution)/shard_map/all_to_all | solution.py:72
  27.3 7.2 %all-to-all-done.1 = f32[4,264,128]{2,1,0:T(8,128)S(1)} async-done(((f32[4,264,128]{2,1,0:T(8,128)}), f32[4,264,128]{2,1,0:T(8,128)S(1)}, u32[]{:S(2)}, u32[]{:S(2)}) %all-to-all-start.1) | async-done | bytes 540704 | tf_op jit(solution)/shard_map/all_to_all | solution.py:72
  36.0 1.3 fusion.7
  38.2 4.9 %all-to-all-start.2 = ((f32[8,128,128]{2,1,0:T(8,128)}), f32[8,128,128]{2,1,0:T(8,128)S(1)}, u32[]{:S(2)}, u32[]{:S(2)}) async-start(f32[8,128,128]{2,1,0:T(8,128)} %bitcast.23), calls=%async_computation.2 | async-start | bytes 1048576 | tf_op jit(solution)/shard_map/all_to_all | solution.py:91
  43.1 15.3 %all-to-all-done.2 = f32[8,128,128]{2,1,0:T(8,128)S(1)} async-done(((f32[8,128,128]{2,1,0:T(8,128)}), f32[8,128,128]{2,1,0:T(8,128)S(1)}, u32[]{:S(2)}, u32[]{:S(2)}) %all-to-all-start.2) | async-done | bytes 524320 | tf_op jit(solution)/shard_map/all_to_all | solution.py:91
  60.0 3.5 %all-to-all-start.3 = ((f32[8,128,128]{2,1,0:T(8,128)}), f32[8,128,128]{2,1,0:T(8,128)S(1)}, u32[]{:S(2)}, u32[]{:S(2)}) async-start(f32[8,128,128]{2,1,0:T(8,128)} %copy.19), calls=%async_computation.3 | async-start | bytes 1048576 | tf_op jit(solution)/shard_map/all_to_all | solution.py:94
  64.3 7.2 %sort.57.cloned.1.call-done = (s32[4,1024]{1,0:T(4,128)}, s32[4,1024]{1,0:T(4,128)}) async-done(((s32[4,1024]{1,0:T(4,128)}, s32[4,1024]{1,0:T(4,128)}), (s32[4,1024]{1,0:T(4,128)}, s32[4,1024]{1,0:T(4,128)})) %sort.57.cloned.1.call-update) | async-done | bytes 32784 | tf_op jit(solution)/shard_map/sort | solution.py:56
  73.0 5.7 %all-to-all-done.3 = f32[8,128,128]{2,1,0:T(8,128)S(1)} async-done(((f32[8,128,128]{2,1,0:T(8,128)}), f32[8,128,128]{2,1,0:T(8,128)S(1)}, u32[]{:S(2)}, u32[]{:S(2)}) %all-to-all-start.3) | async-done | bytes 524320 | tf_op jit(solution)/shard_map/all_to_all | solution.py:94
  79.0 1.3 fusion.6
  80.4 1.0 copy.20
  81.4 3.5 %all-to-all-start.4 = ((f32[4,256,128]{1,2,0:T(8,128)}), f32[4,256,128]{1,2,0:T(8,128)S(1)}, u32[]{:S(2)}, u32[]{:S(2)}) async-start(f32[4,256,128]{1,2,0:T(8,128)} %copy.20), calls=%async_computation.4 | async-start | bytes 1048576 | tf_op jit(solution)/shard_map/all_to_all | solution.py:81
  84.8 2.3 fusion.5
  88.0 4.8 %all-to-all-done.4 = f32[4,256,128]{1,2,0:T(8,128)S(1)} async-done(((f32[4,256,128]{1,2,0:T(8,128)}), f32[4,256,128]{1,2,0:T(8,128)S(1)}, u32[]{:S(2)}, u32[]{:S(2)}) %all-to-all-start.4) | async-done | bytes 524320 | tf_op jit(solution)/shard_map/all_to_all | solution.py:81
  93.2 1.3 fusion.4
  95.9 10.6 %all_to_all.85 = f32[4,264,128]{2,1,0:T(8,128)S(1)} all-to-all(f32[4,264,128]{2,1,0:T(8,128)S(1)} %concatenate.80), channel_id=1, replica_groups=mesh['clique'=8,'shard'=4] {'shard'}, dimensions={0} | all-to-all | bytes 1081344 | tf_op jit(solution)/shard_map/all_to_all | solution.py:72
  107.9 1.2 fusion.3
  109.3 18.8 %all_to_all.86 = f32[8,128,128]{2,1,0:T(8,128)S(1)} all-to-all(f32[8,128,128]{2,1,0:T(8,128)S(1)} %bitcast.171), channel_id=1, replica_groups=mesh['clique'=8,'shard'=4] {'clique'}, dimensions={0} | all-to-all | bytes 1048576 | tf_op jit(solution)/shard_map/all_to_all | solution.py:91
  129.0 17.7 %all_to_all.87 = f32[8,128,128]{2,1,0:T(8,128)S(1)} all-to-all(f32[8,128,128]{2,1,0:T(8,128)S(1)} %copy.24), channel_id=1, replica_groups=mesh['clique'=8,'shard'=4] {'clique'}, dimensions={0} | all-to-all | bytes 1048576 | tf_op jit(solution)/shard_map/all_to_all | solution.py:94
  147.0 1.3 fusion.2
  149.2 3.5 %all-to-all-start.8 = ((f32[4,256,128]{2,1,0:T(8,128)}), f32[4,256,128]{2,1,0:T(8,128)S(1)}, u32[]{:S(2)}, u32[]{:S(2)}) async-start(f32[4,256,128]{2,1,0:T(8,128)} %bitcast.30), calls=%async_computation.8 | async-start | bytes 1048576 | tf_op jit(solution)/shard_map/all_to_all | solution.py:81
  152.7 2.4 fusion.1
  155.1 5.4 %all-to-all-done.8 = f32[4,256,128]{2,1,0:T(8,128)S(1)} async-done(((f32[4,256,128]{2,1,0:T(8,128)}), f32[4,256,128]{2,1,0:T(8,128)S(1)}, u32[]{:S(2)}, u32[]{:S(2)}) %all-to-all-start.8) | async-done | bytes 524320 | tf_op jit(solution)/shard_map/all_to_all | solution.py:81
  160.5 2.2 reduce-precision_convert_fusion.13
  164.1 10.5 %all_to_all.88 = f32[4,264,128]{2,1,0:T(8,128)S(1)} all-to-all(f32[4,264,128]{2,1,0:T(8,128)S(1)} %concatenate.84), channel_id=1, replica_groups=mesh['clique'=8,'shard'=4] {'shard'}, dimensions={0} | all-to-all | bytes 1081344 | tf_op jit(solution)/shard_map/all_to_all | solution.py:72
  176.1 1.3 fusion.11
  177.4 18.8 %all_to_all.89 = f32[8,128,128]{2,1,0:T(8,128)S(1)} all-to-all(f32[8,128,128]{2,1,0:T(8,128)S(1)} %bitcast.166), channel_id=1, replica_groups=mesh['clique'=8,'shard'=4] {'clique'}, dimensions={0} | all-to-all | bytes 1048576 | tf_op jit(solution)/shard_map/all_to_all | solution.py:91
  197.0 17.7 %all_to_all.90 = f32[8,128,128]{2,1,0:T(8,128)S(1)} all-to-all(f32[8,128,128]{2,1,0:T(8,128)S(1)} %copy.26), channel_id=1, replica_groups=mesh['clique'=8,'shard'=4] {'clique'}, dimensions={0} | all-to-all | bytes 1048576 | tf_op jit(solution)/shard_map/all_to_all | solution.py:94
  215.0 1.3 fusion.10
  216.4 10.8 %all_to_all.91 = f32[4,256,128]{2,1,0:T(8,128)S(1)} all-to-all(f32[4,256,128]{2,1,0:T(8,128)S(1)} %bitcast.173), channel_id=1, replica_groups=mesh['clique'=8,'shard'=4] {'shard'}, dimensions={0} | all-to-all | bytes 1048576 | tf_op jit(solution)/shard_map/all_to_all | solution.py:81
  227.4 1.3 fusion.15
  230.1 10.1 %all_to_all.92 = f32[4,264,128]{2,1,0:T(8,128)S(1)} all-to-all(f32[4,264,128]{2,1,0:T(8,128)S(1)} %concatenate.88), channel_id=1, replica_groups=mesh['clique'=8,'shard'=4] {'shard'}, dimensions={0} | all-to-all | bytes 1081344 | tf_op jit(solution)/shard_map/all_to_all | solution.py:72
  241.6 1.2 fusion.14
  243.0 18.9 %all_to_all.93 = f32[8,128,128]{2,1,0:T(8,128)S(1)} all-to-all(f32[8,128,128]{2,1,0:T(8,128)S(1)} %bitcast.167), channel_id=1, replica_groups=mesh['clique'=8,'shard'=4] {'clique'}, dimensions={0} | all-to-all | bytes 1048576 | tf_op jit(solution)/shard_map/all_to_all | solution.py:91
  263.4 3.5 %all-to-all-start.15 = ((f32[8,128,128]{2,1,0:T(8,128)}), f32[8,128,128]{2,1,0:T(8,128)S(1)}, u32[]{:S(2)}, u32[]{:S(2)}) async-start(f32[8,128,128]{2,1,0:T(8,128)} %copy.28), calls=%async_computation.15 | async-start | bytes 1048576 | tf_op jit(solution)/shard_map/all_to_all | solution.py:94
  266.9 1.3 fusion
  268.3 13.9 %all-to-all-done.15 = f32[8,128,128]{2,1,0:T(8,128)S(1)} async-done(((f32[8,128,128]{2,1,0:T(8,128)}), f32[8,128,128]{2,1,0:T(8,128)S(1)}, u32[]{:S(2)}, u32[]{:S(2)}) %all-to-all-start.15) | async-done | bytes 524320 | tf_op jit(solution)/shard_map/all_to_all | solution.py:94
  282.4 1.3 fusion.13
  284.6 3.5 %all-to-all-start.16 = ((f32[4,256,128]{2,1,0:T(8,128)}), f32[4,256,128]{2,1,0:T(8,128)S(1)}, u32[]{:S(2)}, u32[]{:S(2)}) async-start(f32[4,256,128]{2,1,0:T(8,128)} %bitcast.49), calls=%async_computation.16 | async-start | bytes 1048576 | tf_op jit(solution)/shard_map/all_to_all | solution.py:81
  288.0 1.3 fusion.9
  289.4 6.6 %all-to-all-done.16 = f32[4,256,128]{2,1,0:T(8,128)S(1)} async-done(((f32[4,256,128]{2,1,0:T(8,128)}), f32[4,256,128]{2,1,0:T(8,128)S(1)}, u32[]{:S(2)}, u32[]{:S(2)}) %all-to-all-start.16) | async-done | bytes 524320 | tf_op jit(solution)/shard_map/all_to_all | solution.py:81
  296.2 1.3 fusion.12
  297.5 1.2 maximum_bitcast_fusion
  (74 shorter events, 23.7 us)
Async XLA Ops:
  6.5 6.5 %sort.55.cloned.1.call-start = ((), (), s32[]{:S(2)}) async-start(), calls=%async_computation.17 | async-start | bytes 147488 | tf_op jit(solution)/shard_map/sort | solution.py:52
  13.9 9.9 %all-to-all-start = ((s32[4,4,256]{2,0,1:T(4,128)}), s32[4,4,256]{2,0,1:T(4,128)S(1)}, u32[]{:S(2)}, u32[]{:S(2)}) async-start(s32[4,4,256]{2,0,1:T(4,128)} %bitcast.174), calls=%async_computation | async-start | bytes 32768 | tf_op jit(solution)/shard_map/all_to_all | solution.py:53
  23.8 10.7 %all-to-all-start.1 = ((f32[4,264,128]{2,1,0:T(8,128)}), f32[4,264,128]{2,1,0:T(8,128)S(1)}, u32[]{:S(2)}, u32[]{:S(2)}) async-start(f32[4,264,128]{2,1,0:T(8,128)} %concatenate.76), calls=%async_computation.1 | async-start | bytes 1081344 | tf_op jit(solution)/shard_map/all_to_all | solution.py:72
  37.3 5.8 %copy-start.3 = (s32[2,8]{1,0:T(2,128)S(1)}, s32[2,8]{1,0:T(2,128)}, u32[]{:S(2)}) copy-start(s32[2,8]{1,0:T(2,128)} %param.7) | copy-start | bytes 196
  38.2 20.2 %all-to-all-start.2 = ((f32[8,128,128]{2,1,0:T(8,128)}), f32[8,128,128]{2,1,0:T(8,128)S(1)}, u32[]{:S(2)}, u32[]{:S(2)}) async-start(f32[8,128,128]{2,1,0:T(8,128)} %bitcast.23), calls=%async_computation.2 | async-start | bytes 1048576 | tf_op jit(solution)/shard_map/all_to_all | solution.py:91
  60.0 18.8 %all-to-all-start.3 = ((f32[8,128,128]{2,1,0:T(8,128)}), f32[8,128,128]{2,1,0:T(8,128)S(1)}, u32[]{:S(2)}, u32[]{:S(2)}) async-start(f32[8,128,128]{2,1,0:T(8,128)} %copy.19), calls=%async_computation.3 | async-start | bytes 1048576 | tf_op jit(solution)/shard_map/all_to_all | solution.py:94
  63.5 8.0 %sort.57.cloned.1.call-start = ((), (), s32[]{:S(2)}) async-start(), calls=%async_computation.18 | async-start | bytes 98336 | tf_op jit(solution)/shard_map/sort | solution.py:56
  64.2 22.9 %sort.59.cloned.1.call-start = ((), (), s32[]{:S(2)}) async-start(), calls=%async_computation.19 | async-start | bytes 49184 | tf_op jit(solution)/shard_map/sort | solution.py:57
  81.4 11.4 %all-to-all-start.4 = ((f32[4,256,128]{1,2,0:T(8,128)}), f32[4,256,128]{1,2,0:T(8,128)S(1)}, u32[]{:S(2)}, u32[]{:S(2)}) async-start(f32[4,256,128]{1,2,0:T(8,128)} %copy.20), calls=%async_computation.4 | async-start | bytes 1048576 | tf_op jit(solution)/shard_map/all_to_all | solution.py:81
  148.3 4.4 %copy-start.1 = (bf16[1024,128]{1,0:T(8,128)(2,1)S(1)}, bf16[1024,128]{1,0:T(8,128)(2,1)}, u32[]{:S(2)}) copy-start(bf16[1024,128]{1,0:T(8,128)(2,1)} %get-tuple-element.30) | copy-start | bytes 786436
  148.3 4.4 %copy-start.2 = (bf16[1024,128]{1,0:T(8,128)(2,1)S(1)}, bf16[1024,128]{1,0:T(8,128)(2,1)}, u32[]{:S(2)}) copy-start(bf16[1024,128]{1,0:T(8,128)(2,1)} %get-tuple-element.31) | copy-start | bytes 786436
  149.2 11.4 %all-to-all-start.8 = ((f32[4,256,128]{2,1,0:T(8,128)}), f32[4,256,128]{2,1,0:T(8,128)S(1)}, u32[]{:S(2)}, u32[]{:S(2)}) async-start(f32[4,256,128]{2,1,0:T(8,128)} %bitcast.30), calls=%async_computation.8 | async-start | bytes 1048576 | tf_op jit(solution)/shard_map/all_to_all | solution.py:81
  261.9 5.1 %copy-start = (bf16[1024,128]{1,0:T(8,128)(2,1)S(1)}, bf16[1024,128]{1,0:T(8,128)(2,1)}, u32[]{:S(2)}) copy-start(bf16[1024,128]{1,0:T(8,128)(2,1)} %get-tuple-element.13) | copy-start | bytes 786436
  263.4 18.8 %all-to-all-start.15 = ((f32[8,128,128]{2,1,0:T(8,128)}), f32[8,128,128]{2,1,0:T(8,128)S(1)}, u32[]{:S(2)}, u32[]{:S(2)}) async-start(f32[8,128,128]{2,1,0:T(8,128)} %copy.28), calls=%async_computation.15 | async-start | bytes 1048576 | tf_op jit(solution)/shard_map/all_to_all | solution.py:94
  284.6 11.5 %all-to-all-start.16 = ((f32[4,256,128]{2,1,0:T(8,128)}), f32[4,256,128]{2,1,0:T(8,128)S(1)}, u32[]{:S(2)}, u32[]{:S(2)}) async-start(f32[4,256,128]{2,1,0:T(8,128)} %bitcast.49), calls=%async_computation.16 | async-start | bytes 1048576 | tf_op jit(solution)/shard_map/all_to_all | solution.py:81
Sparse Core Ops, SparseCore 0:
  9.8 2.8 sort.61.cloned.1.call-done
  66.8 4.4 sort.63.cloned.1.call-done
  74.0 4.4 sort.65.cloned.1.call-done
  (3 shorter events, 0.0 us)

commit v3 on v2

--- a/solution.py
+++ b/solution.py
@@ -72,19 +72,28 @@
         arrived_rows = lax.all_to_all(payload, "shard", 0, 0, tiled=True)
         total = jnp.sum(arrived_rows[:, per_peer, 0])
         rows = arrived_rows[:, :per_peer].reshape(block_count, lane_count)
-        message = segment_rows(rows, arrived[which], per_owner)
-        return message * (sep_states / total)
+        return segment_rows(rows, arrived[which], per_owner), total
 
-    def fetch(owned_rows, which):
+    def fetch(owned_rows, which, partial=None):
         owned_rows = jnp.where(jnp.isfinite(owned_rows), owned_rows, 0.0)
-        picked = gather_rows(owned_rows, arrived[which])
-        back = lax.all_to_all(
-            picked.reshape(shard_count, per_peer, lane_count), "shard", 0, 0, tiled=True
-        )
-        return back.reshape(block_count, lane_count)
+        picked = gather_rows(owned_rows, arrived[which]).reshape(shard_count, per_peer, lane_count)
+        if partial is not None:
+            picked = jnp.concatenate(
+                [picked, jnp.broadcast_to(partial, (shard_count, PAD, lane_count))], axis=1
+            )
+        back = lax.all_to_all(picked, "shard", 0, 0, tiled=True)
+        if partial is None:
+            return back.reshape(block_count, lane_count)
+        rows = back[:, :per_peer].reshape(block_count, lane_count)
+        return rows, jnp.sum(back[:, per_peer, 0])
 
-    def route(owned_rows, mixing):
-        pieces = owned_rows.reshape(clique_count, per_owner // clique_count, lane_count)
+    def route(owned_rows, mixing, partial=None):
+        piece_rows = per_owner // clique_count
+        pieces = owned_rows.reshape(clique_count, piece_rows, lane_count)
+        if partial is not None:
+            pieces = jnp.concatenate(
+                [pieces, jnp.broadcast_to(partial, (clique_count, PAD, lane_count))], axis=1
+            )
         combined = jnp.einsum(
             "oi,ixl->oxl",
             mixing,
@@ -92,7 +101,9 @@
             precision=lax.Precision.HIGHEST,
         )
         moved = lax.all_to_all(combined, "clique", split_axis=0, concat_axis=0, tiled=True)
-        return moved.reshape(per_owner, lane_count)
+        if partial is None:
+            return moved.reshape(per_owner, lane_count)
+        return moved[:, :piece_rows].reshape(per_owner, lane_count), moved[0, piece_rows, 0]
 
     clique_ids = jnp.arange(clique_count, dtype=jnp.int32)
     sel = [
@@ -100,21 +111,28 @@
     ]
     t0, t1, t2 = tables[0, 0], tables[1, 0], tables[2, 0]
 
+    t0_down0 = gather_rows(t0, order[2])
+    down0_message, _ = send(t0_down0, 2)
+
     t2_up1 = gather_rows(t2, order[0])
-    scaled1 = send(t2_up1, 0)
+    message, total = send(t2_up1, 0)
+    scaled1 = message * (sep_states / total)
     incoming1 = jnp.exp(route(jnp.log(scaled1), sel[1].T))
     t1_down1 = gather_rows(t1, order[3]) * fetch(incoming1, 3)
     t1_up0 = gather_rows(t1_down1, moves[0])
-    scaled0 = send(t1_up0, 1)
+    message, total = send(t1_up0, 1)
+    scaled0 = message * (sep_states / total)
     incoming0 = jnp.exp(route(jnp.log(scaled0), sel[0].T))
-    t0_down0 = gather_rows(t0, order[2]) * fetch(incoming0, 2)
-    out0 = gather_rows(t0_down0, position[2])
-    fresh0 = send(t0_down0, 2)
-    update0 = route(fresh0, sel[0]) / scaled0
-    t1_up0 = t1_up0 * fetch(update0, 1)
+    incoming0 = jnp.where(jnp.isfinite(incoming0), incoming0, 0.0)
+    out0 = gather_rows(t0_down0 * fetch(incoming0, 2), position[2])
+    fresh0 = down0_message * incoming0
+    from_parent, partial = route(fresh0, sel[0], jnp.sum(fresh0))
+    update0, total = fetch(from_parent / scaled0, 1, partial)
+    t1_up0 = t1_up0 * (update0 * (sep_states / total))
     out1 = gather_rows(t1_up0, position[1])
     t1_down1 = gather_rows(t1_up0, moves[1])
-    fresh1 = send(t1_down1, 3)
+    message, total = send(t1_down1, 3)
+    fresh1 = message * (sep_states / total)
     update1 = route(fresh1, sel[1]) / scaled1
     t2_up1 = t2_up1 * fetch(update1, 0)
     out2 = gather_rows(t2_up1, position[0])

time: 307 us -> 312 us (1.016)
  no operation moved by 1% of the time
where the time goes in v3:
time: 312 us; the launch traced here: 310 us
  blocking collectives  136 us (44%)
  waiting for transfers between devices  59.1 us (19%)
  starting transfers between devices  31 us (10%)
  matrix products  26.3 us (8%)
  local copies, waits for them, and re-layouts  22.4 us (7%)
  other arithmetic  19.4 us (6%)
  between operations  16.4 us (5%)
    all_to_all x3, blocking collectives, route(): lax.all_to_all(pieces, 'clique', split_axis=0, concat_axis=0, tiled=True)  56.1 us
    all_to_all x2, blocking collectives, route(): lax.all_to_all(combined, 'clique', split_axis=0, concat_axis=0, tiled=True)  36.1 us
    all_to_all x3, blocking collectives, send(): arrived_rows = lax.all_to_all(payload, 'shard', 0, 0, tiled=True)  31.7 us
    dot_general x16, matrix products, split_dot(): y = jnp.dot(one_hot, parts, preferred_element_type=jnp.float32)  23.7 us
    all_to_all x2, waiting for transfers between devices, route(): lax.all_to_all(combined, 'clique', split_axis=0, concat_axis=0, tiled=True)  19.6 us
    all_to_all x3, waiting for transfers between devices, fetch(): back = lax.all_to_all(picked, 'shard', 0, 0, tiled=True)  15.8 us
    all_to_all x1, waiting for transfers between devices, route(): lax.all_to_all(pieces, 'clique', split_axis=0, concat_axis=0, tiled=True)  15.3 us
    all_to_all x1, blocking collectives, fetch(): back = lax.all_to_all(picked, 'shard', 0, 0, tiled=True)  11.8 us
  transfers between devices with their start and end apart: 8, of which 8 were waited for; matrix products, arithmetic and copies ran while one was open for 5% of the time, Pallas kernels for 0%

profile of v3, /device:TPU:0, one launch (start us, length us, event | category | flops | bytes accessed | tf_op | source)
XLA Modules:
  0.0 310.2 jit_solution(9427646195823119263)
XLA Ops:
  8.6 2.7 reduce-precision_convert_fusion.29
  11.3 1.8 sort.55.cloned.1.call-done
  13.9 5.2 %all-to-all-start = ((s32[4,4,256]{2,0,1:T(4,128)}), s32[4,4,256]{2,0,1:T(4,128)S(1)}, u32[]{:S(2)}, u32[]{:S(2)}) async-start(s32[4,4,256]{2,0,1:T(4,128)} %bitcast.186), calls=%async_computation | async-start | bytes 32768 | tf_op jit(solution)/shard_map/all_to_all | solution.py:53
  19.1 1.3 fusion.8
  21.1 1.5 concatenate.82
  22.6 1.2 all-to-all-done
  23.8 3.5 %all-to-all-start.1 = ((f32[4,264,128]{2,1,0:T(8,128)}), f32[4,264,128]{2,1,0:T(8,128)S(1)}, u32[]{:S(2)}, u32[]{:S(2)}) async-start(f32[4,264,128]{2,1,0:T(8,128)} %concatenate.82), calls=%async_computation.1 | async-start | bytes 1081344 | tf_op jit(solution)/shard_map/all_to_all | solution.py:72
  27.3 7.1 %all-to-all-done.1 = f32[4,264,128]{2,1,0:T(8,128)S(1)} async-done(((f32[4,264,128]{2,1,0:T(8,128)}), f32[4,264,128]{2,1,0:T(8,128)S(1)}, u32[]{:S(2)}, u32[]{:S(2)}) %all-to-all-start.1) | async-done | bytes 540704 | tf_op jit(solution)/shard_map/all_to_all | solution.py:72
  35.9 1.3 fusion.7
  38.1 4.9 %all-to-all-start.2 = ((f32[8,128,128]{2,1,0:T(8,128)}), f32[8,128,128]{2,1,0:T(8,128)S(1)}, u32[]{:S(2)}, u32[]{:S(2)}) async-start(f32[8,128,128]{2,1,0:T(8,128)} %bitcast.23), calls=%async_computation.2 | async-start | bytes 1048576 | tf_op jit(solution)/shard_map/all_to_all | solution.py:100
  43.0 15.3 %all-to-all-done.2 = f32[8,128,128]{2,1,0:T(8,128)S(1)} async-done(((f32[8,128,128]{2,1,0:T(8,128)}), f32[8,128,128]{2,1,0:T(8,128)S(1)}, u32[]{:S(2)}, u32[]{:S(2)}) %all-to-all-start.2) | async-done | bytes 524320 | tf_op jit(solution)/shard_map/all_to_all | solution.py:100
  59.9 3.5 %all-to-all-start.3 = ((f32[8,128,128]{2,1,0:T(8,128)}), f32[8,128,128]{2,1,0:T(8,128)S(1)}, u32[]{:S(2)}, u32[]{:S(2)}) async-start(f32[8,128,128]{2,1,0:T(8,128)} %copy.19), calls=%async_computation.3 | async-start | bytes 1048576 | tf_op jit(solution)/shard_map/all_to_all | solution.py:103
  64.2 7.2 %sort.57.cloned.1.call-done = (s32[4,1024]{1,0:T(4,128)}, s32[4,1024]{1,0:T(4,128)}) async-done(((s32[4,1024]{1,0:T(4,128)}, s32[4,1024]{1,0:T(4,128)}), (s32[4,1024]{1,0:T(4,128)}, s32[4,1024]{1,0:T(4,128)})) %sort.57.cloned.1.call-update) | async-done | bytes 32784 | tf_op jit(solution)/shard_map/sort | solution.py:56
  72.9 5.8 %all-to-all-done.3 = f32[8,128,128]{2,1,0:T(8,128)S(1)} async-done(((f32[8,128,128]{2,1,0:T(8,128)}), f32[8,128,128]{2,1,0:T(8,128)S(1)}, u32[]{:S(2)}, u32[]{:S(2)}) %all-to-all-start.3) | async-done | bytes 524320 | tf_op jit(solution)/shard_map/all_to_all | solution.py:103
  78.9 1.3 fusion.6
  81.3 3.5 %all-to-all-start.4 = ((f32[4,256,128]{1,2,0:T(8,128)}), f32[4,256,128]{1,2,0:T(8,128)S(1)}, u32[]{:S(2)}, u32[]{:S(2)}) async-start(f32[4,256,128]{1,2,0:T(8,128)} %copy.20), calls=%async_computation.4 | async-start | bytes 1048576 | tf_op jit(solution)/shard_map/all_to_all | solution.py:84
  84.8 2.3 fusion.5
  87.9 4.8 %all-to-all-done.4 = f32[4,256,128]{1,2,0:T(8,128)S(1)} async-done(((f32[4,256,128]{1,2,0:T(8,128)}), f32[4,256,128]{1,2,0:T(8,128)S(1)}, u32[]{:S(2)}, u32[]{:S(2)}) %all-to-all-start.4) | async-done | bytes 524320 | tf_op jit(solution)/shard_map/all_to_all | solution.py:84
  93.1 1.3 fusion.4
  95.8 10.6 %all_to_all.85 = f32[4,264,128]{2,1,0:T(8,128)S(1)} all-to-all(f32[4,264,128]{2,1,0:T(8,128)S(1)} %concatenate.86), channel_id=1, replica_groups=mesh['clique'=8,'shard'=4] {'shard'}, dimensions={0} | all-to-all | bytes 1081344 | tf_op jit(solution)/shard_map/all_to_all | solution.py:72
  107.9 1.3 fusion.3
  109.2 18.8 %all_to_all.86 = f32[8,128,128]{2,1,0:T(8,128)S(1)} all-to-all(f32[8,128,128]{2,1,0:T(8,128)S(1)} %bitcast.182), channel_id=1, replica_groups=mesh['clique'=8,'shard'=4] {'clique'}, dimensions={0} | all-to-all | bytes 1048576 | tf_op jit(solution)/shard_map/all_to_all | solution.py:100
  128.9 17.7 %all_to_all.87 = f32[8,128,128]{2,1,0:T(8,128)S(1)} all-to-all(f32[8,128,128]{2,1,0:T(8,128)S(1)} %copy.24), channel_id=1, replica_groups=mesh['clique'=8,'shard'=4] {'clique'}, dimensions={0} | all-to-all | bytes 1048576 | tf_op jit(solution)/shard_map/all_to_all | solution.py:103
  146.9 1.3 fusion.2
  149.1 3.5 %all-to-all-start.8 = ((f32[4,256,128]{2,1,0:T(8,128)}), f32[4,256,128]{2,1,0:T(8,128)S(1)}, u32[]{:S(2)}, u32[]{:S(2)}) async-start(f32[4,256,128]{2,1,0:T(8,128)} %bitcast.180), calls=%async_computation.8 | async-start | bytes 1048576 | tf_op jit(solution)/shard_map/all_to_all | solution.py:84
  152.6 3.5 %fusion.1 = f32[1024,384]{1,0:T(8,128)} fusion(s32[1024]{0:T(1024)S(1)} %bitcast.188, bf16[1024,128]{1,0:T(8,128)(2,1)} %get-tuple-element.32, bf16[1024,128]{1,0:T(8,128)(2,1)} %get-tuple-element.33, bf16[1024,128]{1,0:T(8,128)(2,1)S(1)} %get-tuple-element.29), kind=kOutput, calls=%fused_computation.17 | convolution fusion | flops 808714240 | bytes 2363392 | tf_op jit(solution)/shard_map/dot_general | solution.py:17
  156.0 4.4 %all-to-all-done.8 = f32[4,256,128]{2,1,0:T(8,128)S(1)} async-done(((f32[4,256,128]{2,1,0:T(8,128)}), f32[4,256,128]{2,1,0:T(8,128)S(1)}, u32[]{:S(2)}, u32[]{:S(2)}) %all-to-all-start.8) | async-done | bytes 524320 | tf_op jit(solution)/shard_map/all_to_all | solution.py:84
  160.5 2.2 reduce-precision_convert_fusion.13
  162.6 1.4 reduce-precision_convert_fusion.12
  164.8 10.5 %all_to_all.88 = f32[4,264,128]{2,1,0:T(8,128)S(1)} all-to-all(f32[4,264,128]{2,1,0:T(8,128)S(1)} %concatenate.90), channel_id=1, replica_groups=mesh['clique'=8,'shard'=4] {'shard'}, dimensions={0} | all-to-all | bytes 1081344 | tf_op jit(solution)/shard_map/all_to_all | solution.py:72
  175.4 1.2 fusion.11
  178.2 19.5 %all_to_all.89 = f32[8,136,128]{2,1,0:T(8,128)S(1)} all-to-all(f32[8,136,128]{2,1,0:T(8,128)S(1)} %concatenate.92), channel_id=1, replica_groups=mesh['clique'=8,'shard'=4] {'clique'}, dimensions={0} | all-to-all | bytes 1114112 | tf_op jit(solution)/shard_map/all_to_all | solution.py:100
  198.2 18.4 %all_to_all.90 = f32[8,136,128]{2,1,0:T(8,128)S(1)} all-to-all(f32[8,136,128]{2,1,0:T(8,128)S(1)} %copy.26), channel_id=1, replica_groups=mesh['clique'=8,'shard'=4] {'clique'}, dimensions={0} | all-to-all | bytes 1114112 | tf_op jit(solution)/shard_map/all_to_all | solution.py:103
  216.9 1.3 fusion.10
  219.5 11.8 %all_to_all.91 = f32[4,264,128]{2,1,0:T(8,128)S(1)} all-to-all(f32[4,264,128]{2,1,0:T(8,128)S(1)} %concatenate.94), channel_id=1, replica_groups=mesh['clique'=8,'shard'=4] {'shard'}, dimensions={0} | all-to-all | bytes 1081344 | tf_op jit(solution)/shard_map/all_to_all | solution.py:84
  232.7 1.3 fusion.15
  235.5 10.7 %all_to_all.92 = f32[4,264,128]{2,1,0:T(8,128)S(1)} all-to-all(f32[4,264,128]{2,1,0:T(8,128)S(1)} %concatenate.96), channel_id=1, replica_groups=mesh['clique'=8,'shard'=4] {'shard'}, dimensions={0} | all-to-all | bytes 1081344 | tf_op jit(solution)/shard_map/all_to_all | solution.py:72
  247.7 1.2 fusion.14
  249.0 17.7 %all_to_all.93 = f32[8,128,128]{2,1,0:T(8,128)S(1)} all-to-all(f32[8,128,128]{2,1,0:T(8,128)S(1)} %bitcast.177), channel_id=1, replica_groups=mesh['clique'=8,'shard'=4] {'clique'}, dimensions={0} | all-to-all | bytes 1048576 | tf_op jit(solution)/shard_map/all_to_all | solution.py:100
  268.3 3.5 %all-to-all-start.15 = ((f32[8,128,128]{2,1,0:T(8,128)}), f32[8,128,128]{2,1,0:T(8,128)S(1)}, u32[]{:S(2)}, u32[]{:S(2)}) async-start(f32[8,128,128]{2,1,0:T(8,128)} %copy.28), calls=%async_computation.15 | async-start | bytes 1048576 | tf_op jit(solution)/shard_map/all_to_all | solution.py:103
  271.8 1.3 fusion
  273.2 13.9 %all-to-all-done.15 = f32[8,128,128]{2,1,0:T(8,128)S(1)} async-done(((f32[8,128,128]{2,1,0:T(8,128)}), f32[8,128,128]{2,1,0:T(8,128)S(1)}, u32[]{:S(2)}, u32[]{:S(2)}) %all-to-all-start.15) | async-done | bytes 524320 | tf_op jit(solution)/shard_map/all_to_all | solution.py:103
  287.3 1.3 fusion.13
  289.4 3.5 %all-to-all-start.16 = ((f32[4,256,128]{2,1,0:T(8,128)}), f32[4,256,128]{2,1,0:T(8,128)S(1)}, u32[]{:S(2)}, u32[]{:S(2)}) async-start(f32[4,256,128]{2,1,0:T(8,128)} %bitcast.50), calls=%async_computation.16 | async-start | bytes 1048576 | tf_op jit(solution)/shard_map/all_to_all | solution.py:84
  292.9 1.3 fusion.9
  294.3 6.6 %all-to-all-done.16 = f32[4,256,128]{2,1,0:T(8,128)S(1)} async-done(((f32[4,256,128]{2,1,0:T(8,128)}), f32[4,256,128]{2,1,0:T(8,128)S(1)}, u32[]{:S(2)}, u32[]{:S(2)}) %all-to-all-start.16) | async-done | bytes 524320 | tf_op jit(solution)/shard_map/all_to_all | solution.py:84
  301.1 1.3 fusion.12
  302.4 1.2 maximum_bitcast_fusion
  (77 shorter events, 26.3 us)
Async XLA Ops:
  6.5 6.5 %sort.55.cloned.1.call-start = ((), (), s32[]{:S(2)}) async-start(), calls=%async_computation.17 | async-start | bytes 147488 | tf_op jit(solution)/shard_map/sort | solution.py:52
  13.9 9.9 %all-to-all-start = ((s32[4,4,256]{2,0,1:T(4,128)}), s32[4,4,256]{2,0,1:T(4,128)S(1)}, u32[]{:S(2)}, u32[]{:S(2)}) async-start(s32[4,4,256]{2,0,1:T(4,128)} %bitcast.186), calls=%async_computation | async-start | bytes 32768 | tf_op jit(solution)/shard_map/all_to_all | solution.py:53
  23.8 10.6 %all-to-all-start.1 = ((f32[4,264,128]{2,1,0:T(8,128)}), f32[4,264,128]{2,1,0:T(8,128)S(1)}, u32[]{:S(2)}, u32[]{:S(2)}) async-start(f32[4,264,128]{2,1,0:T(8,128)} %concatenate.82), calls=%async_computation.1 | async-start | bytes 1081344 | tf_op jit(solution)/shard_map/all_to_all | solution.py:72
  37.2 5.8 %copy-start.2 = (s32[2,8]{1,0:T(2,128)S(1)}, s32[2,8]{1,0:T(2,128)}, u32[]{:S(2)}) copy-start(s32[2,8]{1,0:T(2,128)} %param.7) | copy-start | bytes 196
  38.1 20.2 %all-to-all-start.2 = ((f32[8,128,128]{2,1,0:T(8,128)}), f32[8,128,128]{2,1,0:T(8,128)S(1)}, u32[]{:S(2)}, u32[]{:S(2)}) async-start(f32[8,128,128]{2,1,0:T(8,128)} %bitcast.23), calls=%async_computation.2 | async-start | bytes 1048576 | tf_op jit(solution)/shard_map/all_to_all | solution.py:100
  59.9 18.8 %all-to-all-start.3 = ((f32[8,128,128]{2,1,0:T(8,128)}), f32[8,128,128]{2,1,0:T(8,128)S(1)}, u32[]{:S(2)}, u32[]{:S(2)}) async-start(f32[8,128,128]{2,1,0:T(8,128)} %copy.19), calls=%async_computation.3 | async-start | bytes 1048576 | tf_op jit(solution)/shard_map/all_to_all | solution.py:103
  63.4 8.0 %sort.57.cloned.1.call-start = ((), (), s32[]{:S(2)}) async-start(), calls=%async_computation.18 | async-start | bytes 98336 | tf_op jit(solution)/shard_map/sort | solution.py:56
  64.2 22.9 %sort.59.cloned.1.call-start = ((), (), s32[]{:S(2)}) async-start(), calls=%async_computation.19 | async-start | bytes 49184 | tf_op jit(solution)/shard_map/sort | solution.py:57
  81.3 11.4 %all-to-all-start.4 = ((f32[4,256,128]{1,2,0:T(8,128)}), f32[4,256,128]{1,2,0:T(8,128)S(1)}, u32[]{:S(2)}, u32[]{:S(2)}) async-start(f32[4,256,128]{1,2,0:T(8,128)} %copy.20), calls=%async_computation.4 | async-start | bytes 1048576 | tf_op jit(solution)/shard_map/all_to_all | solution.py:84
  149.1 11.4 %all-to-all-start.8 = ((f32[4,256,128]{2,1,0:T(8,128)}), f32[4,256,128]{2,1,0:T(8,128)S(1)}, u32[]{:S(2)}, u32[]{:S(2)}) async-start(f32[4,256,128]{2,1,0:T(8,128)} %bitcast.180), calls=%async_computation.8 | async-start | bytes 1048576 | tf_op jit(solution)/shard_map/all_to_all | solution.py:84
  266.7 5.1 %copy-start = (bf16[1024,128]{1,0:T(8,128)(2,1)S(1)}, bf16[1024,128]{1,0:T(8,128)(2,1)}, u32[]{:S(2)}) copy-start(bf16[1024,128]{1,0:T(8,128)(2,1)} %get-tuple-element.39) | copy-start | bytes 786436
  266.7 5.1 %copy-start.1 = (bf16[1024,128]{1,0:T(8,128)(2,1)S(1)}, bf16[1024,128]{1,0:T(8,128)(2,1)}, u32[]{:S(2)}) copy-start(bf16[1024,128]{1,0:T(8,128)(2,1)} %get-tuple-element.13) | copy-start | bytes 786436
  268.3 18.8 %all-to-all-start.15 = ((f32[8,128,128]{2,1,0:T(8,128)}), f32[8,128,128]{2,1,0:T(8,128)S(1)}, u32[]{:S(2)}, u32[]{:S(2)}) async-start(f32[8,128,128]{2,1,0:T(8,128)} %copy.28), calls=%async_computation.15 | async-start | bytes 1048576 | tf_op jit(solution)/shard_map/all_to_all | solution.py:103
  289.4 11.4 %all-to-all-start.16 = ((f32[4,256,128]{2,1,0:T(8,128)}), f32[4,256,128]{2,1,0:T(8,128)S(1)}, u32[]{:S(2)}, u32[]{:S(2)}) async-start(f32[4,256,128]{2,1,0:T(8,128)} %bitcast.50), calls=%async_computation.16 | async-start | bytes 1048576 | tf_op jit(solution)/shard_map/all_to_all | solution.py:84
Sparse Core Ops, SparseCore 0:
  9.8 2.9 sort.61.cloned.1.call-done
  66.7 4.3 sort.63.cloned.1.call-done
  73.9 4.4 sort.65.cloned.1.call-done
  (3 shorter events, 0.0 us)

commit v4 on v3

v4 whole, which is shorter than its diff:
```python
import jax
import jax.numpy as jnp
from jax import lax
from jax.sharding import PartitionSpec as P

SEPB = 4096
PAD = 8


def split_dot(one_hot, x, transposed=False):
    lanes = x.shape[-1]
    hi = lax.reduce_precision(x, exponent_bits=8, mantissa_bits=7)
    rest = x - hi
    mid = lax.reduce_precision(rest, exponent_bits=8, mantissa_bits=7)
    lo = rest - mid
    parts = jnp.concatenate([hi, mid, lo], axis=1).astype(jnp.bfloat16)
    contract = 0 if transposed else 1
    y = lax.dot_general(
        one_hot, parts, (((contract,), (0,)), ((), ())), preferred_element_type=jnp.float32
    )
    return (y[:, :lanes] + y[:, lanes : 2 * lanes]) + y[:, 2 * lanes :]


def one_hot_of(index, count):
    return (index[:, None] == jnp.arange(count, dtype=jnp.int32)[None, :]).astype(jnp.bfloat16)


def gather_rows(x, index):
    one_hot = (index[:, None] == jnp.arange(x.shape[0], dtype=jnp.int32)[None, :]).astype(
        jnp.bfloat16
    )
    return split_dot(one_hot, x)


def segment_rows(x, segment, count):
    one_hot = (jnp.arange(count, dtype=jnp.int32)[:, None] == segment[None, :]).astype(
        jnp.bfloat16
    )
    return split_dot(one_hot, x)


def shards(tables, up_map, down_map, parents):
    shard_count = lax.axis_size("shard")
    clique_count = lax.axis_size("clique")
    block_count = tables.shape[2]
    lane_count = tables.shape[3]
    per_owner = SEPB // shard_count
    per_peer = block_count // shard_count
    sep_states = float(SEPB * lane_count)

    lists = jnp.stack([up_map[1, 0], up_map[0, 0], down_map[0, 0], down_map[1, 0]])
    owner = lists // per_owner
    slot = lists % per_owner
    blocks = jnp.broadcast_to(jnp.arange(block_count, dtype=jnp.int32), lists.shape)
    _, sent_slots, order = lax.sort((owner, slot, blocks), dimension=1, num_keys=1, is_stable=True)
    arrived = lax.all_to_all(
        sent_slots.reshape(4, shard_count, per_peer), "shard", 1, 1, tiled=True
    ).reshape(4, block_count)
    sorting = [one_hot_of(order[which], block_count) for which in range(4)]
    down1_to_up0 = lax.dot_general(
        sorting[1], sorting[3], (((1,), (1,)), ((), ())), preferred_element_type=jnp.float32
    ).astype(jnp.bfloat16)

    def send(items):
        partial_sum = jnp.sum(items[0][0])
        chunks = [rows.reshape(shard_count, per_peer, lane_count) for rows, _ in items]
        chunks.append(jnp.broadcast_to(partial_sum, (shard_count, PAD, lane_count)))
        arrived_rows = lax.all_to_all(jnp.concatenate(chunks, axis=1), "shard", 0, 0, tiled=True)
        total = jnp.sum(arrived_rows[:, len(items) * per_peer, 0])
        messages = []
        for number, (_, which) in enumerate(items):
            rows = arrived_rows[:, number * per_peer : (number + 1) * per_peer]
            messages.append(
                segment_rows(rows.reshape(block_count, lane_count), arrived[which], per_owner)
            )
        return messages, total

    def fetch(items, partial=None):
        chunks = []
        for owned_rows, which in items:
            owned_rows = jnp.where(jnp.isfinite(owned_rows), owned_rows, 0.0)
            picked = gather_rows(owned_rows, arrived[which])
            chunks.append(picked.reshape(shard_count, per_peer, lane_count))
        if partial is not None:
            chunks.append(jnp.broadcast_to(partial, (shard_count, PAD, lane_count)))
        back = lax.all_to_all(jnp.concatenate(chunks, axis=1), "shard", 0, 0, tiled=True)
        rows = [
            back[:, number * per_peer : (number + 1) * per_peer].reshape(block_count, lane_count)
            for number in range(len(items))
        ]
        if partial is None:
            return rows, None
        return rows, jnp.sum(back[:, len(items) * per_peer, 0])

    def route(owned_rows, mixing, partial=None):
        piece_rows = per_owner // clique_count
        pieces = owned_rows.reshape(clique_count, piece_rows, lane_count)
        if partial is not None:
            pieces = jnp.concatenate(
                [pieces, jnp.broadcast_to(partial, (clique_count, PAD, lane_count))], axis=1
            )
        combined = jnp.einsum(
            "oi,ixl->oxl",
            mixing,
            lax.all_to_all(pieces, "clique", split_axis=0, concat_axis=0, tiled=True),
            precision=lax.Precision.HIGHEST,
        )
        moved = lax.all_to_all(combined, "clique", split_axis=0, concat_axis=0, tiled=True)
        if partial is None:
            return moved.reshape(per_owner, lane_count)
        return moved[:, :piece_rows].reshape(per_owner, lane_count), moved[0, piece_rows, 0]

    clique_ids = jnp.arange(clique_count, dtype=jnp.int32)
    sel = [
        (parents[edge][:, None] == clique_ids[None, :]).astype(jnp.float32) for edge in (0, 1)
    ]
    t0, t1, t2 = tables[0, 0], tables[1, 0], tables[2, 0]

    t2_up1 = split_dot(sorting[0], t2)
    t0_down0 = split_dot(sorting[2], t0)
    (message, down0_message), total = send([(t2_up1, 0), (t0_down0, 2)])
    scaled1 = message * (sep_states / total)
    incoming1 = jnp.exp(route(jnp.log(scaled1), sel[1].T))
    (picked,), _ = fetch([(incoming1, 3)])
    t1_down1 = split_dot(sorting[3], t1) * picked
    t1_up0 = split_dot(down1_to_up0, t1_down1)
    (message,), total = send([(t1_up0, 1)])
    scaled0 = message * (sep_states / total)
    incoming0 = jnp.exp(route(jnp.log(scaled0), sel[0].T))
    incoming0 = jnp.where(jnp.isfinite(incoming0), incoming0, 0.0)
    fresh0 = down0_message * incoming0
    from_parent, partial = route(fresh0, sel[0], jnp.sum(fresh0))
    (picked, update0), total = fetch([(incoming0, 2), (from_parent / scaled0, 1)], partial)
    out0 = split_dot(sorting[2], t0_down0 * picked, transposed=True)
    t1_up0 = t1_up0 * (update0 * (sep_states / total))
    out1 = split_dot(sorting[1], t1_up0, transposed=True)
    t1_down1 = split_dot(down1_to_up0, t1_up0, transposed=True)
    (message,), total = send([(t1_down1, 3)])
    fresh1 = message * (sep_states / total)
    update1 = route(fresh1, sel[1]) / scaled1
    (picked,), _ = fetch([(update1, 0)])
    out2 = split_dot(sorting[0], t2_up1 * picked, transposed=True)
    return jnp.stack([out0, out1, out2])[:, None]


def solution(mesh):
    return jax.shard_map(
        shards,
        mesh=mesh,
        in_specs=(
            P(None, "clique", "shard", None),
            P(None, "clique", "shard"),
            P(None, "clique", "shard"),
            P(),
        ),
        out_specs=P(None, "clique", "shard", None),
        check_vma=False,
    )
```

time: 312 us -> 311 us (level)
  blocking collectives: 136 us -> 93.5 us
  waiting for transfers between devices: 59.1 us -> 84.9 us
  matrix products: 26.3 us -> 36.5 us
  other arithmetic: 19.4 us -> 27.6 us
  local copies, waits for them, and re-layouts: 22.4 us -> 15.6 us
  starting transfers between devices: 31 us -> 34.9 us
    all_to_all x6 -> x3, blocking collectives: 79.7 us -> 38 us  [the longest x2 21 us: send(): lax.all_to_all(jnp.concatenate(chunks, axis=1), 'shard', 0, 0, tiled=True)]
    all_to_all x2 -> x4, waiting for transfers between devices: 19.6 us -> 45.6 us  [route(): lax.all_to_all(combined, 'clique', split_axis=0, concat_axis=0, tiled=True)]
    dot_general x16 -> x17, matrix products: 23.7 us -> 33.9 us  [the longest x16 30 us: split_dot(): lax.dot_general(one_hot, parts, (((contract,), (0,)), ((), ())), preferre...]
    sort x4 -> x0, local copies, waits for them, and re-layouts: 7.27 us -> none  [the longest x2 7.21 us: shards(): position = lax.sort((order, blocks), dimension=1, num_keys=1)[1]]
    all_to_all x2 -> x4, starting transfers between devices: 6.99 us -> 14.2 us  [route(): lax.all_to_all(combined, 'clique', split_axis=0, concat_axis=0, tiled=True)]
    another operation x16 -> x14, other arithmetic: 8.89 us -> 12.6 us
    all_to_all x4 -> x3, starting transfers between devices: 13.9 us -> 10.6 us  [the longest x2 7.12 us: fetch(): lax.all_to_all(jnp.concatenate(chunks, axis=1), 'shard', 0, 0, tiled=True)]
    all_to_all x4 -> x3, waiting for transfers between devices: 23 us -> 22.4 us  [the longest x1 12.6 us: send(): lax.all_to_all(jnp.concatenate(chunks, axis=1), 'shard', 0, 0, tiled=True)]
  transfers between devices with their start and end apart: 8 -> 9, of which waited for: 8 -> 9; matrix products, arithmetic and copies ran while one was open for 5% -> 8% of each run, Pallas kernels for 0% -> 0%
where the time goes in v4:
time: 311 us; the launch traced here: 310 us
  blocking collectives  93.5 us (30%)
  waiting for transfers between devices  84.9 us (27%)
  matrix products  36.5 us (12%)
  starting transfers between devices  34.9 us (11%)
  other arithmetic  27.6 us (9%)
  between operations  16.6 us (5%)
  local copies, waits for them, and re-layouts  15.6 us (5%)
    all_to_all x3, blocking collectives, route(): lax.all_to_all(pieces, 'clique', split_axis=0, concat_axis=0, tiled=True)  55.5 us
    all_to_all x4, waiting for transfers between devices, route(): lax.all_to_all(combined, 'clique', split_axis=0, concat_axis=0, tiled=True)  45.6 us
    dot_general x16, matrix products, split_dot(): lax.dot_general(one_hot, parts, (((contract,), (0,)), ((), ())), preferre...  30 us
    all_to_all x2, blocking collectives, send(): lax.all_to_all(jnp.concatenate(chunks, axis=1), 'shard', 0, 0, tiled=True)  21 us
    all_to_all x1, blocking collectives, fetch(): lax.all_to_all(jnp.concatenate(chunks, axis=1), 'shard', 0, 0, tiled=True)  17 us
    all_to_all x1, waiting for transfers between devices, route(): lax.all_to_all(pieces, 'clique', split_axis=0, concat_axis=0, tiled=True)  15.3 us
    all_to_all x4, starting transfers between devices, route(): lax.all_to_all(combined, 'clique', split_axis=0, concat_axis=0, tiled=True)  14.2 us
    another operation x14, other arithmetic  12.6 us
  transfers between devices with their start and end apart: 9, of which 9 were waited for; matrix products, arithmetic and copies ran while one was open for 8% of the time, Pallas kernels for 0%

profile of v4, /device:TPU:0, one launch (start us, length us, event | category | flops | bytes accessed | tf_op | source)
XLA Modules:
  0.0 309.5 jit_solution(2012349244835203448)
XLA Ops:
  8.6 2.6 reduce-precision_convert_fusion.27
  11.2 1.8 sort.23.cloned.1.call-done
  13.9 1.3 fusion.1
  15.9 5.2 %all-to-all-start = ((s32[4,4,256]{2,0,1:T(4,128)}), s32[4,4,256]{2,0,1:T(4,128)S(1)}, u32[]{:S(2)}, u32[]{:S(2)}) async-start(s32[4,4,256]{2,0,1:T(4,128)} %bitcast.6), calls=%async_computation | async-start | bytes 32768 | tf_op jit(solution)/shard_map/all_to_all | solution.py:56
  21.1 1.3 fusion.6
  24.3 1.6 all-to-all-done
  25.9 3.5 %all-to-all-start.1 = ((f32[4,520,128]{2,1,0:T(8,128)}), f32[4,520,128]{2,1,0:T(8,128)S(1)}, u32[]{:S(2)}, u32[]{:S(2)}) async-start(f32[4,520,128]{2,1,0:T(8,128)} %maximum_maximum_fusion), calls=%async_computation.1 | async-start | bytes 2129920 | tf_op jit(solution)/shard_map/all_to_all | solution.py:68
  29.4 12.6 %all-to-all-done.1 = f32[4,520,128]{2,1,0:T(8,128)S(1)} async-done(((f32[4,520,128]{2,1,0:T(8,128)}), f32[4,520,128]{2,1,0:T(8,128)S(1)}, u32[]{:S(2)}, u32[]{:S(2)}) %all-to-all-start.1) | async-done | bytes 1064992 | tf_op jit(solution)/shard_map/all_to_all | solution.py:68
  45.0 2.3 fusion.10
  48.3 4.8 %all-to-all-start.2 = ((f32[8,128,128]{2,1,0:T(8,128)}), f32[8,128,128]{2,1,0:T(8,128)S(1)}, u32[]{:S(2)}, u32[]{:S(2)}) async-start(f32[8,128,128]{2,1,0:T(8,128)} %bitcast.23), calls=%async_computation.2 | async-start | bytes 1048576 | tf_op jit(solution)/shard_map/all_to_all | solution.py:105
  53.2 15.3 %all-to-all-done.2 = f32[8,128,128]{2,1,0:T(8,128)S(1)} async-done(((f32[8,128,128]{2,1,0:T(8,128)}), f32[8,128,128]{2,1,0:T(8,128)S(1)}, u32[]{:S(2)}, u32[]{:S(2)}) %all-to-all-start.2) | async-done | bytes 524320 | tf_op jit(solution)/shard_map/all_to_all | solution.py:105
  70.2 3.5 %all-to-all-start.3 = ((f32[8,128,128]{2,1,0:T(8,128)}), f32[8,128,128]{2,1,0:T(8,128)S(1)}, u32[]{:S(2)}, u32[]{:S(2)}) async-start(f32[8,128,128]{2,1,0:T(8,128)} %copy.19), calls=%async_computation.3 | async-start | bytes 1048576 | tf_op jit(solution)/shard_map/all_to_all | solution.py:108
  73.7 2.4 fusion.2
  76.1 12.9 %all-to-all-done.3 = f32[8,128,128]{2,1,0:T(8,128)S(1)} async-done(((f32[8,128,128]{2,1,0:T(8,128)}), f32[8,128,128]{2,1,0:T(8,128)S(1)}, u32[]{:S(2)}, u32[]{:S(2)}) %all-to-all-start.3) | async-done | bytes 524320 | tf_op jit(solution)/shard_map/all_to_all | solution.py:108
  89.2 1.3 fusion.9
  91.6 3.6 %all-to-all-start.4 = ((f32[4,256,128]{1,2,0:T(8,128)}), f32[4,256,128]{1,2,0:T(8,128)S(1)}, u32[]{:S(2)}, u32[]{:S(2)}) async-start(f32[4,256,128]{1,2,0:T(8,128)} %copy.20), calls=%async_computation.4 | async-start | bytes 1048576 | tf_op jit(solution)/shard_map/all_to_all | solution.py:86
  95.2 4.0 %fusion.31 = bf16[1024,1024]{1,0:T(8,128)(2,1)} fusion(s32[1024]{0:T(1024)S(1)} %bitcast.199, s32[1024]{0:T(1024)S(1)} %bitcast.188), kind=kOutput, calls=%fused_computation.43 | convolution fusion | flops 2150629376 | bytes 2105344 | tf_op jit(solution)/shard_map/dot_general | solution.py:60
  99.2 3.8 %all-to-all-done.4 = f32[4,256,128]{1,2,0:T(8,128)S(1)} async-done(((f32[4,256,128]{1,2,0:T(8,128)}), f32[4,256,128]{1,2,0:T(8,128)S(1)}, u32[]{:S(2)}, u32[]{:S(2)}) %all-to-all-start.4) | async-done | bytes 524320 | tf_op jit(solution)/shard_map/all_to_all | solution.py:86
  103.1 1.7 reduce-precision_convert_fusion.19
  105.1 1.3 fusion.57
  107.8 10.5 %all_to_all.75 = f32[4,264,128]{2,1,0:T(8,128)S(1)} all-to-all(f32[4,264,128]{2,1,0:T(8,128)S(1)} %concatenate.83), channel_id=1, replica_groups=mesh['clique'=8,'shard'=4] {'shard'}, dimensions={0} | all-to-all | bytes 1081344 | tf_op jit(solution)/shard_map/all_to_all | solution.py:68
  119.9 1.3 fusion.8
  122.0 18.7 %all_to_all.76 = f32[8,128,128]{2,1,0:T(8,128)S(1)} all-to-all(f32[8,128,128]{2,1,0:T(8,128)S(1)} %bitcast.178), channel_id=1, replica_groups=mesh['clique'=8,'shard'=4] {'clique'}, dimensions={0} | all-to-all | bytes 1048576 | tf_op jit(solution)/shard_map/all_to_all | solution.py:105
  142.4 3.5 %all-to-all-start.7 = ((f32[8,128,128]{2,1,0:T(8,128)}), f32[8,128,128]{2,1,0:T(8,128)S(1)}, u32[]{:S(2)}, u32[]{:S(2)}) async-start(f32[8,128,128]{2,1,0:T(8,128)} %copy.24), calls=%async_computation.7 | async-start | bytes 1048576 | tf_op jit(solution)/shard_map/all_to_all | solution.py:108
  147.1 2.4 fusion.12
  149.4 11.7 %all-to-all-done.7 = f32[8,128,128]{2,1,0:T(8,128)S(1)} async-done(((f32[8,128,128]{2,1,0:T(8,128)}), f32[8,128,128]{2,1,0:T(8,128)S(1)}, u32[]{:S(2)}, u32[]{:S(2)}) %all-to-all-start.7) | async-done | bytes 524320 | tf_op jit(solution)/shard_map/all_to_all | solution.py:108
  161.2 3.0 reduce-precision_convert_fusion.15
  164.8 18.4 %all_to_all.77 = f32[8,136,128]{2,1,0:T(8,128)S(1)} all-to-all(f32[8,136,128]{2,1,0:T(8,128)S(1)} %concatenate.87), channel_id=1, replica_groups=mesh['clique'=8,'shard'=4] {'clique'}, dimensions={0} | all-to-all | bytes 1114112 | tf_op jit(solution)/shard_map/all_to_all | solution.py:105
  184.6 3.8 %all-to-all-start.9 = ((f32[8,136,128]{2,1,0:T(8,128)}), f32[8,136,128]{2,1,0:T(8,128)S(1)}, u32[]{:S(2)}, u32[]{:S(2)}) async-start(f32[8,136,128]{2,1,0:T(8,128)} %copy.26), calls=%async_computation.9 | async-start | bytes 1114112 | tf_op jit(solution)/shard_map/all_to_all | solution.py:108
  188.4 2.3 fusion.7
  191.5 12.5 %all-to-all-done.9 = f32[8,136,128]{2,1,0:T(8,128)S(1)} async-done(((f32[8,136,128]{2,1,0:T(8,128)}), f32[8,136,128]{2,1,0:T(8,128)S(1)}, u32[]{:S(2)}, u32[]{:S(2)}) %all-to-all-start.9) | async-done | bytes 557088 | tf_op jit(solution)/shard_map/all_to_all | solution.py:108
  204.1 1.3 reduce-precision_convert_fusion.11
  205.4 1.3 fusion.11
  208.1 17.0 %all_to_all.78 = f32[4,520,128]{2,1,0:T(8,128)S(1)} all-to-all(f32[4,520,128]{2,1,0:T(8,128)S(1)} %maximum_maximum_fusion.1), channel_id=1, replica_groups=mesh['clique'=8,'shard'=4] {'shard'}, dimensions={0} | all-to-all | bytes 2129920 | tf_op jit(solution)/shard_map/all_to_all | solution.py:86
  227.5 1.4 fusion.172
  229.4 1.3 fusion.134
  232.1 10.5 %all_to_all.79 = f32[4,264,128]{2,1,0:T(8,128)S(1)} all-to-all(f32[4,264,128]{2,1,0:T(8,128)S(1)} %concatenate.92), channel_id=1, replica_groups=mesh['clique'=8,'shard'=4] {'shard'}, dimensions={0} | all-to-all | bytes 1081344 | tf_op jit(solution)/shard_map/all_to_all | solution.py:68
  244.8 2.2 fusion.14
  247.1 18.4 %all_to_all.80 = f32[8,128,128]{2,1,0:T(8,128)S(1)} all-to-all(f32[8,128,128]{2,1,0:T(8,128)S(1)} %bitcast.174), channel_id=1, replica_groups=mesh['clique'=8,'shard'=4] {'clique'}, dimensions={0} | all-to-all | bytes 1048576 | tf_op jit(solution)/shard_map/all_to_all | solution.py:105
  267.0 3.5 %all-to-all-start.13 = ((f32[8,128,128]{2,1,0:T(8,128)}), f32[8,128,128]{2,1,0:T(8,128)S(1)}, u32[]{:S(2)}, u32[]{:S(2)}) async-start(f32[8,128,128]{2,1,0:T(8,128)} %copy.28), calls=%async_computation.13 | async-start | bytes 1048576 | tf_op jit(solution)/shard_map/all_to_all | solution.py:108
  270.5 3.8 %fusion.4 = f32[1024,384]{1,0:T(8,128)} fusion(s32[1024]{0:T(1024)S(1)} %bitcast.189, bf16[1024,128]{1,0:T(8,128)(2,1)} %copy-done.4, bf16[1024,128]{1,0:T(8,128)(2,1)} %copy-done.5, bf16[1024,128]{1,0:T(8,128)(2,1)S(1)} %get-tuple-element.45), kind=kOutput, calls=%fused_computation.13 | convolution fusion | flops 808714240 | bytes 2363392 | tf_op jit(solution)/shard_map/dot_general | solution.py:18
  274.5 2.8 fusion.5
  277.3 8.5 %all-to-all-done.13 = f32[8,128,128]{2,1,0:T(8,128)S(1)} async-done(((f32[8,128,128]{2,1,0:T(8,128)}), f32[8,128,128]{2,1,0:T(8,128)S(1)}, u32[]{:S(2)}, u32[]{:S(2)}) %all-to-all-start.13) | async-done | bytes 524320 | tf_op jit(solution)/shard_map/all_to_all | solution.py:108
  286.0 1.3 fusion.13
  288.2 3.5 %all-to-all-start.14 = ((f32[4,256,128]{2,1,0:T(8,128)}), f32[4,256,128]{2,1,0:T(8,128)S(1)}, u32[]{:S(2)}, u32[]{:S(2)}) async-start(f32[4,256,128]{2,1,0:T(8,128)} %bitcast.46), calls=%async_computation.14 | async-start | bytes 1048576 | tf_op jit(solution)/shard_map/all_to_all | solution.py:86
  291.7 1.6 fusion.122
  293.6 6.0 %all-to-all-done.14 = f32[4,256,128]{2,1,0:T(8,128)S(1)} async-done(((f32[4,256,128]{2,1,0:T(8,128)}), f32[4,256,128]{2,1,0:T(8,128)S(1)}, u32[]{:S(2)}, u32[]{:S(2)}) %all-to-all-start.14) | async-done | bytes 524320 | tf_op jit(solution)/shard_map/all_to_all | solution.py:86
  299.8 1.6 fusion
  (86 shorter events, 32.3 us)
Async XLA Ops:
  6.5 6.5 %sort.23.cloned.1.call-start = ((), (), s32[]{:S(2)}) async-start(), calls=%async_computation.15 | async-start | bytes 147488 | tf_op jit(solution)/shard_map/sort | solution.py:55
  15.9 9.9 %all-to-all-start = ((s32[4,4,256]{2,0,1:T(4,128)}), s32[4,4,256]{2,0,1:T(4,128)S(1)}, u32[]{:S(2)}, u32[]{:S(2)}) async-start(s32[4,4,256]{2,0,1:T(4,128)} %bitcast.6), calls=%async_computation | async-start | bytes 32768 | tf_op jit(solution)/shard_map/all_to_all | solution.py:56
  25.9 16.2 %all-to-all-start.1 = ((f32[4,520,128]{2,1,0:T(8,128)}), f32[4,520,128]{2,1,0:T(8,128)S(1)}, u32[]{:S(2)}, u32[]{:S(2)}) async-start(f32[4,520,128]{2,1,0:T(8,128)} %maximum_maximum_fusion), calls=%async_computation.1 | async-start | bytes 2129920 | tf_op jit(solution)/shard_map/all_to_all | solution.py:68
  47.3 5.9 %copy-start.9 = (s32[2,8]{1,0:T(2,128)S(1)}, s32[2,8]{1,0:T(2,128)}, u32[]{:S(2)}) copy-start(s32[2,8]{1,0:T(2,128)} %param.7) | copy-start | bytes 196
  48.3 20.2 %all-to-all-start.2 = ((f32[8,128,128]{2,1,0:T(8,128)}), f32[8,128,128]{2,1,0:T(8,128)S(1)}, u32[]{:S(2)}, u32[]{:S(2)}) async-start(f32[8,128,128]{2,1,0:T(8,128)} %bitcast.23), calls=%async_computation.2 | async-start | bytes 1048576 | tf_op jit(solution)/shard_map/all_to_all | solution.py:105
  68.5 5.2 %copy-start.6 = (bf16[1024,128]{1,0:T(8,128)(2,1)S(1)}, bf16[1024,128]{1,0:T(8,128)(2,1)}, u32[]{:S(2)}) copy-start(bf16[1024,128]{1,0:T(8,128)(2,1)} %get-tuple-element.23) | copy-start | bytes 786436
  68.5 5.2 %copy-start.7 = (bf16[1024,128]{1,0:T(8,128)(2,1)S(1)}, bf16[1024,128]{1,0:T(8,128)(2,1)}, u32[]{:S(2)}) copy-start(bf16[1024,128]{1,0:T(8,128)(2,1)} %get-tuple-element.25) | copy-start | bytes 786436
  68.5 5.2 %copy-start.8 = (bf16[1024,128]{1,0:T(8,128)(2,1)S(1)}, bf16[1024,128]{1,0:T(8,128)(2,1)}, u32[]{:S(2)}) copy-start(bf16[1024,128]{1,0:T(8,128)(2,1)} %get-tuple-element.28) | copy-start | bytes 786436
  70.2 18.8 %all-to-all-start.3 = ((f32[8,128,128]{2,1,0:T(8,128)}), f32[8,128,128]{2,1,0:T(8,128)S(1)}, u32[]{:S(2)}, u32[]{:S(2)}) async-start(f32[8,128,128]{2,1,0:T(8,128)} %copy.19), calls=%async_computation.3 | async-start | bytes 1048576 | tf_op jit(solution)/shard_map/all_to_all | solution.py:108
  91.6 11.4 %all-to-all-start.4 = ((f32[4,256,128]{1,2,0:T(8,128)}), f32[4,256,128]{1,2,0:T(8,128)S(1)}, u32[]{:S(2)}, u32[]{:S(2)}) async-start(f32[4,256,128]{1,2,0:T(8,128)} %copy.20), calls=%async_computation.4 | async-start | bytes 1048576 | tf_op jit(solution)/shard_map/all_to_all | solution.py:86
  103.1 2.1 copy-start.10
  142.4 18.8 %all-to-all-start.7 = ((f32[8,128,128]{2,1,0:T(8,128)}), f32[8,128,128]{2,1,0:T(8,128)S(1)}, u32[]{:S(2)}, u32[]{:S(2)}) async-start(f32[8,128,128]{2,1,0:T(8,128)} %copy.24), calls=%async_computation.7 | async-start | bytes 1048576 | tf_op jit(solution)/shard_map/all_to_all | solution.py:108
  184.6 19.5 %all-to-all-start.9 = ((f32[8,136,128]{2,1,0:T(8,128)}), f32[8,136,128]{2,1,0:T(8,128)S(1)}, u32[]{:S(2)}, u32[]{:S(2)}) async-start(f32[8,136,128]{2,1,0:T(8,128)} %copy.26), calls=%async_computation.9 | async-start | bytes 1114112 | tf_op jit(solution)/shard_map/all_to_all | solution.py:108
  206.7 1.3 copy-start.2
  225.1 1.0 copy-start
  227.5 1.9 copy-start.11
  229.1 1.6 copy-start.4
  229.1 1.6 copy-start.5
  267.0 18.8 %all-to-all-start.13 = ((f32[8,128,128]{2,1,0:T(8,128)}), f32[8,128,128]{2,1,0:T(8,128)S(1)}, u32[]{:S(2)}, u32[]{:S(2)}) async-start(f32[8,128,128]{2,1,0:T(8,128)} %copy.28), calls=%async_computation.13 | async-start | bytes 1048576 | tf_op jit(solution)/shard_map/all_to_all | solution.py:108
  274.5 11.3 %copy-start.1 = (f32[1024,128]{1,0:T(8,128)S(1)}, f32[1024,128]{1,0:T(8,128)}, u32[]{:S(2)}) copy-start(f32[1024,128]{1,0:T(8,128)} %get-tuple-element.20) | copy-start | bytes 1572868
  288.2 11.4 %all-to-all-start.14 = ((f32[4,256,128]{2,1,0:T(8,128)}), f32[4,256,128]{2,1,0:T(8,128)S(1)}, u32[]{:S(2)}, u32[]{:S(2)}) async-start(f32[4,256,128]{2,1,0:T(8,128)} %bitcast.46), calls=%async_computation.14 | async-start | bytes 1048576 | tf_op jit(solution)/shard_map/all_to_all | solution.py:86
  291.7 1.9 copy-start.3
Sparse Core Ops, SparseCore 0:
  9.8 2.8 sort.25.cloned.1.call-done
  (1 shorter events, 0.0 us)

commit v5 on v4

--- a/solution.py
+++ b/solution.py
@@ -53,20 +53,34 @@
     slot = lists % per_owner
     blocks = jnp.broadcast_to(jnp.arange(block_count, dtype=jnp.int32), lists.shape)
     _, sent_slots, order = lax.sort((owner, slot, blocks), dimension=1, num_keys=1, is_stable=True)
-    arrived = lax.all_to_all(
-        sent_slots.reshape(4, shard_count, per_peer), "shard", 1, 1, tiled=True
-    ).reshape(4, block_count)
     sorting = [one_hot_of(order[which], block_count) for which in range(4)]
     down1_to_up0 = lax.dot_general(
         sorting[1], sorting[3], (((1,), (1,)), ((), ())), preferred_element_type=jnp.float32
     ).astype(jnp.bfloat16)
+    slot_rows = (4 * per_peer) // lane_count
+    slot_chunk = (
+        sent_slots.reshape(4, shard_count, per_peer)
+        .transpose(1, 0, 2)
+        .reshape(shard_count, slot_rows, lane_count)
+        .astype(jnp.float32)
+    )
+    arrived = [None] * 4
+    piece_rows = per_owner // clique_count
 
-    def send(items):
+    def send(items, with_slots=False):
         partial_sum = jnp.sum(items[0][0])
         chunks = [rows.reshape(shard_count, per_peer, lane_count) for rows, _ in items]
         chunks.append(jnp.broadcast_to(partial_sum, (shard_count, PAD, lane_count)))
+        if with_slots:
+            chunks.append(slot_chunk)
         arrived_rows = lax.all_to_all(jnp.concatenate(chunks, axis=1), "shard", 0, 0, tiled=True)
-        total = jnp.sum(arrived_rows[:, len(items) * per_peer, 0])
+        head = len(items) * per_peer
+        total = jnp.sum(arrived_rows[:, head, 0])
+        if with_slots:
+            got = arrived_rows[:, head + PAD :].reshape(shard_count, 4, per_peer)
+            got = got.transpose(1, 0, 2).reshape(4, block_count).astype(jnp.int32)
+            for which in range(4):
+                arrived[which] = got[which]
         messages = []
         for number, (_, which) in enumerate(items):
             rows = arrived_rows[:, number * per_peer : (number + 1) * per_peer]
@@ -92,23 +106,26 @@
             return rows, None
         return rows, jnp.sum(back[:, len(items) * per_peer, 0])
 
-    def route(owned_rows, mixing, partial=None):
-        piece_rows = per_owner // clique_count
-        pieces = owned_rows.reshape(clique_count, piece_rows, lane_count)
+    def to_middle(arrays):
+        pieces = [a.reshape(clique_count, piece_rows, lane_count) for a in arrays]
+        got = lax.all_to_all(jnp.concatenate(pieces, axis=1), "clique", 0, 0, tiled=True)
+        return [got[:, n * piece_rows : (n + 1) * piece_rows] for n in range(len(arrays))]
+
+    def from_middle(arrays, partial=None):
+        chunks = list(arrays)
         if partial is not None:
-            pieces = jnp.concatenate(
-                [pieces, jnp.broadcast_to(partial, (clique_count, PAD, lane_count))], axis=1
-            )
-        combined = jnp.einsum(
-            "oi,ixl->oxl",
-            mixing,
-            lax.all_to_all(pieces, "clique", split_axis=0, concat_axis=0, tiled=True),
-            precision=lax.Precision.HIGHEST,
-        )
-        moved = lax.all_to_all(combined, "clique", split_axis=0, concat_axis=0, tiled=True)
+            chunks.append(jnp.broadcast_to(partial[:, None, None], (clique_count, PAD, lane_count)))
+        got = lax.all_to_all(jnp.concatenate(chunks, axis=1), "clique", 0, 0, tiled=True)
+        outs = [
+            got[:, n * piece_rows : (n + 1) * piece_rows].reshape(per_owner, lane_count)
+            for n in range(len(arrays))
+        ]
         if partial is None:
-            return moved.reshape(per_owner, lane_count)
-        return moved[:, :piece_rows].reshape(per_owner, lane_count), moved[0, piece_rows, 0]
+            return outs, None
+        return outs, jnp.sum(got[:, len(arrays) * piece_rows, 0])
+
+    def mix(mixing, pieces):
+        return jnp.einsum("oi,ixl->oxl", mixing, pieces, precision=lax.Precision.HIGHEST)
 
     clique_ids = jnp.arange(clique_count, dtype=jnp.int32)
     sel = [
@@ -118,26 +135,31 @@
 
     t2_up1 = split_dot(sorting[0], t2)
     t0_down0 = split_dot(sorting[2], t0)
-    (message, down0_message), total = send([(t2_up1, 0), (t0_down0, 2)])
+    (message, down0_message), total = send([(t2_up1, 0), (t0_down0, 2)], with_slots=True)
     scaled1 = message * (sep_states / total)
-    incoming1 = jnp.exp(route(jnp.log(scaled1), sel[1].T))
+    scaled1_mid, down0_mid = to_middle([scaled1, down0_message])
+    (incoming1,), _ = from_middle([jnp.exp(mix(sel[1].T, jnp.log(scaled1_mid)))])
     (picked,), _ = fetch([(incoming1, 3)])
     t1_down1 = split_dot(sorting[3], t1) * picked
     t1_up0 = split_dot(down1_to_up0, t1_down1)
     (message,), total = send([(t1_up0, 1)])
     scaled0 = message * (sep_states / total)
-    incoming0 = jnp.exp(route(jnp.log(scaled0), sel[0].T))
-    incoming0 = jnp.where(jnp.isfinite(incoming0), incoming0, 0.0)
-    fresh0 = down0_message * incoming0
-    from_parent, partial = route(fresh0, sel[0], jnp.sum(fresh0))
-    (picked, update0), total = fetch([(incoming0, 2), (from_parent / scaled0, 1)], partial)
+    (scaled0_mid,) = to_middle([scaled0])
+    incoming0_mid = jnp.exp(mix(sel[0].T, jnp.log(scaled0_mid)))
+    incoming0_mid = jnp.where(jnp.isfinite(incoming0_mid), incoming0_mid, 0.0)
+    fresh0_mid = down0_mid * incoming0_mid
+    partial = jnp.dot(sel[0], jnp.sum(fresh0_mid, axis=(1, 2)), precision=lax.Precision.HIGHEST)
+    update0_mid = mix(sel[0], fresh0_mid) / scaled0_mid
+    (update0, incoming0), range_total = from_middle([update0_mid, incoming0_mid], partial)
+    (picked, update0), total = fetch([(incoming0, 2), (update0, 1)], range_total)
     out0 = split_dot(sorting[2], t0_down0 * picked, transposed=True)
     t1_up0 = t1_up0 * (update0 * (sep_states / total))
     out1 = split_dot(sorting[1], t1_up0, transposed=True)
     t1_down1 = split_dot(down1_to_up0, t1_up0, transposed=True)
     (message,), total = send([(t1_down1, 3)])
     fresh1 = message * (sep_states / total)
-    update1 = route(fresh1, sel[1]) / scaled1
+    (fresh1_mid,) = to_middle([fresh1])
+    (update1,), _ = from_middle([mix(sel[1], fresh1_mid) / scaled1_mid])
     (picked,), _ = fetch([(update1, 0)])
     out2 = split_dot(sorting[0], t2_up1 * picked, transposed=True)
     return jnp.stack([out0, out1, out2])[:, None]

time: 311 us -> 290 us (0.932)
  blocking collectives: 93.5 us -> 125 us
  waiting for transfers between devices: 84.9 us -> 57.8 us
  starting transfers between devices: 34.9 us -> 19.1 us
  other arithmetic: 27.6 us -> 21.6 us
    all_to_all x7 -> x3, waiting for transfers between devices: 75.1 us -> 48 us  [the longest x1 26.5 us: to_middle(): lax.all_to_all(jnp.concatenate(pieces, axis=1), 'clique', 0, 0, tiled=True)]
    all_to_all x2 -> x3, blocking collectives: 21 us -> 41.1 us  [send(): lax.all_to_all(jnp.concatenate(chunks, axis=1), 'shard', 0, 0, tiled=True)]
    all_to_all x7 -> x3, starting transfers between devices: 27.8 us -> 12 us  [the longest x2 6.98 us: from_middle(): lax.all_to_all(jnp.concatenate(chunks, axis=1), 'clique', 0, 0, tiled=True)]
    all_to_all x3, blocking collectives: 55.5 us -> 66.3 us  [the longest x2 36.7 us: to_middle(): lax.all_to_all(jnp.concatenate(pieces, axis=1), 'clique', 0, 0, tiled=True)]
    another operation x14, other arithmetic: 12.6 us -> 6.89 us
    dot_general x4 -> x0, local copies, waits for them, and re-layouts: 3.62 us -> none  [route(): jnp.einsum('oi,ixl->oxl', mixing, lax.all_to_all(pieces, 'clique', split_...]
    dot_general x16, matrix products: 30 us -> 26.8 us  [split_dot(): lax.dot_general(one_hot, parts, (((contract,), (0,)), ((), ())), preferre...]
  transfers between devices with their start and end apart: 9 -> 5, of which waited for: 9 -> 5; matrix products, arithmetic and copies ran while one was open for 8% -> 5% of each run, Pallas kernels for 0% -> 0%
where the time goes in v5:
time: 290 us; the launch traced here: 289 us
  blocking collectives  125 us (43%)
  waiting for transfers between devices  57.8 us (20%)
  matrix products  34.6 us (12%)
  other arithmetic  21.6 us (7%)
  starting transfers between devices  19.1 us (7%)
  between operations  16.6 us (6%)
  local copies, waits for them, and re-layouts  14.6 us (5%)
    all_to_all x3, blocking collectives, send(): lax.all_to_all(jnp.concatenate(chunks, axis=1), 'shard', 0, 0, tiled=True)  41.1 us
    all_to_all x2, blocking collectives, to_middle(): lax.all_to_all(jnp.concatenate(pieces, axis=1), 'clique', 0, 0, tiled=True)  36.7 us
    all_to_all x1, blocking collectives, from_middle(): lax.all_to_all(jnp.concatenate(chunks, axis=1), 'clique', 0, 0, tiled=True)  29.7 us
    dot_general x16, matrix products, split_dot(): lax.dot_general(one_hot, parts, (((contract,), (0,)), ((), ())), preferre...  26.8 us
    all_to_all x1, waiting for transfers between devices, to_middle(): lax.all_to_all(jnp.concatenate(pieces, axis=1), 'clique', 0, 0, tiled=True)  26.5 us
    all_to_all x2, waiting for transfers between devices, from_middle(): lax.all_to_all(jnp.concatenate(chunks, axis=1), 'clique', 0, 0, tiled=True)  21.4 us
    all_to_all x1, blocking collectives, fetch(): lax.all_to_all(jnp.concatenate(chunks, axis=1), 'shard', 0, 0, tiled=True)  17.4 us
    all_to_all x2, waiting for transfers between devices, fetch(): lax.all_to_all(jnp.concatenate(chunks, axis=1), 'shard', 0, 0, tiled=True)  9.85 us
  transfers between devices with their start and end apart: 5, of which 5 were waited for; matrix products, arithmetic and copies ran while one was open for 5% of the time, Pallas kernels for 0%

profile of v5, /device:TPU:0, one launch (start us, length us, event | category | flops | bytes accessed | tf_op | source)
XLA Modules:
  0.0 289.3 jit_solution(2455293372234123228)
XLA Ops:
  8.6 2.6 reduce-precision_convert_fusion.21
  11.2 1.8 sort.23.cloned.1.call-done
  14.6 1.3 fusion.6
  16.0 1.3 fusion.4
  18.9 19.8 %all_to_all.60 = f32[4,528,128]{2,1,0:T(8,128)S(1)} all-to-all(f32[4,528,128]{2,1,0:T(8,128)S(1)} %pad_maximum_fusion), channel_id=1, replica_groups=mesh['clique'=8,'shard'=4] {'shard'}, dimensions={0} | all-to-all | bytes 2162688 | tf_op jit(solution)/shard_map/all_to_all | solution.py:76
  38.8 1.0 reduce-precision_convert_fusion.25
  39.8 1.3 fusion.9
  43.3 2.3 fusion.8
  45.7 0.9 copy-done.4
  46.7 1.0 pad_maximum_fusion.2
  47.7 5.0 %all-to-all-start.1 = ((f32[8,256,128]{2,1,0:T(8,128)}), f32[8,256,128]{2,1,0:T(8,128)S(1)}, u32[]{:S(2)}, u32[]{:S(2)}) async-start(f32[8,256,128]{2,1,0:T(8,128)} %pad_maximum_fusion.2), calls=%async_computation.1 | async-start | bytes 2097152 | tf_op jit(solution)/shard_map/all_to_all | solution.py:111
  52.7 26.5 %all-to-all-done.1 = f32[8,256,128]{2,1,0:T(8,128)S(1)} async-done(((f32[8,256,128]{2,1,0:T(8,128)}), f32[8,256,128]{2,1,0:T(8,128)S(1)}, u32[]{:S(2)}, u32[]{:S(2)}) %all-to-all-start.1) | async-done | bytes 1048608 | tf_op jit(solution)/shard_map/all_to_all | solution.py:111
  82.6 3.5 %all-to-all-start.2 = ((f32[8,128,128]{2,1,0:T(8,128)}), f32[8,128,128]{2,1,0:T(8,128)S(1)}, u32[]{:S(2)}, u32[]{:S(2)}) async-start(f32[8,128,128]{2,1,0:T(8,128)} %copy.27), calls=%async_computation.2 | async-start | bytes 1048576 | tf_op jit(solution)/shard_map/all_to_all | solution.py:118
  86.1 2.4 fusion
  88.5 12.9 %all-to-all-done.2 = f32[8,128,128]{2,1,0:T(8,128)S(1)} async-done(((f32[8,128,128]{2,1,0:T(8,128)}), f32[8,128,128]{2,1,0:T(8,128)S(1)}, u32[]{:S(2)}, u32[]{:S(2)}) %all-to-all-start.2) | async-done | bytes 524320 | tf_op jit(solution)/shard_map/all_to_all | solution.py:118
  101.5 1.3 fusion.11
  102.9 1.0 copy.28
  103.8 3.6 %all-to-all-start.3 = ((f32[4,256,128]{1,2,0:T(8,128)}), f32[4,256,128]{1,2,0:T(8,128)S(1)}, u32[]{:S(2)}, u32[]{:S(2)}) async-start(f32[4,256,128]{1,2,0:T(8,128)} %copy.28), calls=%async_computation.3 | async-start | bytes 1048576 | tf_op jit(solution)/shard_map/all_to_all | solution.py:100
  107.5 3.9 %fusion.31 = bf16[1024,1024]{1,0:T(8,128)(2,1)} fusion(s32[1024]{0:T(1024)S(1)} %bitcast.202, s32[1024]{0:T(1024)S(1)} %bitcast.191), kind=kOutput, calls=%fused_computation.43 | convolution fusion | flops 2150629376 | bytes 2105344 | tf_op jit(solution)/shard_map/dot_general | solution.py:57
  111.4 3.9 %all-to-all-done.3 = f32[4,256,128]{1,2,0:T(8,128)S(1)} async-done(((f32[4,256,128]{1,2,0:T(8,128)}), f32[4,256,128]{1,2,0:T(8,128)S(1)}, u32[]{:S(2)}, u32[]{:S(2)}) %all-to-all-start.3) | async-done | bytes 524320 | tf_op jit(solution)/shard_map/all_to_all | solution.py:100
  115.4 1.7 reduce-precision_convert_fusion.17
  117.4 1.3 fusion.62
  120.1 10.6 %all_to_all.61 = f32[4,264,128]{2,1,0:T(8,128)S(1)} all-to-all(f32[4,264,128]{2,1,0:T(8,128)S(1)} %concatenate.88), channel_id=1, replica_groups=mesh['clique'=8,'shard'=4] {'shard'}, dimensions={0} | all-to-all | bytes 1081344 | tf_op jit(solution)/shard_map/all_to_all | solution.py:76
  132.2 1.3 fusion.10
  133.5 18.8 %all_to_all.62 = f32[8,128,128]{2,1,0:T(8,128)S(1)} all-to-all(f32[8,128,128]{2,1,0:T(8,128)S(1)} %bitcast.174), channel_id=1, replica_groups=mesh['clique'=8,'shard'=4] {'clique'}, dimensions={0} | all-to-all | bytes 1048576 | tf_op jit(solution)/shard_map/all_to_all | solution.py:111
  152.4 1.1 fusion.131
  153.7 0.9 convolution_divide_fusion.1
  155.0 29.7 %all_to_all.63 = f32[8,264,128]{2,1,0:T(8,128)S(1)} all-to-all(f32[8,264,128]{2,1,0:T(8,128)S(1)} %copy.33), channel_id=1, replica_groups=mesh['clique'=8,'shard'=4] {'clique'}, dimensions={0} | all-to-all | bytes 2162688 | tf_op jit(solution)/shard_map/all_to_all | solution.py:118
  186.2 1.3 fusion.7
  187.7 1.3 fusion.12
  189.2 17.4 %all_to_all.64 = f32[4,520,128]{2,1,0:T(8,128)S(1)} all-to-all(f32[4,520,128]{2,1,0:T(8,128)S(1)} %maximum_maximum_fusion), channel_id=1, replica_groups=mesh['clique'=8,'shard'=4] {'shard'}, dimensions={0} | all-to-all | bytes 2129920 | tf_op jit(solution)/shard_map/all_to_all | solution.py:100
  206.6 1.0 copy-done
  208.9 1.4 fusion.167
  210.8 1.3 fusion.130
  213.5 10.7 %all_to_all.65 = f32[4,264,128]{2,1,0:T(8,128)S(1)} all-to-all(f32[4,264,128]{2,1,0:T(8,128)S(1)} %concatenate.96), channel_id=1, replica_groups=mesh['clique'=8,'shard'=4] {'shard'}, dimensions={0} | all-to-all | bytes 1081344 | tf_op jit(solution)/shard_map/all_to_all | solution.py:76
  225.7 1.3 fusion.14
  227.1 17.9 %all_to_all.66 = f32[8,128,128]{2,1,0:T(8,128)S(1)} all-to-all(f32[8,128,128]{2,1,0:T(8,128)S(1)} %bitcast.175), channel_id=1, replica_groups=mesh['clique'=8,'shard'=4] {'clique'}, dimensions={0} | all-to-all | bytes 1048576 | tf_op jit(solution)/shard_map/all_to_all | solution.py:111
  245.0 0.9 convolution_divide_fusion
  246.8 3.5 %all-to-all-start.10 = ((f32[8,128,128]{2,1,0:T(8,128)}), f32[8,128,128]{2,1,0:T(8,128)S(1)}, u32[]{:S(2)}, u32[]{:S(2)}) async-start(f32[8,128,128]{2,1,0:T(8,128)} %copy.35), calls=%async_computation.10 | async-start | bytes 1048576 | tf_op jit(solution)/shard_map/all_to_all | solution.py:118
  250.3 3.8 %fusion.2 = f32[1024,384]{1,0:T(8,128)} fusion(s32[1024]{0:T(1024)S(1)} %bitcast.192, bf16[1024,128]{1,0:T(8,128)(2,1)} %copy-done.6, bf16[1024,128]{1,0:T(8,128)(2,1)} %copy-done.7, bf16[1024,128]{1,0:T(8,128)(2,1)S(1)} %get-tuple-element.38), kind=kOutput, calls=%fused_computation.8 | convolution fusion | flops 808714240 | bytes 2363392 | tf_op jit(solution)/shard_map/dot_general | solution.py:18
  254.2 2.7 fusion.5
  257.0 8.6 %all-to-all-done.10 = f32[8,128,128]{2,1,0:T(8,128)S(1)} async-done(((f32[8,128,128]{2,1,0:T(8,128)}), f32[8,128,128]{2,1,0:T(8,128)S(1)}, u32[]{:S(2)}, u32[]{:S(2)}) %all-to-all-start.10) | async-done | bytes 524320 | tf_op jit(solution)/shard_map/all_to_all | solution.py:118
  265.7 1.3 fusion.13
  267.9 3.5 %all-to-all-start.11 = ((f32[4,256,128]{2,1,0:T(8,128)}), f32[4,256,128]{2,1,0:T(8,128)S(1)}, u32[]{:S(2)}, u32[]{:S(2)}) async-start(f32[4,256,128]{2,1,0:T(8,128)} %bitcast.49), calls=%async_computation.11 | async-start | bytes 1048576 | tf_op jit(solution)/shard_map/all_to_all | solution.py:100
  271.4 1.6 fusion.120
  273.4 6.0 %all-to-all-done.11 = f32[4,256,128]{2,1,0:T(8,128)S(1)} async-done(((f32[4,256,128]{2,1,0:T(8,128)}), f32[4,256,128]{2,1,0:T(8,128)S(1)}, u32[]{:S(2)}, u32[]{:S(2)}) %all-to-all-start.11) | async-done | bytes 524320 | tf_op jit(solution)/shard_map/all_to_all | solution.py:100
  279.5 1.6 fusion.3
  281.2 1.2 maximum_bitcast_fusion
  (89 shorter events, 21.9 us)
Async XLA Ops:
  6.5 6.5 %sort.23.cloned.1.call-start = ((), (), s32[]{:S(2)}) async-start(), calls=%async_computation.12 | async-start | bytes 147488 | tf_op jit(solution)/shard_map/sort | solution.py:55
  45.6 1.0 copy-start.4
  47.7 5.0 %copy-start.11 = (s32[2,8]{1,0:T(2,128)S(1)}, s32[2,8]{1,0:T(2,128)}, u32[]{:S(2)}) copy-start(s32[2,8]{1,0:T(2,128)} %param.7) | copy-start | bytes 196
  47.7 31.6 %all-to-all-start.1 = ((f32[8,256,128]{2,1,0:T(8,128)}), f32[8,256,128]{2,1,0:T(8,128)S(1)}, u32[]{:S(2)}, u32[]{:S(2)}) async-start(f32[8,256,128]{2,1,0:T(8,128)} %pad_maximum_fusion.2), calls=%async_computation.1 | async-start | bytes 2097152 | tf_op jit(solution)/shard_map/all_to_all | solution.py:111
  80.1 0.8 copy-start.1
  80.9 5.2 %copy-start.8 = (bf16[1024,128]{1,0:T(8,128)(2,1)S(1)}, bf16[1024,128]{1,0:T(8,128)(2,1)}, u32[]{:S(2)}) copy-start(bf16[1024,128]{1,0:T(8,128)(2,1)} %get-tuple-element.17) | copy-start | bytes 786436
  80.9 5.2 %copy-start.9 = (bf16[1024,128]{1,0:T(8,128)(2,1)S(1)}, bf16[1024,128]{1,0:T(8,128)(2,1)}, u32[]{:S(2)}) copy-start(bf16[1024,128]{1,0:T(8,128)(2,1)} %get-tuple-element.18) | copy-start | bytes 786436
  80.9 5.2 %copy-start.10 = (bf16[1024,128]{1,0:T(8,128)(2,1)S(1)}, bf16[1024,128]{1,0:T(8,128)(2,1)}, u32[]{:S(2)}) copy-start(bf16[1024,128]{1,0:T(8,128)(2,1)} %get-tuple-element.23) | copy-start | bytes 786436
  82.6 18.8 %all-to-all-start.2 = ((f32[8,128,128]{2,1,0:T(8,128)}), f32[8,128,128]{2,1,0:T(8,128)S(1)}, u32[]{:S(2)}, u32[]{:S(2)}) async-start(f32[8,128,128]{2,1,0:T(8,128)} %copy.27), calls=%async_computation.2 | async-start | bytes 1048576 | tf_op jit(solution)/shard_map/all_to_all | solution.py:118
  103.8 11.5 %all-to-all-start.3 = ((f32[4,256,128]{1,2,0:T(8,128)}), f32[4,256,128]{1,2,0:T(8,128)S(1)}, u32[]{:S(2)}, u32[]{:S(2)}) async-start(f32[4,256,128]{1,2,0:T(8,128)} %copy.28), calls=%async_computation.3 | async-start | bytes 1048576 | tf_op jit(solution)/shard_map/all_to_all | solution.py:100
  115.4 2.1 copy-start.12
  133.4 18.9 %copy-start.3 = (f32[8,128,128]{2,1,0:T(8,128)S(1)}, f32[8,128,128]{2,1,0:T(8,128)}, u32[]{:S(2)}) copy-start(f32[8,128,128]{2,1,0:T(8,128)} %get-tuple-element.41) | copy-start | bytes 1572868
  206.6 1.0 copy-start
  208.9 1.9 copy-start.13
  210.5 1.6 copy-start.6
  210.5 1.6 copy-start.7
  227.0 18.0 %copy-start.2 = (f32[8,128,128]{2,1,0:T(8,128)S(1)}, f32[8,128,128]{2,1,0:T(8,128)}, u32[]{:S(2)}) copy-start(f32[8,128,128]{2,1,0:T(8,128)} %copy-done.1) | copy-start | bytes 1572868
  246.8 18.8 %all-to-all-start.10 = ((f32[8,128,128]{2,1,0:T(8,128)}), f32[8,128,128]{2,1,0:T(8,128)S(1)}, u32[]{:S(2)}, u32[]{:S(2)}) async-start(f32[8,128,128]{2,1,0:T(8,128)} %copy.35), calls=%async_computation.10 | async-start | bytes 1048576 | tf_op jit(solution)/shard_map/all_to_all | solution.py:118
  267.9 11.4 %all-to-all-start.11 = ((f32[4,256,128]{2,1,0:T(8,128)}), f32[4,256,128]{2,1,0:T(8,128)S(1)}, u32[]{:S(2)}, u32[]{:S(2)}) async-start(f32[4,256,128]{2,1,0:T(8,128)} %bitcast.49), calls=%async_computation.11 | async-start | bytes 1048576 | tf_op jit(solution)/shard_map/all_to_all | solution.py:100
  271.4 1.9 copy-start.5
Sparse Core Ops, SparseCore 0:
  9.8 2.8 sort.25.cloned.1.call-done
  (1 shorter events, 0.0 us)

commit v6 on v5

--- a/solution.py
+++ b/solution.py
@@ -10,15 +10,13 @@
 def split_dot(one_hot, x, transposed=False):
     lanes = x.shape[-1]
     hi = lax.reduce_precision(x, exponent_bits=8, mantissa_bits=7)
-    rest = x - hi
-    mid = lax.reduce_precision(rest, exponent_bits=8, mantissa_bits=7)
-    lo = rest - mid
-    parts = jnp.concatenate([hi, mid, lo], axis=1).astype(jnp.bfloat16)
+    lo = x - hi
+    parts = jnp.concatenate([hi, lo], axis=1).astype(jnp.bfloat16)
     contract = 0 if transposed else 1
     y = lax.dot_general(
         one_hot, parts, (((contract,), (0,)), ((), ())), preferred_element_type=jnp.float32
     )
-    return (y[:, :lanes] + y[:, lanes : 2 * lanes]) + y[:, 2 * lanes :]
+    return y[:, :lanes] + y[:, lanes:]
 
 
 def one_hot_of(index, count):

time: 290 us -> 280 us (0.966)
  matrix products: 34.6 us -> 26.8 us
  other arithmetic: 21.6 us -> 18.7 us
    dot_general x16, matrix products: 26.8 us -> 19 us  [split_dot(): lax.dot_general(one_hot, parts, (((contract,), (0,)), ((), ())), preferre...]
    another operation x14 -> x13, other arithmetic: 6.89 us -> 5.7 us
  transfers between devices with their start and end apart: 5 -> 5, of which waited for: 5 -> 5; matrix products, arithmetic and copies ran while one was open for 5% -> 4% of each run, Pallas kernels for 0% -> 0%
where the time goes in v6:
time: 280 us; the launch traced here: 279 us
  blocking collectives  125 us (45%)
  waiting for transfers between devices  60.4 us (22%)
  matrix products  26.8 us (10%)
  starting transfers between devices  19 us (7%)
  other arithmetic  18.7 us (7%)
  between operations  16.7 us (6%)
  local copies, waits for them, and re-layouts  12.4 us (4%)
    all_to_all x3, blocking collectives, send(): lax.all_to_all(jnp.concatenate(chunks, axis=1), 'shard', 0, 0, tiled=True)  41 us
    all_to_all x2, blocking collectives, to_middle(): lax.all_to_all(jnp.concatenate(pieces, axis=1), 'clique', 0, 0, tiled=True)  36.5 us
    all_to_all x1, blocking collectives, from_middle(): lax.all_to_all(jnp.concatenate(chunks, axis=1), 'clique', 0, 0, tiled=True)  29.7 us
    all_to_all x1, waiting for transfers between devices, to_middle(): lax.all_to_all(jnp.concatenate(pieces, axis=1), 'clique', 0, 0, tiled=True)  26.5 us
    all_to_all x2, waiting for transfers between devices, from_middle(): lax.all_to_all(jnp.concatenate(chunks, axis=1), 'clique', 0, 0, tiled=True)  23.2 us
    dot_general x16, matrix products, split_dot(): lax.dot_general(one_hot, parts, (((contract,), (0,)), ((), ())), preferre...  19 us
    all_to_all x1, blocking collectives, fetch(): lax.all_to_all(jnp.concatenate(chunks, axis=1), 'shard', 0, 0, tiled=True)  17.4 us
    all_to_all x2, waiting for transfers between devices, fetch(): lax.all_to_all(jnp.concatenate(chunks, axis=1), 'shard', 0, 0, tiled=True)  10.7 us
  transfers between devices with their start and end apart: 5, of which 5 were waited for; matrix products, arithmetic and copies ran while one was open for 4% of the time, Pallas kernels for 0%

profile of v6, /device:TPU:0, one launch (start us, length us, event | category | flops | bytes accessed | tf_op | source)
XLA Modules:
  0.0 278.6 jit_solution(660698017445796492)
XLA Ops:
  8.6 2.3 reduce-precision_convert_fusion.10
  10.9 2.1 sort.23.cloned.1.call-done
  13.0 0.9 fusion.141
  14.6 0.8 fusion.6
  15.5 0.8 fusion.4
  17.9 19.8 %all_to_all.60 = f32[4,528,128]{2,1,0:T(8,128)S(1)} all-to-all(f32[4,528,128]{2,1,0:T(8,128)S(1)} %pad_maximum_fusion), channel_id=1, replica_groups=mesh['clique'=8,'shard'=4] {'shard'}, dimensions={0} | all-to-all | bytes 2162688 | tf_op jit(solution)/shard_map/all_to_all | solution.py:74
  37.8 0.9 reduce-precision_convert_fusion.12
  38.8 0.8 fusion.9
  41.0 1.8 fusion.8
  42.9 1.0 pad_maximum_fusion.2
  44.0 4.9 %all-to-all-start.1 = ((f32[8,256,128]{2,1,0:T(8,128)}), f32[8,256,128]{2,1,0:T(8,128)S(1)}, u32[]{:S(2)}, u32[]{:S(2)}) async-start(f32[8,256,128]{2,1,0:T(8,128)} %pad_maximum_fusion.2), calls=%async_computation.1 | async-start | bytes 2097152 | tf_op jit(solution)/shard_map/all_to_all | solution.py:109
  48.9 26.5 %all-to-all-done.1 = f32[8,256,128]{2,1,0:T(8,128)S(1)} async-done(((f32[8,256,128]{2,1,0:T(8,128)}), f32[8,256,128]{2,1,0:T(8,128)S(1)}, u32[]{:S(2)}, u32[]{:S(2)}) %all-to-all-start.1) | async-done | bytes 1048608 | tf_op jit(solution)/shard_map/all_to_all | solution.py:109
  77.1 0.9 copy.27
  78.0 3.5 %all-to-all-start.2 = ((f32[8,128,128]{2,1,0:T(8,128)}), f32[8,128,128]{2,1,0:T(8,128)S(1)}, u32[]{:S(2)}, u32[]{:S(2)}) async-start(f32[8,128,128]{2,1,0:T(8,128)} %copy.27), calls=%async_computation.2 | async-start | bytes 1048576 | tf_op jit(solution)/shard_map/all_to_all | solution.py:116
  81.5 2.1 fusion
  83.6 13.1 %all-to-all-done.2 = f32[8,128,128]{2,1,0:T(8,128)S(1)} async-done(((f32[8,128,128]{2,1,0:T(8,128)}), f32[8,128,128]{2,1,0:T(8,128)S(1)}, u32[]{:S(2)}, u32[]{:S(2)}) %all-to-all-start.2) | async-done | bytes 524320 | tf_op jit(solution)/shard_map/all_to_all | solution.py:116
  96.8 0.8 fusion.11
  97.7 1.0 copy.28
  98.7 3.5 %all-to-all-start.3 = ((f32[4,256,128]{1,2,0:T(8,128)}), f32[4,256,128]{1,2,0:T(8,128)S(1)}, u32[]{:S(2)}, u32[]{:S(2)}) async-start(f32[4,256,128]{1,2,0:T(8,128)} %copy.28), calls=%async_computation.3 | async-start | bytes 1048576 | tf_op jit(solution)/shard_map/all_to_all | solution.py:98
  102.2 3.9 %fusion.31 = bf16[1024,1024]{1,0:T(8,128)(2,1)} fusion(s32[1024]{0:T(1024)S(1)} %bitcast.160, s32[1024]{0:T(1024)S(1)} %bitcast.149), kind=kOutput, calls=%fused_computation.43 | convolution fusion | flops 2150629376 | bytes 2105344 | tf_op jit(solution)/shard_map/dot_general | solution.py:55
  106.2 4.0 %all-to-all-done.3 = f32[4,256,128]{1,2,0:T(8,128)S(1)} async-done(((f32[4,256,128]{1,2,0:T(8,128)}), f32[4,256,128]{1,2,0:T(8,128)S(1)}, u32[]{:S(2)}, u32[]{:S(2)}) %all-to-all-start.3) | async-done | bytes 524320 | tf_op jit(solution)/shard_map/all_to_all | solution.py:98
  110.2 1.5 reduce-precision_convert_fusion.8
  114.3 10.6 %all_to_all.61 = f32[4,264,128]{2,1,0:T(8,128)S(1)} all-to-all(f32[4,264,128]{2,1,0:T(8,128)S(1)} %concatenate.88), channel_id=1, replica_groups=mesh['clique'=8,'shard'=4] {'shard'}, dimensions={0} | all-to-all | bytes 1081344 | tf_op jit(solution)/shard_map/all_to_all | solution.py:74
  126.2 0.8 fusion.10
  127.1 18.6 %all_to_all.62 = f32[8,128,128]{2,1,0:T(8,128)S(1)} all-to-all(f32[8,128,128]{2,1,0:T(8,128)S(1)} %bitcast.139), channel_id=1, replica_groups=mesh['clique'=8,'shard'=4] {'clique'}, dimensions={0} | all-to-all | bytes 1048576 | tf_op jit(solution)/shard_map/all_to_all | solution.py:109
  145.8 1.1 fusion.103
  147.1 0.9 convolution_divide_fusion.1
  148.4 29.7 %all_to_all.63 = f32[8,264,128]{2,1,0:T(8,128)S(1)} all-to-all(f32[8,264,128]{2,1,0:T(8,128)S(1)} %copy.33), channel_id=1, replica_groups=mesh['clique'=8,'shard'=4] {'clique'}, dimensions={0} | all-to-all | bytes 2162688 | tf_op jit(solution)/shard_map/all_to_all | solution.py:116
  179.5 0.8 fusion.7
  180.5 0.8 fusion.12
  181.5 17.4 %all_to_all.64 = f32[4,520,128]{2,1,0:T(8,128)S(1)} all-to-all(f32[4,520,128]{2,1,0:T(8,128)S(1)} %maximum_maximum_fusion), channel_id=1, replica_groups=mesh['clique'=8,'shard'=4] {'shard'}, dimensions={0} | all-to-all | bytes 2129920 | tf_op jit(solution)/shard_map/all_to_all | solution.py:98
  200.2 0.9 fusion.138
  202.8 0.8 fusion.133
  204.2 10.7 %all_to_all.65 = f32[4,264,128]{2,1,0:T(8,128)S(1)} all-to-all(f32[4,264,128]{2,1,0:T(8,128)S(1)} %concatenate.96), channel_id=1, replica_groups=mesh['clique'=8,'shard'=4] {'shard'}, dimensions={0} | all-to-all | bytes 1081344 | tf_op jit(solution)/shard_map/all_to_all | solution.py:74
  217.3 17.9 %all_to_all.66 = f32[8,128,128]{2,1,0:T(8,128)S(1)} all-to-all(f32[8,128,128]{2,1,0:T(8,128)S(1)} %bitcast.140), channel_id=1, replica_groups=mesh['clique'=8,'shard'=4] {'clique'}, dimensions={0} | all-to-all | bytes 1048576 | tf_op jit(solution)/shard_map/all_to_all | solution.py:109
  235.1 0.9 convolution_divide_fusion
  236.1 0.9 copy.35
  236.9 3.7 %all-to-all-start.10 = ((f32[8,128,128]{2,1,0:T(8,128)}), f32[8,128,128]{2,1,0:T(8,128)S(1)}, u32[]{:S(2)}, u32[]{:S(2)}) async-start(f32[8,128,128]{2,1,0:T(8,128)} %copy.35), calls=%async_computation.10 | async-start | bytes 1048576 | tf_op jit(solution)/shard_map/all_to_all | solution.py:116
  240.7 2.4 fusion.2
  243.3 2.4 fusion.5
  245.6 10.0 %all-to-all-done.10 = f32[8,128,128]{2,1,0:T(8,128)S(1)} async-done(((f32[8,128,128]{2,1,0:T(8,128)}), f32[8,128,128]{2,1,0:T(8,128)S(1)}, u32[]{:S(2)}, u32[]{:S(2)}) %all-to-all-start.10) | async-done | bytes 524320 | tf_op jit(solution)/shard_map/all_to_all | solution.py:116
  255.8 0.8 fusion.13
  256.6 0.8 slice_add_fusion.1
  257.5 3.5 %all-to-all-start.11 = ((f32[4,256,128]{2,1,0:T(8,128)}), f32[4,256,128]{2,1,0:T(8,128)S(1)}, u32[]{:S(2)}, u32[]{:S(2)}) async-start(f32[4,256,128]{2,1,0:T(8,128)} %bitcast.49), calls=%async_computation.11 | async-start | bytes 1048576 | tf_op jit(solution)/shard_map/all_to_all | solution.py:98
  261.0 1.3 fusion.50
  262.3 6.7 %all-to-all-done.11 = f32[4,256,128]{2,1,0:T(8,128)S(1)} async-done(((f32[4,256,128]{2,1,0:T(8,128)}), f32[4,256,128]{2,1,0:T(8,128)S(1)}, u32[]{:S(2)}, u32[]{:S(2)}) %all-to-all-start.11) | async-done | bytes 524320 | tf_op jit(solution)/shard_map/all_to_all | solution.py:98
  269.0 1.4 fusion.3
  270.5 1.2 maximum_bitcast_fusion
  (76 shorter events, 17.7 us)
Async XLA Ops:
  6.5 6.5 %sort.23.cloned.1.call-start = ((), (), s32[]{:S(2)}) async-start(), calls=%async_computation.12 | async-start | bytes 147488 | tf_op jit(solution)/shard_map/sort | solution.py:53
  42.9 5.9 %copy-start.5 = (s32[2,8]{1,0:T(2,128)S(1)}, s32[2,8]{1,0:T(2,128)}, u32[]{:S(2)}) copy-start(s32[2,8]{1,0:T(2,128)} %param.7) | copy-start | bytes 196
  44.0 31.5 %all-to-all-start.1 = ((f32[8,256,128]{2,1,0:T(8,128)}), f32[8,256,128]{2,1,0:T(8,128)S(1)}, u32[]{:S(2)}, u32[]{:S(2)}) async-start(f32[8,256,128]{2,1,0:T(8,128)} %pad_maximum_fusion.2), calls=%async_computation.1 | async-start | bytes 2097152 | tf_op jit(solution)/shard_map/all_to_all | solution.py:109
  75.5 0.8 copy-start.1
  75.5 5.9 %copy-start.3 = (bf16[1024,128]{1,0:T(8,128)(2,1)S(1)}, bf16[1024,128]{1,0:T(8,128)(2,1)}, u32[]{:S(2)}) copy-start(bf16[1024,128]{1,0:T(8,128)(2,1)} %get-tuple-element.20) | copy-start | bytes 786436
  78.0 18.8 %all-to-all-start.2 = ((f32[8,128,128]{2,1,0:T(8,128)}), f32[8,128,128]{2,1,0:T(8,128)S(1)}, u32[]{:S(2)}, u32[]{:S(2)}) async-start(f32[8,128,128]{2,1,0:T(8,128)} %copy.27), calls=%async_computation.2 | async-start | bytes 1048576 | tf_op jit(solution)/shard_map/all_to_all | solution.py:116
  98.7 11.4 %all-to-all-start.3 = ((f32[4,256,128]{1,2,0:T(8,128)}), f32[4,256,128]{1,2,0:T(8,128)S(1)}, u32[]{:S(2)}, u32[]{:S(2)}) async-start(f32[4,256,128]{1,2,0:T(8,128)} %copy.28), calls=%async_computation.3 | async-start | bytes 1048576 | tf_op jit(solution)/shard_map/all_to_all | solution.py:98
  110.2 1.9 copy-start.6
  200.2 1.8 copy-start.7
  201.2 2.3 copy-start.4
  217.2 17.9 %copy-start.2 = (f32[8,128,128]{2,1,0:T(8,128)S(1)}, f32[8,128,128]{2,1,0:T(8,128)}, u32[]{:S(2)}) copy-start(f32[8,128,128]{2,1,0:T(8,128)} %copy-done.1) | copy-start | bytes 1572868
  236.9 18.8 %all-to-all-start.10 = ((f32[8,128,128]{2,1,0:T(8,128)}), f32[8,128,128]{2,1,0:T(8,128)S(1)}, u32[]{:S(2)}, u32[]{:S(2)}) async-start(f32[8,128,128]{2,1,0:T(8,128)} %copy.35), calls=%async_computation.10 | async-start | bytes 1048576 | tf_op jit(solution)/shard_map/all_to_all | solution.py:116
  240.7 2.4 copy-start
  257.5 11.4 %all-to-all-start.11 = ((f32[4,256,128]{2,1,0:T(8,128)}), f32[4,256,128]{2,1,0:T(8,128)S(1)}, u32[]{:S(2)}, u32[]{:S(2)}) async-start(f32[4,256,128]{2,1,0:T(8,128)} %bitcast.49), calls=%async_computation.11 | async-start | bytes 1048576 | tf_op jit(solution)/shard_map/all_to_all | solution.py:98
Sparse Core Ops, SparseCore 0:
  9.8 2.8 sort.25.cloned.1.call-done
  (1 shorter events, 0.0 us)

commit v7 on v6

--- a/solution.py
+++ b/solution.py
@@ -49,9 +49,25 @@
     lists = jnp.stack([up_map[1, 0], up_map[0, 0], down_map[0, 0], down_map[1, 0]])
     owner = lists // per_owner
     slot = lists % per_owner
-    blocks = jnp.broadcast_to(jnp.arange(block_count, dtype=jnp.int32), lists.shape)
-    _, sent_slots, order = lax.sort((owner, slot, blocks), dimension=1, num_keys=1, is_stable=True)
-    sorting = [one_hot_of(order[which], block_count) for which in range(4)]
+    owned = (owner[:, :, None] == jnp.arange(shard_count, dtype=jnp.int32)).astype(jnp.bfloat16)
+    earlier = (
+        jnp.arange(block_count, dtype=jnp.int32)[:, None]
+        >= jnp.arange(block_count, dtype=jnp.int32)[None, :]
+    ).astype(jnp.bfloat16)
+    counts = jnp.einsum("bc,lco->lbo", earlier, owned, preferred_element_type=jnp.float32)
+    rank = jnp.sum(counts * owned.astype(jnp.float32), axis=2).astype(jnp.int32) - 1
+    position = owner * per_peer + rank
+    sorting = [
+        (jnp.arange(block_count, dtype=jnp.int32)[:, None] == position[which][None, :]).astype(
+            jnp.bfloat16
+        )
+        for which in range(4)
+    ]
+    halves = jnp.stack([slot // 32, slot % 32], axis=2).astype(jnp.bfloat16)
+    sent_halves = jnp.einsum(
+        "lib,lbh->lih", jnp.stack(sorting), halves, preferred_element_type=jnp.float32
+    )
+    sent_slots = (sent_halves[:, :, 0] * 32 + sent_halves[:, :, 1]).astype(jnp.int32)
     down1_to_up0 = lax.dot_general(
         sorting[1], sorting[3], (((1,), (1,)), ((), ())), preferred_element_type=jnp.float32
     ).astype(jnp.bfloat16)

time: 280 us -> 266 us (0.950)
  between operations: 16.7 us -> 3.43 us
  local copies, waits for them, and re-layouts: 12.4 us -> 8.89 us
    eq x0 -> x4, other arithmetic: none -> 3.23 us  [shards(): jnp.arange(block_count, dtype=jnp.int32)[:, None]]
    dot_general x0 -> x2, matrix products: none -> 3.19 us  [the longest x1 2.66 us: shards(): jnp.einsum('lib,lbh->lih', jnp.stack(sorting), halves, preferred_element_...]
    another operation x13 -> x15, other arithmetic: 5.7 us -> 4.48 us
where the time goes in v7:
time: 266 us; the launch traced here: 265 us
  blocking collectives  125 us (47%)
  waiting for transfers between devices  61 us (23%)
  matrix products  29.2 us (11%)
  other arithmetic  19.4 us (7%)
  starting transfers between devices  19 us (7%)
  local copies, waits for them, and re-layouts  8.89 us (3%)
  between operations  3.43 us (1%)
    all_to_all x3, blocking collectives, send(): lax.all_to_all(jnp.concatenate(chunks, axis=1), 'shard', 0, 0, tiled=True)  41 us
    all_to_all x2, blocking collectives, to_middle(): lax.all_to_all(jnp.concatenate(pieces, axis=1), 'clique', 0, 0, tiled=True)  36.5 us
    all_to_all x1, blocking collectives, from_middle(): lax.all_to_all(jnp.concatenate(chunks, axis=1), 'clique', 0, 0, tiled=True)  29.7 us
    all_to_all x1, waiting for transfers between devices, to_middle(): lax.all_to_all(jnp.concatenate(pieces, axis=1), 'clique', 0, 0, tiled=True)  26.5 us
    all_to_all x2, waiting for transfers between devices, from_middle(): lax.all_to_all(jnp.concatenate(chunks, axis=1), 'clique', 0, 0, tiled=True)  23.6 us
    dot_general x16, matrix products, split_dot(): lax.dot_general(one_hot, parts, (((contract,), (0,)), ((), ())), preferre...  18.4 us
    all_to_all x1, blocking collectives, fetch(): lax.all_to_all(jnp.concatenate(chunks, axis=1), 'shard', 0, 0, tiled=True)  17.4 us
    all_to_all x2, waiting for transfers between devices, fetch(): lax.all_to_all(jnp.concatenate(chunks, axis=1), 'shard', 0, 0, tiled=True)  10.9 us
  transfers between devices with their start and end apart: 5, of which 5 were waited for; matrix products, arithmetic and copies ran while one was open for 4% of the time, Pallas kernels for 0%

profile of v7, /device:TPU:0, one launch (start us, length us, event | category | flops | bytes accessed | tf_op | source)
XLA Modules:
  0.0 265.5 jit_solution(8466189723437217705)
XLA Ops:
  1.6 0.8 iota_compare_fusion.14
  2.4 0.8 iota_compare_fusion.16
  3.2 0.8 iota_compare_fusion.17
  4.0 0.8 iota_compare_fusion.15
  4.9 2.7 %fusion = f32[4,1024,2]{1,2,0:T(2,128)S(1)} fusion(pred[1,1024,1024]{2,1,0:T(32,128)(4,1)S(1)} %iota_compare_fusion.14, pred[1,1024,1024]{2,1,0:T(32,128)(4,1)S(1)} %iota_compare_fusion.15, pred[1,1024,1024]{2,1,0:T(32,128)(4,1)S(1)} %iota_compare_fusion.16, pred[1,1024,1024]{2,1,0:T(32,128)(4,1)S(1)} %iota_compare_fusion.17, ...), kind=kOutput, calls=%fused_computation.1 | convolution fusion | flops 29392896 | bytes 4243456 | tf_op jit(solution)/shard_map/lib,lbh->lih/dot_general | solution.py:67
  7.7 0.9 reduce-precision_convert_fusion.10
  9.5 0.8 fusion.5
  11.8 19.7 %all_to_all.60 = f32[4,528,128]{2,1,0:T(8,128)S(1)} all-to-all(f32[4,528,128]{2,1,0:T(8,128)S(1)} %pad_maximum_fusion), channel_id=1, replica_groups=mesh['clique'=8,'shard'=4] {'shard'}, dimensions={0} | all-to-all | bytes 2162688 | tf_op jit(solution)/shard_map/all_to_all | solution.py:90
  31.7 0.9 reduce-precision_convert_fusion.12
  32.6 0.8 fusion.11
  34.9 1.8 fusion.10
  36.8 1.0 pad_maximum_fusion.2
  37.9 4.9 %all-to-all-start.1 = ((f32[8,256,128]{2,1,0:T(8,128)}), f32[8,256,128]{2,1,0:T(8,128)S(1)}, u32[]{:S(2)}, u32[]{:S(2)}) async-start(f32[8,256,128]{2,1,0:T(8,128)} %pad_maximum_fusion.2), calls=%async_computation.1 | async-start | bytes 2097152 | tf_op jit(solution)/shard_map/all_to_all | solution.py:125
  42.8 26.5 %all-to-all-done.1 = f32[8,256,128]{2,1,0:T(8,128)S(1)} async-done(((f32[8,256,128]{2,1,0:T(8,128)}), f32[8,256,128]{2,1,0:T(8,128)S(1)}, u32[]{:S(2)}, u32[]{:S(2)}) %all-to-all-start.1) | async-done | bytes 1048608 | tf_op jit(solution)/shard_map/all_to_all | solution.py:125
  71.0 0.9 copy.30
  71.9 3.7 %all-to-all-start.2 = ((f32[8,128,128]{2,1,0:T(8,128)}), f32[8,128,128]{2,1,0:T(8,128)S(1)}, u32[]{:S(2)}, u32[]{:S(2)}) async-start(f32[8,128,128]{2,1,0:T(8,128)} %copy.30), calls=%async_computation.2 | async-start | bytes 1048576 | tf_op jit(solution)/shard_map/all_to_all | solution.py:132
  75.5 2.0 fusion.1
  77.6 13.0 %all-to-all-done.2 = f32[8,128,128]{2,1,0:T(8,128)S(1)} async-done(((f32[8,128,128]{2,1,0:T(8,128)}), f32[8,128,128]{2,1,0:T(8,128)S(1)}, u32[]{:S(2)}, u32[]{:S(2)}) %all-to-all-start.2) | async-done | bytes 524320 | tf_op jit(solution)/shard_map/all_to_all | solution.py:132
  90.7 0.8 fusion.13
  91.6 1.0 copy.31
  92.6 3.5 %all-to-all-start.3 = ((f32[4,256,128]{1,2,0:T(8,128)}), f32[4,256,128]{1,2,0:T(8,128)S(1)}, u32[]{:S(2)}, u32[]{:S(2)}) async-start(f32[4,256,128]{1,2,0:T(8,128)} %copy.31), calls=%async_computation.3 | async-start | bytes 1048576 | tf_op jit(solution)/shard_map/all_to_all | solution.py:114
  96.1 3.8 %fusion.35 = bf16[1024,1024]{1,0:T(8,128)(2,1)} fusion(s32[1024]{0:T(1024)S(1)} %bitcast.177, s32[1024]{0:T(1024)S(1)} %bitcast.173), kind=kOutput, calls=%fused_computation.52 | convolution fusion | flops 2150629376 | bytes 2105344 | tf_op jit(solution)/shard_map/dot_general | solution.py:71
  99.9 4.2 %all-to-all-done.3 = f32[4,256,128]{1,2,0:T(8,128)S(1)} async-done(((f32[4,256,128]{1,2,0:T(8,128)}), f32[4,256,128]{1,2,0:T(8,128)S(1)}, u32[]{:S(2)}, u32[]{:S(2)}) %all-to-all-start.3) | async-done | bytes 524320 | tf_op jit(solution)/shard_map/all_to_all | solution.py:114
  104.1 1.5 reduce-precision_convert_fusion.8
  108.2 10.6 %all_to_all.61 = f32[4,264,128]{2,1,0:T(8,128)S(1)} all-to-all(f32[4,264,128]{2,1,0:T(8,128)S(1)} %concatenate.130), channel_id=1, replica_groups=mesh['clique'=8,'shard'=4] {'shard'}, dimensions={0} | all-to-all | bytes 1081344 | tf_op jit(solution)/shard_map/all_to_all | solution.py:90
  121.0 18.6 %all_to_all.62 = f32[8,128,128]{2,1,0:T(8,128)S(1)} all-to-all(f32[8,128,128]{2,1,0:T(8,128)S(1)} %bitcast.160), channel_id=1, replica_groups=mesh['clique'=8,'shard'=4] {'clique'}, dimensions={0} | all-to-all | bytes 1048576 | tf_op jit(solution)/shard_map/all_to_all | solution.py:125
  139.6 1.1 fusion.116
  141.0 0.9 convolution_divide_fusion.1
  142.3 29.7 %all_to_all.63 = f32[8,264,128]{2,1,0:T(8,128)S(1)} all-to-all(f32[8,264,128]{2,1,0:T(8,128)S(1)} %copy.36), channel_id=1, replica_groups=mesh['clique'=8,'shard'=4] {'clique'}, dimensions={0} | all-to-all | bytes 2162688 | tf_op jit(solution)/shard_map/all_to_all | solution.py:132
  173.4 0.8 fusion.9
  174.4 0.8 fusion.14
  175.4 17.4 %all_to_all.64 = f32[4,520,128]{2,1,0:T(8,128)S(1)} all-to-all(f32[4,520,128]{2,1,0:T(8,128)S(1)} %maximum_maximum_fusion), channel_id=1, replica_groups=mesh['clique'=8,'shard'=4] {'shard'}, dimensions={0} | all-to-all | bytes 2129920 | tf_op jit(solution)/shard_map/all_to_all | solution.py:114
  194.1 0.9 fusion.165
  198.1 10.7 %all_to_all.65 = f32[4,264,128]{2,1,0:T(8,128)S(1)} all-to-all(f32[4,264,128]{2,1,0:T(8,128)S(1)} %concatenate.138), channel_id=1, replica_groups=mesh['clique'=8,'shard'=4] {'shard'}, dimensions={0} | all-to-all | bytes 1081344 | tf_op jit(solution)/shard_map/all_to_all | solution.py:90
  211.1 17.9 %all_to_all.66 = f32[8,128,128]{2,1,0:T(8,128)S(1)} all-to-all(f32[8,128,128]{2,1,0:T(8,128)S(1)} %bitcast.161), channel_id=1, replica_groups=mesh['clique'=8,'shard'=4] {'clique'}, dimensions={0} | all-to-all | bytes 1048576 | tf_op jit(solution)/shard_map/all_to_all | solution.py:125
  229.0 0.9 convolution_divide_fusion
  229.9 0.9 copy.38
  230.8 3.5 %all-to-all-start.10 = ((f32[8,128,128]{2,1,0:T(8,128)}), f32[8,128,128]{2,1,0:T(8,128)S(1)}, u32[]{:S(2)}, u32[]{:S(2)}) async-start(f32[8,128,128]{2,1,0:T(8,128)} %copy.38), calls=%async_computation.10 | async-start | bytes 1048576 | tf_op jit(solution)/shard_map/all_to_all | solution.py:132
  234.3 2.3 fusion.3
  236.7 2.2 fusion.6
  239.0 10.6 %all-to-all-done.10 = f32[8,128,128]{2,1,0:T(8,128)S(1)} async-done(((f32[8,128,128]{2,1,0:T(8,128)}), f32[8,128,128]{2,1,0:T(8,128)S(1)}, u32[]{:S(2)}, u32[]{:S(2)}) %all-to-all-start.10) | async-done | bytes 524320 | tf_op jit(solution)/shard_map/all_to_all | solution.py:132
  249.7 0.8 fusion.15
  250.5 0.9 slice_add_fusion.1
  251.3 3.5 %all-to-all-start.11 = ((f32[4,256,128]{2,1,0:T(8,128)}), f32[4,256,128]{2,1,0:T(8,128)S(1)}, u32[]{:S(2)}, u32[]{:S(2)}) async-start(f32[4,256,128]{2,1,0:T(8,128)} %bitcast.54), calls=%async_computation.11 | async-start | bytes 1048576 | tf_op jit(solution)/shard_map/all_to_all | solution.py:114
  254.9 1.3 fusion.63
  256.1 6.7 %all-to-all-done.11 = f32[4,256,128]{2,1,0:T(8,128)S(1)} async-done(((f32[4,256,128]{2,1,0:T(8,128)}), f32[4,256,128]{2,1,0:T(8,128)S(1)}, u32[]{:S(2)}, u32[]{:S(2)}) %all-to-all-start.11) | async-done | bytes 524320 | tf_op jit(solution)/shard_map/all_to_all | solution.py:114
  262.9 1.3 fusion.4
  264.2 1.2 maximum_bitcast_fusion
  (85 shorter events, 19.0 us)
Async XLA Ops:
  4.9 2.8 %copy-start.3 = (f32[3,1,1024,128]{3,2,1,0:T(8,128)S(1)}, f32[3,1,1024,128]{3,2,1,0:T(8,128)}, u32[]{:S(2)}) copy-start(f32[3,1,1024,128]{3,2,1,0:T(8,128)} %param.4) | copy-start | bytes 4718596
  36.8 6.0 %copy-start.6 = (s32[2,8]{1,0:T(2,128)S(1)}, s32[2,8]{1,0:T(2,128)}, u32[]{:S(2)}) copy-start(s32[2,8]{1,0:T(2,128)} %param.7) | copy-start | bytes 196
  37.9 31.5 %all-to-all-start.1 = ((f32[8,256,128]{2,1,0:T(8,128)}), f32[8,256,128]{2,1,0:T(8,128)S(1)}, u32[]{:S(2)}, u32[]{:S(2)}) async-start(f32[8,256,128]{2,1,0:T(8,128)} %pad_maximum_fusion.2), calls=%async_computation.1 | async-start | bytes 2097152 | tf_op jit(solution)/shard_map/all_to_all | solution.py:125
  69.4 0.8 copy-start.1
  69.4 6.1 %copy-start.4 = (bf16[1024,128]{1,0:T(8,128)(2,1)S(1)}, bf16[1024,128]{1,0:T(8,128)(2,1)}, u32[]{:S(2)}) copy-start(bf16[1024,128]{1,0:T(8,128)(2,1)} %get-tuple-element.18) | copy-start | bytes 786436
  71.9 18.8 %all-to-all-start.2 = ((f32[8,128,128]{2,1,0:T(8,128)}), f32[8,128,128]{2,1,0:T(8,128)S(1)}, u32[]{:S(2)}, u32[]{:S(2)}) async-start(f32[8,128,128]{2,1,0:T(8,128)} %copy.30), calls=%async_computation.2 | async-start | bytes 1048576 | tf_op jit(solution)/shard_map/all_to_all | solution.py:132
  92.6 11.4 %all-to-all-start.3 = ((f32[4,256,128]{1,2,0:T(8,128)}), f32[4,256,128]{1,2,0:T(8,128)S(1)}, u32[]{:S(2)}, u32[]{:S(2)}) async-start(f32[4,256,128]{1,2,0:T(8,128)} %copy.31), calls=%async_computation.3 | async-start | bytes 1048576 | tf_op jit(solution)/shard_map/all_to_all | solution.py:114
  104.1 1.9 copy-start.7
  194.1 1.8 copy-start.8
  195.1 2.3 copy-start.5
  211.0 17.9 %copy-start.2 = (f32[8,128,128]{2,1,0:T(8,128)S(1)}, f32[8,128,128]{2,1,0:T(8,128)}, u32[]{:S(2)}) copy-start(f32[8,128,128]{2,1,0:T(8,128)} %copy-done.1) | copy-start | bytes 1572868
  230.8 18.8 %all-to-all-start.10 = ((f32[8,128,128]{2,1,0:T(8,128)}), f32[8,128,128]{2,1,0:T(8,128)S(1)}, u32[]{:S(2)}, u32[]{:S(2)}) async-start(f32[8,128,128]{2,1,0:T(8,128)} %copy.38), calls=%async_computation.10 | async-start | bytes 1048576 | tf_op jit(solution)/shard_map/all_to_all | solution.py:132
  234.3 2.3 copy-start
  251.3 11.4 %all-to-all-start.11 = ((f32[4,256,128]{2,1,0:T(8,128)}), f32[4,256,128]{2,1,0:T(8,128)S(1)}, u32[]{:S(2)}, u32[]{:S(2)}) async-start(f32[4,256,128]{2,1,0:T(8,128)} %bitcast.54), calls=%async_computation.11 | async-start | bytes 1048576 | tf_op jit(solution)/shard_map/all_to_all | solution.py:114

commit v8 on v7

--- a/solution.py
+++ b/solution.py
@@ -54,7 +54,9 @@
         jnp.arange(block_count, dtype=jnp.int32)[:, None]
         >= jnp.arange(block_count, dtype=jnp.int32)[None, :]
     ).astype(jnp.bfloat16)
-    counts = jnp.einsum("bc,lco->lbo", earlier, owned, preferred_element_type=jnp.float32)
+    owned_all = owned.transpose(1, 0, 2).reshape(block_count, 4 * shard_count)
+    counts = jnp.dot(earlier, owned_all, preferred_element_type=jnp.float32)
+    counts = counts.reshape(block_count, 4, shard_count).transpose(1, 0, 2)
     rank = jnp.sum(counts * owned.astype(jnp.float32), axis=2).astype(jnp.int32) - 1
     position = owner * per_peer + rank
     sorting = [

time: 266 us -> 267 us (level)
  no operation moved by 1% of the time
where the time goes in v8:
time: 267 us; the launch traced here: 266 us
  blocking collectives  125 us (47%)
  waiting for transfers between devices  61 us (23%)
  matrix products  29.2 us (11%)
  other arithmetic  19.5 us (7%)
  starting transfers between devices  19 us (7%)
  local copies, waits for them, and re-layouts  9.03 us (3%)
  between operations  3.46 us (1%)
    all_to_all x3, blocking collectives, send(): lax.all_to_all(jnp.concatenate(chunks, axis=1), 'shard', 0, 0, tiled=True)  41 us
    all_to_all x2, blocking collectives, to_middle(): lax.all_to_all(jnp.concatenate(pieces, axis=1), 'clique', 0, 0, tiled=True)  36.5 us
    all_to_all x1, blocking collectives, from_middle(): lax.all_to_all(jnp.concatenate(chunks, axis=1), 'clique', 0, 0, tiled=True)  29.7 us
    all_to_all x1, waiting for transfers between devices, to_middle(): lax.all_to_all(jnp.concatenate(pieces, axis=1), 'clique', 0, 0, tiled=True)  26.5 us
    all_to_all x2, waiting for transfers between devices, from_middle(): lax.all_to_all(jnp.concatenate(chunks, axis=1), 'clique', 0, 0, tiled=True)  23.6 us
    dot_general x16, matrix products, split_dot(): lax.dot_general(one_hot, parts, (((contract,), (0,)), ((), ())), preferre...  18.4 us
    all_to_all x1, blocking collectives, fetch(): lax.all_to_all(jnp.concatenate(chunks, axis=1), 'shard', 0, 0, tiled=True)  17.4 us
    all_to_all x2, waiting for transfers between devices, fetch(): lax.all_to_all(jnp.concatenate(chunks, axis=1), 'shard', 0, 0, tiled=True)  10.9 us
  transfers between devices with their start and end apart: 5, of which 5 were waited for; matrix products, arithmetic and copies ran while one was open for 4% of the time, Pallas kernels for 0%

profile of v8, /device:TPU:0, one launch (start us, length us, event | category | flops | bytes accessed | tf_op | source)
XLA Modules:
  0.0 265.8 jit_solution(5651623463467168781)
XLA Ops:
  1.9 0.8 iota_compare_fusion.14
  2.7 0.8 iota_compare_fusion.16
  3.5 0.8 iota_compare_fusion.17
  4.4 0.8 iota_compare_fusion.15
  5.2 2.7 %fusion = f32[4,1024,2]{1,2,0:T(2,128)S(1)} fusion(pred[1,1024,1024]{2,1,0:T(32,128)(4,1)S(1)} %iota_compare_fusion.14, pred[1,1024,1024]{2,1,0:T(32,128)(4,1)S(1)} %iota_compare_fusion.15, pred[1,1024,1024]{2,1,0:T(32,128)(4,1)S(1)} %iota_compare_fusion.16, pred[1,1024,1024]{2,1,0:T(32,128)(4,1)S(1)} %iota_compare_fusion.17, ...), kind=kOutput, calls=%fused_computation.1 | convolution fusion | flops 29392896 | bytes 4243456 | tf_op jit(solution)/shard_map/lib,lbh->lih/dot_general | solution.py:69
  8.0 0.9 reduce-precision_convert_fusion.10
  9.8 0.8 fusion.5
  12.1 19.8 %all_to_all.60 = f32[4,528,128]{2,1,0:T(8,128)S(1)} all-to-all(f32[4,528,128]{2,1,0:T(8,128)S(1)} %pad_maximum_fusion), channel_id=1, replica_groups=mesh['clique'=8,'shard'=4] {'shard'}, dimensions={0} | all-to-all | bytes 2162688 | tf_op jit(solution)/shard_map/all_to_all | solution.py:92
  32.0 0.9 reduce-precision_convert_fusion.12
  33.0 0.8 fusion.11
  35.2 1.8 fusion.10
  37.1 1.0 pad_maximum_fusion.2
  38.2 4.9 %all-to-all-start.1 = ((f32[8,256,128]{2,1,0:T(8,128)}), f32[8,256,128]{2,1,0:T(8,128)S(1)}, u32[]{:S(2)}, u32[]{:S(2)}) async-start(f32[8,256,128]{2,1,0:T(8,128)} %pad_maximum_fusion.2), calls=%async_computation.1 | async-start | bytes 2097152 | tf_op jit(solution)/shard_map/all_to_all | solution.py:127
  43.1 26.5 %all-to-all-done.1 = f32[8,256,128]{2,1,0:T(8,128)S(1)} async-done(((f32[8,256,128]{2,1,0:T(8,128)}), f32[8,256,128]{2,1,0:T(8,128)S(1)}, u32[]{:S(2)}, u32[]{:S(2)}) %all-to-all-start.1) | async-done | bytes 1048608 | tf_op jit(solution)/shard_map/all_to_all | solution.py:127
  71.3 0.9 copy.30
  72.2 3.7 %all-to-all-start.2 = ((f32[8,128,128]{2,1,0:T(8,128)}), f32[8,128,128]{2,1,0:T(8,128)S(1)}, u32[]{:S(2)}, u32[]{:S(2)}) async-start(f32[8,128,128]{2,1,0:T(8,128)} %copy.30), calls=%async_computation.2 | async-start | bytes 1048576 | tf_op jit(solution)/shard_map/all_to_all | solution.py:134
  75.9 2.0 fusion.1
  77.9 13.0 %all-to-all-done.2 = f32[8,128,128]{2,1,0:T(8,128)S(1)} async-done(((f32[8,128,128]{2,1,0:T(8,128)}), f32[8,128,128]{2,1,0:T(8,128)S(1)}, u32[]{:S(2)}, u32[]{:S(2)}) %all-to-all-start.2) | async-done | bytes 524320 | tf_op jit(solution)/shard_map/all_to_all | solution.py:134
  91.0 0.8 fusion.13
  91.9 1.0 copy.31
  92.9 3.5 %all-to-all-start.3 = ((f32[4,256,128]{1,2,0:T(8,128)}), f32[4,256,128]{1,2,0:T(8,128)S(1)}, u32[]{:S(2)}, u32[]{:S(2)}) async-start(f32[4,256,128]{1,2,0:T(8,128)} %copy.31), calls=%async_computation.3 | async-start | bytes 1048576 | tf_op jit(solution)/shard_map/all_to_all | solution.py:116
  96.4 3.8 %fusion.35 = bf16[1024,1024]{1,0:T(8,128)(2,1)} fusion(s32[1024]{0:T(1024)S(1)} %bitcast.184, s32[1024]{0:T(1024)S(1)} %bitcast.180), kind=kOutput, calls=%fused_computation.52 | convolution fusion | flops 2150629376 | bytes 2105344 | tf_op jit(solution)/shard_map/dot_general | solution.py:73
  100.2 4.2 %all-to-all-done.3 = f32[4,256,128]{1,2,0:T(8,128)S(1)} async-done(((f32[4,256,128]{1,2,0:T(8,128)}), f32[4,256,128]{1,2,0:T(8,128)S(1)}, u32[]{:S(2)}, u32[]{:S(2)}) %all-to-all-start.3) | async-done | bytes 524320 | tf_op jit(solution)/shard_map/all_to_all | solution.py:116
  104.4 1.5 reduce-precision_convert_fusion.8
  108.5 10.6 %all_to_all.61 = f32[4,264,128]{2,1,0:T(8,128)S(1)} all-to-all(f32[4,264,128]{2,1,0:T(8,128)S(1)} %concatenate.130), channel_id=1, replica_groups=mesh['clique'=8,'shard'=4] {'shard'}, dimensions={0} | all-to-all | bytes 1081344 | tf_op jit(solution)/shard_map/all_to_all | solution.py:92
  121.3 18.7 %all_to_all.62 = f32[8,128,128]{2,1,0:T(8,128)S(1)} all-to-all(f32[8,128,128]{2,1,0:T(8,128)S(1)} %bitcast.167), channel_id=1, replica_groups=mesh['clique'=8,'shard'=4] {'clique'}, dimensions={0} | all-to-all | bytes 1048576 | tf_op jit(solution)/shard_map/all_to_all | solution.py:127
  140.0 1.1 fusion.116
  141.3 0.9 convolution_divide_fusion.1
  142.6 29.7 %all_to_all.63 = f32[8,264,128]{2,1,0:T(8,128)S(1)} all-to-all(f32[8,264,128]{2,1,0:T(8,128)S(1)} %copy.36), channel_id=1, replica_groups=mesh['clique'=8,'shard'=4] {'clique'}, dimensions={0} | all-to-all | bytes 2162688 | tf_op jit(solution)/shard_map/all_to_all | solution.py:134
  173.7 0.8 fusion.9
  174.7 0.8 fusion.14
  175.7 17.4 %all_to_all.64 = f32[4,520,128]{2,1,0:T(8,128)S(1)} all-to-all(f32[4,520,128]{2,1,0:T(8,128)S(1)} %maximum_maximum_fusion), channel_id=1, replica_groups=mesh['clique'=8,'shard'=4] {'shard'}, dimensions={0} | all-to-all | bytes 2129920 | tf_op jit(solution)/shard_map/all_to_all | solution.py:116
  194.4 0.9 fusion.164
  198.4 10.7 %all_to_all.65 = f32[4,264,128]{2,1,0:T(8,128)S(1)} all-to-all(f32[4,264,128]{2,1,0:T(8,128)S(1)} %concatenate.138), channel_id=1, replica_groups=mesh['clique'=8,'shard'=4] {'shard'}, dimensions={0} | all-to-all | bytes 1081344 | tf_op jit(solution)/shard_map/all_to_all | solution.py:92
  211.4 17.9 %all_to_all.66 = f32[8,128,128]{2,1,0:T(8,128)S(1)} all-to-all(f32[8,128,128]{2,1,0:T(8,128)S(1)} %bitcast.168), channel_id=1, replica_groups=mesh['clique'=8,'shard'=4] {'clique'}, dimensions={0} | all-to-all | bytes 1048576 | tf_op jit(solution)/shard_map/all_to_all | solution.py:127
  229.3 0.9 convolution_divide_fusion
  230.2 0.9 copy.38
  231.1 3.5 %all-to-all-start.10 = ((f32[8,128,128]{2,1,0:T(8,128)}), f32[8,128,128]{2,1,0:T(8,128)S(1)}, u32[]{:S(2)}, u32[]{:S(2)}) async-start(f32[8,128,128]{2,1,0:T(8,128)} %copy.38), calls=%async_computation.10 | async-start | bytes 1048576 | tf_op jit(solution)/shard_map/all_to_all | solution.py:134
  234.6 2.3 fusion.3
  237.1 2.2 fusion.6
  239.3 10.6 %all-to-all-done.10 = f32[8,128,128]{2,1,0:T(8,128)S(1)} async-done(((f32[8,128,128]{2,1,0:T(8,128)}), f32[8,128,128]{2,1,0:T(8,128)S(1)}, u32[]{:S(2)}, u32[]{:S(2)}) %all-to-all-start.10) | async-done | bytes 524320 | tf_op jit(solution)/shard_map/all_to_all | solution.py:134
  250.0 0.8 fusion.15
  250.8 0.9 slice_add_fusion.1
  251.7 3.5 %all-to-all-start.11 = ((f32[4,256,128]{2,1,0:T(8,128)}), f32[4,256,128]{2,1,0:T(8,128)S(1)}, u32[]{:S(2)}, u32[]{:S(2)}) async-start(f32[4,256,128]{2,1,0:T(8,128)} %bitcast.56), calls=%async_computation.11 | async-start | bytes 1048576 | tf_op jit(solution)/shard_map/all_to_all | solution.py:116
  255.2 1.3 fusion.63
  256.5 6.7 %all-to-all-done.11 = f32[4,256,128]{2,1,0:T(8,128)S(1)} async-done(((f32[4,256,128]{2,1,0:T(8,128)}), f32[4,256,128]{2,1,0:T(8,128)S(1)}, u32[]{:S(2)}, u32[]{:S(2)}) %all-to-all-start.11) | async-done | bytes 524320 | tf_op jit(solution)/shard_map/all_to_all | solution.py:116
  263.2 1.3 fusion.4
  264.6 1.2 maximum_bitcast_fusion
  (92 shorter events, 19.2 us)
Async XLA Ops:
  5.2 2.8 %copy-start.3 = (f32[3,1,1024,128]{3,2,1,0:T(8,128)S(1)}, f32[3,1,1024,128]{3,2,1,0:T(8,128)}, u32[]{:S(2)}) copy-start(f32[3,1,1024,128]{3,2,1,0:T(8,128)} %param.4) | copy-start | bytes 4718596
  37.1 5.9 %copy-start.6 = (s32[2,8]{1,0:T(2,128)S(1)}, s32[2,8]{1,0:T(2,128)}, u32[]{:S(2)}) copy-start(s32[2,8]{1,0:T(2,128)} %param.7) | copy-start | bytes 196
  38.2 31.4 %all-to-all-start.1 = ((f32[8,256,128]{2,1,0:T(8,128)}), f32[8,256,128]{2,1,0:T(8,128)S(1)}, u32[]{:S(2)}, u32[]{:S(2)}) async-start(f32[8,256,128]{2,1,0:T(8,128)} %pad_maximum_fusion.2), calls=%async_computation.1 | async-start | bytes 2097152 | tf_op jit(solution)/shard_map/all_to_all | solution.py:127
  69.7 0.8 copy-start.1
  69.7 6.1 %copy-start.4 = (bf16[1024,128]{1,0:T(8,128)(2,1)S(1)}, bf16[1024,128]{1,0:T(8,128)(2,1)}, u32[]{:S(2)}) copy-start(bf16[1024,128]{1,0:T(8,128)(2,1)} %get-tuple-element.18) | copy-start | bytes 786436
  72.2 18.8 %all-to-all-start.2 = ((f32[8,128,128]{2,1,0:T(8,128)}), f32[8,128,128]{2,1,0:T(8,128)S(1)}, u32[]{:S(2)}, u32[]{:S(2)}) async-start(f32[8,128,128]{2,1,0:T(8,128)} %copy.30), calls=%async_computation.2 | async-start | bytes 1048576 | tf_op jit(solution)/shard_map/all_to_all | solution.py:134
  92.9 11.4 %all-to-all-start.3 = ((f32[4,256,128]{1,2,0:T(8,128)}), f32[4,256,128]{1,2,0:T(8,128)S(1)}, u32[]{:S(2)}, u32[]{:S(2)}) async-start(f32[4,256,128]{1,2,0:T(8,128)} %copy.31), calls=%async_computation.3 | async-start | bytes 1048576 | tf_op jit(solution)/shard_map/all_to_all | solution.py:116
  104.4 1.9 copy-start.7
  194.4 1.8 copy-start.8
  195.4 2.3 copy-start.5
  211.4 17.9 %copy-start.2 = (f32[8,128,128]{2,1,0:T(8,128)S(1)}, f32[8,128,128]{2,1,0:T(8,128)}, u32[]{:S(2)}) copy-start(f32[8,128,128]{2,1,0:T(8,128)} %copy-done.1) | copy-start | bytes 1572868
  231.1 18.8 %all-to-all-start.10 = ((f32[8,128,128]{2,1,0:T(8,128)}), f32[8,128,128]{2,1,0:T(8,128)S(1)}, u32[]{:S(2)}, u32[]{:S(2)}) async-start(f32[8,128,128]{2,1,0:T(8,128)} %copy.38), calls=%async_computation.10 | async-start | bytes 1048576 | tf_op jit(solution)/shard_map/all_to_all | solution.py:134
  234.6 2.3 copy-start
  251.7 11.4 %all-to-all-start.11 = ((f32[4,256,128]{2,1,0:T(8,128)}), f32[4,256,128]{2,1,0:T(8,128)S(1)}, u32[]{:S(2)}, u32[]{:S(2)}) async-start(f32[4,256,128]{2,1,0:T(8,128)} %bitcast.56), calls=%async_computation.11 | async-start | bytes 1048576 | tf_op jit(solution)/shard_map/all_to_all | solution.py:116

commit v9 on v8

--- a/solution.py
+++ b/solution.py
@@ -167,8 +167,9 @@
     partial = jnp.dot(sel[0], jnp.sum(fresh0_mid, axis=(1, 2)), precision=lax.Precision.HIGHEST)
     update0_mid = mix(sel[0], fresh0_mid) / scaled0_mid
     (update0, incoming0), range_total = from_middle([update0_mid, incoming0_mid], partial)
-    (picked, update0), total = fetch([(incoming0, 2), (update0, 1)], range_total)
-    out0 = split_dot(sorting[2], t0_down0 * picked, transposed=True)
+    (update0,), total = fetch([(update0, 1)], range_total)
+    incoming0 = lax.all_gather(incoming0, "shard", axis=0, tiled=True)
+    out0 = t0 * gather_rows(incoming0, lists[2])
     t1_up0 = t1_up0 * (update0 * (sep_states / total))
     out1 = split_dot(sorting[1], t1_up0, transposed=True)
     t1_down1 = split_dot(down1_to_up0, t1_up0, transposed=True)

time: 267 us -> 277 us (1.037)
  between operations: 3.46 us -> 16.8 us
  blocking collectives: 125 us -> 119 us
  waiting for transfers between devices: 61 us -> 65.6 us
    all_to_all x2 -> x1, blocking collectives: 36.5 us -> 18.6 us  [to_middle(): lax.all_to_all(jnp.concatenate(pieces, axis=1), 'clique', 0, 0, tiled=True)]
    all_to_all x1 -> x2, blocking collectives: 29.7 us -> 47.4 us  [from_middle(): lax.all_to_all(jnp.concatenate(chunks, axis=1), 'clique', 0, 0, tiled=True)]
    all_to_all x1 -> x2, waiting for transfers between devices: 26.5 us -> 41.1 us  [to_middle(): lax.all_to_all(jnp.concatenate(pieces, axis=1), 'clique', 0, 0, tiled=True)]
    all_to_all x2 -> x1, waiting for transfers between devices: 23.6 us -> 13.1 us  [from_middle(): lax.all_to_all(jnp.concatenate(chunks, axis=1), 'clique', 0, 0, tiled=True)]
    all_to_all x1, blocking collectives: 17.4 us -> 11.8 us  [fetch(): lax.all_to_all(jnp.concatenate(chunks, axis=1), 'shard', 0, 0, tiled=True)]
    all_to_all x1 -> x2, starting transfers between devices: 4.87 us -> 8.37 us  [to_middle(): lax.all_to_all(jnp.concatenate(pieces, axis=1), 'clique', 0, 0, tiled=True)]
    all_to_all x2 -> x1, starting transfers between devices: 7.16 us -> 3.67 us  [from_middle(): lax.all_to_all(jnp.concatenate(chunks, axis=1), 'clique', 0, 0, tiled=True)]
    dot_general x16 -> x15, matrix products: 18.4 us -> 16.1 us  [split_dot(): lax.dot_general(one_hot, parts, (((contract,), (0,)), ((), ())), preferre...]
  transfers between devices with their start and end apart: 5 -> 6, of which waited for: 5 -> 5; matrix products, arithmetic and copies ran while one was open for 4% -> 4% of each run, Pallas kernels for 0% -> 0%
where the time goes in v9:
time: 277 us; the launch traced here: 276 us
  blocking collectives  119 us (43%)
  waiting for transfers between devices  65.6 us (24%)
  matrix products  27 us (10%)
  starting transfers between devices  19 us (7%)
  other arithmetic  18.9 us (7%)
  between operations  16.8 us (6%)
  local copies, waits for them, and re-layouts  10.1 us (4%)
    all_to_all x2, blocking collectives, from_middle(): lax.all_to_all(jnp.concatenate(chunks, axis=1), 'clique', 0, 0, tiled=True)  47.4 us
    all_to_all x2, waiting for transfers between devices, to_middle(): lax.all_to_all(jnp.concatenate(pieces, axis=1), 'clique', 0, 0, tiled=True)  41.1 us
    all_to_all x3, blocking collectives, send(): lax.all_to_all(jnp.concatenate(chunks, axis=1), 'shard', 0, 0, tiled=True)  41 us
    all_to_all x1, blocking collectives, to_middle(): lax.all_to_all(jnp.concatenate(pieces, axis=1), 'clique', 0, 0, tiled=True)  18.6 us
    dot_general x15, matrix products, split_dot(): lax.dot_general(one_hot, parts, (((contract,), (0,)), ((), ())), preferre...  16.1 us
    all_to_all x1, waiting for transfers between devices, from_middle(): lax.all_to_all(jnp.concatenate(chunks, axis=1), 'clique', 0, 0, tiled=True)  13.1 us
    all_to_all x1, blocking collectives, fetch(): lax.all_to_all(jnp.concatenate(chunks, axis=1), 'shard', 0, 0, tiled=True)  11.8 us
    all_to_all x2, waiting for transfers between devices, fetch(): lax.all_to_all(jnp.concatenate(chunks, axis=1), 'shard', 0, 0, tiled=True)  10.8 us
  transfers between devices with their start and end apart: 6, of which 5 were waited for; matrix products, arithmetic and copies ran while one was open for 4% of the time, Pallas kernels for 0%

profile of v9, /device:TPU:0, one launch (start us, length us, event | category | flops | bytes accessed | tf_op | source)
XLA Modules:
  0.0 276.3 jit_solution(7213583799183751425)
XLA Ops:
  6.5 0.9 slice_bitcast_fusion.4
  8.4 0.9 reduce-precision_convert_fusion.9
  9.3 0.8 iota_compare_fusion.17
  11.7 0.8 iota_compare_fusion.14
  12.5 0.8 iota_compare_fusion.15
  13.3 0.8 iota_compare_fusion.16
  14.3 2.7 fusion.1
  17.1 0.8 fusion.10
  18.8 19.7 %all_to_all.60 = f32[4,528,128]{2,1,0:T(8,128)S(1)} all-to-all(f32[4,528,128]{2,1,0:T(8,128)S(1)} %pad_maximum_fusion), channel_id=1, replica_groups=mesh['clique'=8,'shard'=4] {'shard'}, dimensions={0} | all-to-all | bytes 2162688 | tf_op jit(solution)/shard_map/all_to_all | solution.py:92
  41.9 1.0 pad_maximum_fusion.2
  42.9 4.9 %all-to-all-start.1 = ((f32[8,256,128]{2,1,0:T(8,128)}), f32[8,256,128]{2,1,0:T(8,128)S(1)}, u32[]{:S(2)}, u32[]{:S(2)}) async-start(f32[8,256,128]{2,1,0:T(8,128)} %pad_maximum_fusion.2), calls=%async_computation.1 | async-start | bytes 2097152 | tf_op jit(solution)/shard_map/all_to_all | solution.py:127
  47.8 26.5 %all-to-all-done.1 = f32[8,256,128]{2,1,0:T(8,128)S(1)} async-done(((f32[8,256,128]{2,1,0:T(8,128)}), f32[8,256,128]{2,1,0:T(8,128)S(1)}, u32[]{:S(2)}, u32[]{:S(2)}) %all-to-all-start.1) | async-done | bytes 1048608 | tf_op jit(solution)/shard_map/all_to_all | solution.py:127
  75.2 0.9 copy.30
  76.1 3.7 %all-to-all-start.2 = ((f32[8,128,128]{2,1,0:T(8,128)}), f32[8,128,128]{2,1,0:T(8,128)S(1)}, u32[]{:S(2)}, u32[]{:S(2)}) async-start(f32[8,128,128]{2,1,0:T(8,128)} %copy.30), calls=%async_computation.2 | async-start | bytes 1048576 | tf_op jit(solution)/shard_map/all_to_all | solution.py:134
  79.8 2.0 fusion.3
  81.8 13.1 %all-to-all-done.2 = f32[8,128,128]{2,1,0:T(8,128)S(1)} async-done(((f32[8,128,128]{2,1,0:T(8,128)}), f32[8,128,128]{2,1,0:T(8,128)S(1)}, u32[]{:S(2)}, u32[]{:S(2)}) %all-to-all-start.2) | async-done | bytes 524320 | tf_op jit(solution)/shard_map/all_to_all | solution.py:134
  95.0 0.8 fusion.13
  95.9 1.0 copy.31
  96.9 3.5 %all-to-all-start.3 = ((f32[4,256,128]{1,2,0:T(8,128)}), f32[4,256,128]{1,2,0:T(8,128)S(1)}, u32[]{:S(2)}, u32[]{:S(2)}) async-start(f32[4,256,128]{1,2,0:T(8,128)} %copy.31), calls=%async_computation.3 | async-start | bytes 1048576 | tf_op jit(solution)/shard_map/all_to_all | solution.py:116
  100.3 3.8 %fusion.37 = bf16[1024,1024]{1,0:T(8,128)(2,1)} fusion(s32[1024]{0:T(1024)S(1)} %bitcast.170, s32[1024]{0:T(1024)S(1)} %bitcast.166), kind=kOutput, calls=%fused_computation.56 | convolution fusion | flops 2150629376 | bytes 2105344 | tf_op jit(solution)/shard_map/dot_general | solution.py:73
  104.1 4.2 %all-to-all-done.3 = f32[4,256,128]{1,2,0:T(8,128)S(1)} async-done(((f32[4,256,128]{1,2,0:T(8,128)}), f32[4,256,128]{1,2,0:T(8,128)S(1)}, u32[]{:S(2)}, u32[]{:S(2)}) %all-to-all-start.3) | async-done | bytes 524320 | tf_op jit(solution)/shard_map/all_to_all | solution.py:116
  108.5 1.4 copy-done.2
  112.1 10.6 %all_to_all.61 = f32[4,264,128]{2,1,0:T(8,128)S(1)} all-to-all(f32[4,264,128]{2,1,0:T(8,128)S(1)} %concatenate.126), channel_id=1, replica_groups=mesh['clique'=8,'shard'=4] {'shard'}, dimensions={0} | all-to-all | bytes 1081344 | tf_op jit(solution)/shard_map/all_to_all | solution.py:92
  124.9 18.6 %all_to_all.62 = f32[8,128,128]{2,1,0:T(8,128)S(1)} all-to-all(f32[8,128,128]{2,1,0:T(8,128)S(1)} %bitcast.156), channel_id=1, replica_groups=mesh['clique'=8,'shard'=4] {'clique'}, dimensions={0} | all-to-all | bytes 1048576 | tf_op jit(solution)/shard_map/all_to_all | solution.py:127
  143.6 1.1 fusion.111
  144.9 0.9 convolution_divide_fusion.1
  146.2 29.7 %all_to_all.63 = f32[8,264,128]{2,1,0:T(8,128)S(1)} all-to-all(f32[8,264,128]{2,1,0:T(8,128)S(1)} %copy.36), channel_id=1, replica_groups=mesh['clique'=8,'shard'=4] {'clique'}, dimensions={0} | all-to-all | bytes 2162688 | tf_op jit(solution)/shard_map/all_to_all | solution.py:134
  175.9 0.9 fusion.156
  176.9 0.8 fusion.14
  179.1 11.8 %all_to_all.64 = f32[4,264,128]{2,1,0:T(8,128)S(1)} all-to-all(f32[4,264,128]{2,1,0:T(8,128)S(1)} %concatenate.131), channel_id=1, replica_groups=mesh['clique'=8,'shard'=4] {'shard'}, dimensions={0} | all-to-all | bytes 1081344 | tf_op jit(solution)/shard_map/all_to_all | solution.py:116
  192.4 1.4 copy-done.3
  194.6 0.8 fusion.153
  196.1 10.7 %all_to_all.65 = f32[4,264,128]{2,1,0:T(8,128)S(1)} all-to-all(f32[4,264,128]{2,1,0:T(8,128)S(1)} %concatenate.133), channel_id=1, replica_groups=mesh['clique'=8,'shard'=4] {'shard'}, dimensions={0} | all-to-all | bytes 1081344 | tf_op jit(solution)/shard_map/all_to_all | solution.py:92
  209.1 0.9 fusion.61
  210.0 3.5 %all-to-all-start.9 = ((f32[8,128,128]{2,1,0:T(8,128)}), f32[8,128,128]{2,1,0:T(8,128)S(1)}, u32[]{:S(2)}, u32[]{:S(2)}) async-start(f32[8,128,128]{2,1,0:T(8,128)} %bitcast.53), calls=%async_computation.9 | async-start | bytes 1048576 | tf_op jit(solution)/shard_map/all_to_all | solution.py:127
  214.2 14.5 %all-to-all-done.9 = f32[8,128,128]{2,1,0:T(8,128)S(1)} async-done(((f32[8,128,128]{2,1,0:T(8,128)}), f32[8,128,128]{2,1,0:T(8,128)S(1)}, u32[]{:S(2)}, u32[]{:S(2)}) %all-to-all-start.9) | async-done | bytes 524320 | tf_op jit(solution)/shard_map/all_to_all | solution.py:127
  228.8 0.9 convolution_divide_fusion
  229.8 17.7 %all_to_all.66 = f32[8,128,128]{2,1,0:T(8,128)S(1)} all-to-all(f32[8,128,128]{2,1,0:T(8,128)S(1)} %copy.38), channel_id=1, replica_groups=mesh['clique'=8,'shard'=4] {'clique'}, dimensions={0} | all-to-all | bytes 1048576 | tf_op jit(solution)/shard_map/all_to_all | solution.py:134
  247.6 0.8 fusion.15
  248.5 0.9 slice_add_fusion.1
  249.3 3.5 %all-to-all-start.11 = ((f32[4,256,128]{2,1,0:T(8,128)}), f32[4,256,128]{2,1,0:T(8,128)S(1)}, u32[]{:S(2)}, u32[]{:S(2)}) async-start(f32[4,256,128]{2,1,0:T(8,128)} %bitcast.55), calls=%async_computation.11 | async-start | bytes 1048576 | tf_op jit(solution)/shard_map/all_to_all | solution.py:116
  252.8 1.3 fusion.5
  254.2 6.6 %all-to-all-done.11 = f32[4,256,128]{2,1,0:T(8,128)S(1)} async-done(((f32[4,256,128]{2,1,0:T(8,128)}), f32[4,256,128]{2,1,0:T(8,128)S(1)}, u32[]{:S(2)}, u32[]{:S(2)}) %all-to-all-start.11) | async-done | bytes 524320 | tf_op jit(solution)/shard_map/all_to_all | solution.py:116
  260.9 1.3 fusion.6
  262.2 1.9 reduce-precision_convert_fusion
  264.2 2.9 %fusion = f32[1024,256]{1,0:T(8,128)S(1)} fusion(s32[1024]{0:T(1024)S(1)} %bitcast.173, bf16[4096,128]{1,0:T(8,128)(2,1)S(1)} %get-tuple-element.14, bf16[4096,128]{1,0:T(8,128)(2,1)S(1)} %get-tuple-element.13), kind=kOutput, calls=%fused_computation.1 | convolution fusion | flops 2155872256 | bytes 3149824 | tf_op jit(solution)/shard_map/dot_general | solution.py:16
  267.0 1.1 fusion.64
  268.2 1.2 maximum_bitcast_fusion
  (80 shorter events, 18.1 us)
Async XLA Ops:
  6.5 1.9 copy-start
  41.9 5.9 %copy-start.1 = (s32[2,8]{1,0:T(2,128)S(1)}, s32[2,8]{1,0:T(2,128)}, u32[]{:S(2)}) copy-start(s32[2,8]{1,0:T(2,128)} %param.7) | copy-start | bytes 196
  42.9 31.4 %all-to-all-start.1 = ((f32[8,256,128]{2,1,0:T(8,128)}), f32[8,256,128]{2,1,0:T(8,128)S(1)}, u32[]{:S(2)}, u32[]{:S(2)}) async-start(f32[8,256,128]{2,1,0:T(8,128)} %pad_maximum_fusion.2), calls=%async_computation.1 | async-start | bytes 2097152 | tf_op jit(solution)/shard_map/all_to_all | solution.py:127
  76.1 18.8 %all-to-all-start.2 = ((f32[8,128,128]{2,1,0:T(8,128)}), f32[8,128,128]{2,1,0:T(8,128)S(1)}, u32[]{:S(2)}, u32[]{:S(2)}) async-start(f32[8,128,128]{2,1,0:T(8,128)} %copy.30), calls=%async_computation.2 | async-start | bytes 1048576 | tf_op jit(solution)/shard_map/all_to_all | solution.py:134
  96.9 11.4 %all-to-all-start.3 = ((f32[4,256,128]{1,2,0:T(8,128)}), f32[4,256,128]{1,2,0:T(8,128)S(1)}, u32[]{:S(2)}, u32[]{:S(2)}) async-start(f32[4,256,128]{1,2,0:T(8,128)} %copy.31), calls=%async_computation.3 | async-start | bytes 1048576 | tf_op jit(solution)/shard_map/all_to_all | solution.py:116
  108.3 1.6 copy-start.2
  192.2 1.6 copy-start.3
  210.0 18.8 %all-to-all-start.9 = ((f32[8,128,128]{2,1,0:T(8,128)}), f32[8,128,128]{2,1,0:T(8,128)S(1)}, u32[]{:S(2)}, u32[]{:S(2)}) async-start(f32[8,128,128]{2,1,0:T(8,128)} %bitcast.53), calls=%async_computation.9 | async-start | bytes 1048576 | tf_op jit(solution)/shard_map/all_to_all | solution.py:127
  213.5 48.7 %all-gather.2.cloned.1.call-start = ((), (), s32[]{:S(2)}) async-start(), calls=%async_computation.12 | async-start | bytes 2621440 | tf_op jit(solution)/shard_map/all_gather | solution.py:171
  249.3 11.4 %all-to-all-start.11 = ((f32[4,256,128]{2,1,0:T(8,128)}), f32[4,256,128]{2,1,0:T(8,128)S(1)}, u32[]{:S(2)}, u32[]{:S(2)}) async-start(f32[4,256,128]{2,1,0:T(8,128)} %bitcast.55), calls=%async_computation.11 | async-start | bytes 1048576 | tf_op jit(solution)/shard_map/all_to_all | solution.py:116
Sparse Core Ops, SparseCore 0:
  216.2 34.7 all-gather.1

commit v10 on v8

--- a/solution.py
+++ b/solution.py
@@ -66,9 +66,10 @@
         for which in range(4)
     ]
     halves = jnp.stack([slot // 32, slot % 32], axis=2).astype(jnp.bfloat16)
-    sent_halves = jnp.einsum(
-        "lib,lbh->lih", jnp.stack(sorting), halves, preferred_element_type=jnp.float32
-    )
+    placed = (
+        position[:, :, None] == jnp.arange(block_count, dtype=jnp.int32)[None, None, :]
+    ).astype(jnp.bfloat16)
+    sent_halves = jnp.einsum("lbi,lbh->lih", placed, halves, preferred_element_type=jnp.float32)
     sent_slots = (sent_halves[:, :, 0] * 32 + sent_halves[:, :, 1]).astype(jnp.int32)
     down1_to_up0 = lax.dot_general(
         sorting[1], sorting[3], (((1,), (1,)), ((), ())), preferred_element_type=jnp.float32

time: 267 us -> 264 us (0.989)
  other arithmetic: 19.5 us -> 16.3 us
    eq x4 -> x0, other arithmetic: 3.23 us -> none  [shards(): jnp.arange(block_count, dtype=jnp.int32)[:, None]]
where the time goes in v10:
time: 264 us; the launch traced here: 263 us
  blocking collectives  125 us (47%)
  waiting for transfers between devices  61 us (23%)
  matrix products  29.8 us (11%)
  starting transfers between devices  19 us (7%)
  other arithmetic  16.3 us (6%)
  local copies, waits for them, and re-layouts  9.03 us (3%)
  between operations  3.43 us (1%)
    all_to_all x3, blocking collectives, send(): lax.all_to_all(jnp.concatenate(chunks, axis=1), 'shard', 0, 0, tiled=True)  41 us
    all_to_all x2, blocking collectives, to_middle(): lax.all_to_all(jnp.concatenate(pieces, axis=1), 'clique', 0, 0, tiled=True)  36.6 us
    all_to_all x1, blocking collectives, from_middle(): lax.all_to_all(jnp.concatenate(chunks, axis=1), 'clique', 0, 0, tiled=True)  29.7 us
    all_to_all x1, waiting for transfers between devices, to_middle(): lax.all_to_all(jnp.concatenate(pieces, axis=1), 'clique', 0, 0, tiled=True)  26.5 us
    all_to_all x2, waiting for transfers between devices, from_middle(): lax.all_to_all(jnp.concatenate(chunks, axis=1), 'clique', 0, 0, tiled=True)  23.8 us
    dot_general x16, matrix products, split_dot(): lax.dot_general(one_hot, parts, (((contract,), (0,)), ((), ())), preferre...  18.4 us
    all_to_all x1, blocking collectives, fetch(): lax.all_to_all(jnp.concatenate(chunks, axis=1), 'shard', 0, 0, tiled=True)  17.4 us
    all_to_all x2, waiting for transfers between devices, fetch(): lax.all_to_all(jnp.concatenate(chunks, axis=1), 'shard', 0, 0, tiled=True)  10.7 us
  transfers between devices with their start and end apart: 5, of which 5 were waited for; matrix products, arithmetic and copies ran while one was open for 4% of the time, Pallas kernels for 0%

profile of v10, /device:TPU:0, one launch (start us, length us, event | category | flops | bytes accessed | tf_op | source)
XLA Modules:
  0.0 263.2 jit_solution(9774786126765961025)
XLA Ops:
  1.9 3.3 %fusion = f32[4,1024,2]{1,2,0:T(2,128)S(1)} fusion(s32[4,1024]{1,0:T(4,128)S(1)} %add_add_fusion, bf16[4,1024,1]{1,2,0:T(2,128)(2,1)S(1)} %fusion.120, bf16[4,1024,1]{1,2,0:T(2,128)(2,1)S(1)} %get-tuple-element.11), kind=kOutput, calls=%fused_computation.1 | convolution fusion | flops 21004288 | bytes 65536 | tf_op jit(solution)/shard_map/lbi,lbh->lih/dot_general | solution.py:72
  5.3 0.9 reduce-precision_convert_fusion.10
  7.1 0.8 fusion.6
  9.5 19.8 %all_to_all.60 = f32[4,528,128]{2,1,0:T(8,128)S(1)} all-to-all(f32[4,528,128]{2,1,0:T(8,128)S(1)} %pad_maximum_fusion), channel_id=1, replica_groups=mesh['clique'=8,'shard'=4] {'shard'}, dimensions={0} | all-to-all | bytes 2162688 | tf_op jit(solution)/shard_map/all_to_all | solution.py:93
  29.4 0.9 reduce-precision_convert_fusion.12
  30.3 0.8 fusion.12
  32.6 1.8 fusion.11
  34.5 1.0 pad_maximum_fusion.2
  35.5 4.9 %all-to-all-start.1 = ((f32[8,256,128]{2,1,0:T(8,128)}), f32[8,256,128]{2,1,0:T(8,128)S(1)}, u32[]{:S(2)}, u32[]{:S(2)}) async-start(f32[8,256,128]{2,1,0:T(8,128)} %pad_maximum_fusion.2), calls=%async_computation.1 | async-start | bytes 2097152 | tf_op jit(solution)/shard_map/all_to_all | solution.py:128
  40.4 26.5 %all-to-all-done.1 = f32[8,256,128]{2,1,0:T(8,128)S(1)} async-done(((f32[8,256,128]{2,1,0:T(8,128)}), f32[8,256,128]{2,1,0:T(8,128)S(1)}, u32[]{:S(2)}, u32[]{:S(2)}) %all-to-all-start.1) | async-done | bytes 1048608 | tf_op jit(solution)/shard_map/all_to_all | solution.py:128
  67.1 0.8 copy-done.1
  68.6 0.9 copy.30
  69.5 3.5 %all-to-all-start.2 = ((f32[8,128,128]{2,1,0:T(8,128)}), f32[8,128,128]{2,1,0:T(8,128)S(1)}, u32[]{:S(2)}, u32[]{:S(2)}) async-start(f32[8,128,128]{2,1,0:T(8,128)} %copy.30), calls=%async_computation.2 | async-start | bytes 1048576 | tf_op jit(solution)/shard_map/all_to_all | solution.py:135
  73.0 2.0 fusion.2
  75.1 13.2 %all-to-all-done.2 = f32[8,128,128]{2,1,0:T(8,128)S(1)} async-done(((f32[8,128,128]{2,1,0:T(8,128)}), f32[8,128,128]{2,1,0:T(8,128)S(1)}, u32[]{:S(2)}, u32[]{:S(2)}) %all-to-all-start.2) | async-done | bytes 524320 | tf_op jit(solution)/shard_map/all_to_all | solution.py:135
  88.4 0.8 fusion.14
  89.3 1.0 copy.31
  90.3 3.6 %all-to-all-start.3 = ((f32[4,256,128]{1,2,0:T(8,128)}), f32[4,256,128]{1,2,0:T(8,128)S(1)}, u32[]{:S(2)}, u32[]{:S(2)}) async-start(f32[4,256,128]{1,2,0:T(8,128)} %copy.31), calls=%async_computation.3 | async-start | bytes 1048576 | tf_op jit(solution)/shard_map/all_to_all | solution.py:117
  93.9 3.8 %fusion.36 = bf16[1024,1024]{1,0:T(8,128)(2,1)} fusion(s32[1024]{0:T(1024)S(1)} %bitcast.188, s32[1024]{0:T(1024)S(1)} %bitcast.177), kind=kOutput, calls=%fused_computation.49 | convolution fusion | flops 2150629376 | bytes 2105344 | tf_op jit(solution)/shard_map/dot_general | solution.py:74
  97.7 4.0 %all-to-all-done.3 = f32[4,256,128]{1,2,0:T(8,128)S(1)} async-done(((f32[4,256,128]{1,2,0:T(8,128)}), f32[4,256,128]{1,2,0:T(8,128)S(1)}, u32[]{:S(2)}, u32[]{:S(2)}) %all-to-all-start.3) | async-done | bytes 524320 | tf_op jit(solution)/shard_map/all_to_all | solution.py:117
  101.8 1.5 reduce-precision_convert_fusion.8
  105.8 10.6 %all_to_all.61 = f32[4,264,128]{2,1,0:T(8,128)S(1)} all-to-all(f32[4,264,128]{2,1,0:T(8,128)S(1)} %concatenate.139), channel_id=1, replica_groups=mesh['clique'=8,'shard'=4] {'shard'}, dimensions={0} | all-to-all | bytes 1081344 | tf_op jit(solution)/shard_map/all_to_all | solution.py:93
  117.8 0.8 fusion.13
  118.7 18.7 %all_to_all.62 = f32[8,128,128]{2,1,0:T(8,128)S(1)} all-to-all(f32[8,128,128]{2,1,0:T(8,128)S(1)} %bitcast.167), channel_id=1, replica_groups=mesh['clique'=8,'shard'=4] {'clique'}, dimensions={0} | all-to-all | bytes 1048576 | tf_op jit(solution)/shard_map/all_to_all | solution.py:128
  137.4 1.1 fusion.117
  138.7 0.9 convolution_divide_fusion.1
  140.0 29.7 %all_to_all.63 = f32[8,264,128]{2,1,0:T(8,128)S(1)} all-to-all(f32[8,264,128]{2,1,0:T(8,128)S(1)} %copy.36), channel_id=1, replica_groups=mesh['clique'=8,'shard'=4] {'clique'}, dimensions={0} | all-to-all | bytes 2162688 | tf_op jit(solution)/shard_map/all_to_all | solution.py:135
  171.1 0.8 fusion.10
  172.1 0.8 fusion.15
  173.1 17.4 %all_to_all.64 = f32[4,520,128]{2,1,0:T(8,128)S(1)} all-to-all(f32[4,520,128]{2,1,0:T(8,128)S(1)} %maximum_maximum_fusion), channel_id=1, replica_groups=mesh['clique'=8,'shard'=4] {'shard'}, dimensions={0} | all-to-all | bytes 2129920 | tf_op jit(solution)/shard_map/all_to_all | solution.py:117
  191.9 0.9 fusion.164
  192.8 0.8 copy-done.8
  195.8 10.7 %all_to_all.65 = f32[4,264,128]{2,1,0:T(8,128)S(1)} all-to-all(f32[4,264,128]{2,1,0:T(8,128)S(1)} %concatenate.147), channel_id=1, replica_groups=mesh['clique'=8,'shard'=4] {'shard'}, dimensions={0} | all-to-all | bytes 1081344 | tf_op jit(solution)/shard_map/all_to_all | solution.py:93
  208.0 0.8 fusion.17
  208.8 17.9 %all_to_all.66 = f32[8,128,128]{2,1,0:T(8,128)S(1)} all-to-all(f32[8,128,128]{2,1,0:T(8,128)S(1)} %bitcast.168), channel_id=1, replica_groups=mesh['clique'=8,'shard'=4] {'clique'}, dimensions={0} | all-to-all | bytes 1048576 | tf_op jit(solution)/shard_map/all_to_all | solution.py:128
  226.7 0.9 convolution_divide_fusion
  227.6 0.9 copy.38
  228.5 3.5 %all-to-all-start.10 = ((f32[8,128,128]{2,1,0:T(8,128)}), f32[8,128,128]{2,1,0:T(8,128)S(1)}, u32[]{:S(2)}, u32[]{:S(2)}) async-start(f32[8,128,128]{2,1,0:T(8,128)} %copy.38), calls=%async_computation.10 | async-start | bytes 1048576 | tf_op jit(solution)/shard_map/all_to_all | solution.py:135
  232.0 2.3 fusion.4
  234.5 2.2 fusion.7
  236.7 10.6 %all-to-all-done.10 = f32[8,128,128]{2,1,0:T(8,128)S(1)} async-done(((f32[8,128,128]{2,1,0:T(8,128)}), f32[8,128,128]{2,1,0:T(8,128)S(1)}, u32[]{:S(2)}, u32[]{:S(2)}) %all-to-all-start.10) | async-done | bytes 524320 | tf_op jit(solution)/shard_map/all_to_all | solution.py:135
  247.4 0.8 fusion.16
  248.2 0.9 slice_add_fusion.1
  249.1 3.5 %all-to-all-start.11 = ((f32[4,256,128]{2,1,0:T(8,128)}), f32[4,256,128]{2,1,0:T(8,128)S(1)}, u32[]{:S(2)}, u32[]{:S(2)}) async-start(f32[4,256,128]{2,1,0:T(8,128)} %bitcast.56), calls=%async_computation.11 | async-start | bytes 1048576 | tf_op jit(solution)/shard_map/all_to_all | solution.py:117
  252.6 1.3 fusion.64
  253.9 6.7 %all-to-all-done.11 = f32[4,256,128]{2,1,0:T(8,128)S(1)} async-done(((f32[4,256,128]{2,1,0:T(8,128)}), f32[4,256,128]{2,1,0:T(8,128)S(1)}, u32[]{:S(2)}, u32[]{:S(2)}) %all-to-all-start.11) | async-done | bytes 524320 | tf_op jit(solution)/shard_map/all_to_all | solution.py:117
  260.6 1.3 fusion.5
  262.0 1.2 maximum_bitcast_fusion
  (88 shorter events, 16.1 us)
Async XLA Ops:
  1.9 3.4 %copy-start.3 = (f32[3,1,1024,128]{3,2,1,0:T(8,128)S(1)}, f32[3,1,1024,128]{3,2,1,0:T(8,128)}, u32[]{:S(2)}) copy-start(f32[3,1,1024,128]{3,2,1,0:T(8,128)} %param.4) | copy-start | bytes 4718596
  34.5 5.9 %copy-start.6 = (s32[2,8]{1,0:T(2,128)S(1)}, s32[2,8]{1,0:T(2,128)}, u32[]{:S(2)}) copy-start(s32[2,8]{1,0:T(2,128)} %param.7) | copy-start | bytes 196
  35.5 31.4 %all-to-all-start.1 = ((f32[8,256,128]{2,1,0:T(8,128)}), f32[8,256,128]{2,1,0:T(8,128)S(1)}, u32[]{:S(2)}, u32[]{:S(2)}) async-start(f32[8,256,128]{2,1,0:T(8,128)} %pad_maximum_fusion.2), calls=%async_computation.1 | async-start | bytes 2097152 | tf_op jit(solution)/shard_map/all_to_all | solution.py:128
  67.0 0.8 copy-start.1
  67.1 6.0 %copy-start.4 = (bf16[1024,128]{1,0:T(8,128)(2,1)S(1)}, bf16[1024,128]{1,0:T(8,128)(2,1)}, u32[]{:S(2)}) copy-start(bf16[1024,128]{1,0:T(8,128)(2,1)} %get-tuple-element.18) | copy-start | bytes 786436
  69.5 18.8 %all-to-all-start.2 = ((f32[8,128,128]{2,1,0:T(8,128)}), f32[8,128,128]{2,1,0:T(8,128)S(1)}, u32[]{:S(2)}, u32[]{:S(2)}) async-start(f32[8,128,128]{2,1,0:T(8,128)} %copy.30), calls=%async_computation.2 | async-start | bytes 1048576 | tf_op jit(solution)/shard_map/all_to_all | solution.py:135
  90.3 11.4 %all-to-all-start.3 = ((f32[4,256,128]{1,2,0:T(8,128)}), f32[4,256,128]{1,2,0:T(8,128)S(1)}, u32[]{:S(2)}, u32[]{:S(2)}) async-start(f32[4,256,128]{1,2,0:T(8,128)} %copy.31), calls=%async_computation.3 | async-start | bytes 1048576 | tf_op jit(solution)/shard_map/all_to_all | solution.py:117
  101.7 1.9 copy-start.7
  191.8 1.8 copy-start.8
  192.8 2.3 copy-start.5
  208.8 17.9 %copy-start.2 = (f32[8,128,128]{2,1,0:T(8,128)S(1)}, f32[8,128,128]{2,1,0:T(8,128)}, u32[]{:S(2)}) copy-start(f32[8,128,128]{2,1,0:T(8,128)} %copy-done.1) | copy-start | bytes 1572868
  228.5 18.8 %all-to-all-start.10 = ((f32[8,128,128]{2,1,0:T(8,128)}), f32[8,128,128]{2,1,0:T(8,128)S(1)}, u32[]{:S(2)}, u32[]{:S(2)}) async-start(f32[8,128,128]{2,1,0:T(8,128)} %copy.38), calls=%async_computation.10 | async-start | bytes 1048576 | tf_op jit(solution)/shard_map/all_to_all | solution.py:135
  232.0 2.3 copy-start
  249.1 11.4 %all-to-all-start.11 = ((f32[4,256,128]{2,1,0:T(8,128)}), f32[4,256,128]{2,1,0:T(8,128)S(1)}, u32[]{:S(2)}, u32[]{:S(2)}) async-start(f32[4,256,128]{2,1,0:T(8,128)} %bitcast.56), calls=%async_computation.11 | async-start | bytes 1048576 | tf_op jit(solution)/shard_map/all_to_all | solution.py:117

commit v11 on v10

--- a/solution.py
+++ b/solution.py
@@ -66,10 +66,15 @@
         for which in range(4)
     ]
     halves = jnp.stack([slot // 32, slot % 32], axis=2).astype(jnp.bfloat16)
-    placed = (
-        position[:, :, None] == jnp.arange(block_count, dtype=jnp.int32)[None, None, :]
-    ).astype(jnp.bfloat16)
-    sent_halves = jnp.einsum("lbi,lbh->lih", placed, halves, preferred_element_type=jnp.float32)
+    high = (
+        (position // 32)[:, None, :] == jnp.arange(block_count // 32, dtype=jnp.int32)[None, :, None]
+    ).astype(jnp.bfloat16)
+    low = (
+        (position % 32)[:, :, None] == jnp.arange(32, dtype=jnp.int32)[None, None, :]
+    ).astype(jnp.bfloat16)
+    spread = (low[:, :, :, None] * halves[:, :, None, :]).reshape(4, block_count, 64)
+    sent_halves = jnp.einsum("lkb,lbn->lkn", high, spread, preferred_element_type=jnp.float32)
+    sent_halves = sent_halves.reshape(4, block_count, 2)
     sent_slots = (sent_halves[:, :, 0] * 32 + sent_halves[:, :, 1]).astype(jnp.int32)
     down1_to_up0 = lax.dot_general(
         sorting[1], sorting[3], (((1,), (1,)), ((), ())), preferred_element_type=jnp.float32

time: 264 us -> 266 us (level)
  local copies, waits for them, and re-layouts: 9.03 us -> 13.5 us
  matrix products: 29.8 us -> 26.9 us
    dot_general x1, matrix products: 3.27 us -> 0.26 us  [shards(): jnp.einsum('lkb,lbn->lkn', high, spread, preferred_element_type=jnp.float32)]
where the time goes in v11:
time: 266 us; the launch traced here: 265 us
  blocking collectives  125 us (47%)
  waiting for transfers between devices  61 us (23%)
  matrix products  26.9 us (10%)
  starting transfers between devices  19 us (7%)
  other arithmetic  16.8 us (6%)
  local copies, waits for them, and re-layouts  13.5 us (5%)
  between operations  3.25 us (1%)
    all_to_all x3, blocking collectives, send(): lax.all_to_all(jnp.concatenate(chunks, axis=1), 'shard', 0, 0, tiled=True)  41 us
    all_to_all x2, blocking collectives, to_middle(): lax.all_to_all(jnp.concatenate(pieces, axis=1), 'clique', 0, 0, tiled=True)  36.7 us
    all_to_all x1, blocking collectives, from_middle(): lax.all_to_all(jnp.concatenate(chunks, axis=1), 'clique', 0, 0, tiled=True)  29.7 us
    all_to_all x1, waiting for transfers between devices, to_middle(): lax.all_to_all(jnp.concatenate(pieces, axis=1), 'clique', 0, 0, tiled=True)  26.5 us
    all_to_all x2, waiting for transfers between devices, from_middle(): lax.all_to_all(jnp.concatenate(chunks, axis=1), 'clique', 0, 0, tiled=True)  23.8 us
    dot_general x16, matrix products, split_dot(): lax.dot_general(one_hot, parts, (((contract,), (0,)), ((), ())), preferre...  18.4 us
    all_to_all x1, blocking collectives, fetch(): lax.all_to_all(jnp.concatenate(chunks, axis=1), 'shard', 0, 0, tiled=True)  17.4 us
    all_to_all x2, waiting for transfers between devices, fetch(): lax.all_to_all(jnp.concatenate(chunks, axis=1), 'shard', 0, 0, tiled=True)  10.7 us
  transfers between devices with their start and end apart: 5, of which 5 were waited for; matrix products, arithmetic and copies ran while one was open for 4% of the time, Pallas kernels for 0%

profile of v11, /device:TPU:0, one launch (start us, length us, event | category | flops | bytes accessed | tf_op | source)
XLA Modules:
  0.0 265.2 jit_solution(4522300180642299224)
XLA Ops:
  4.2 0.8 fusion.167
  5.7 2.3 reduce-precision_convert_fusion.10
  8.9 0.8 fusion.4
  11.2 19.7 %all_to_all.60 = f32[4,528,128]{2,1,0:T(8,128)S(1)} all-to-all(f32[4,528,128]{2,1,0:T(8,128)S(1)} %pad_maximum_fusion), channel_id=1, replica_groups=mesh['clique'=8,'shard'=4] {'shard'}, dimensions={0} | all-to-all | bytes 2162688 | tf_op jit(solution)/shard_map/all_to_all | solution.py:98
  31.1 0.9 reduce-precision_convert_fusion.12
  32.0 0.8 fusion.10
  34.1 1.8 fusion.9
  36.0 1.0 pad_maximum_fusion.2
  37.0 4.9 %all-to-all-start.1 = ((f32[8,256,128]{2,1,0:T(8,128)}), f32[8,256,128]{2,1,0:T(8,128)S(1)}, u32[]{:S(2)}, u32[]{:S(2)}) async-start(f32[8,256,128]{2,1,0:T(8,128)} %pad_maximum_fusion.2), calls=%async_computation.1 | async-start | bytes 2097152 | tf_op jit(solution)/shard_map/all_to_all | solution.py:133
  41.9 26.5 %all-to-all-done.1 = f32[8,256,128]{2,1,0:T(8,128)S(1)} async-done(((f32[8,256,128]{2,1,0:T(8,128)}), f32[8,256,128]{2,1,0:T(8,128)S(1)}, u32[]{:S(2)}, u32[]{:S(2)}) %all-to-all-start.1) | async-done | bytes 1048608 | tf_op jit(solution)/shard_map/all_to_all | solution.py:133
  68.5 0.9 fusion.166
  69.4 0.8 copy-done.1
  70.9 0.9 copy.65
  71.8 3.5 %all-to-all-start.2 = ((f32[8,128,128]{2,1,0:T(8,128)}), f32[8,128,128]{2,1,0:T(8,128)S(1)}, u32[]{:S(2)}, u32[]{:S(2)}) async-start(f32[8,128,128]{2,1,0:T(8,128)} %copy.65), calls=%async_computation.2 | async-start | bytes 1048576 | tf_op jit(solution)/shard_map/all_to_all | solution.py:140
  75.3 2.0 fusion
  77.3 13.2 %all-to-all-done.2 = f32[8,128,128]{2,1,0:T(8,128)S(1)} async-done(((f32[8,128,128]{2,1,0:T(8,128)}), f32[8,128,128]{2,1,0:T(8,128)S(1)}, u32[]{:S(2)}, u32[]{:S(2)}) %all-to-all-start.2) | async-done | bytes 524320 | tf_op jit(solution)/shard_map/all_to_all | solution.py:140
  90.7 0.8 fusion.12
  91.6 1.0 copy.66
  92.6 3.6 %all-to-all-start.3 = ((f32[4,256,128]{1,2,0:T(8,128)}), f32[4,256,128]{1,2,0:T(8,128)S(1)}, u32[]{:S(2)}, u32[]{:S(2)}) async-start(f32[4,256,128]{1,2,0:T(8,128)} %copy.66), calls=%async_computation.3 | async-start | bytes 1048576 | tf_op jit(solution)/shard_map/all_to_all | solution.py:122
  96.2 3.8 %fusion.34 = bf16[1024,1024]{1,0:T(8,128)(2,1)} fusion(s32[1024]{0:T(1024)S(1)} %bitcast.199, s32[1024]{0:T(1024)S(1)} %bitcast.188), kind=kOutput, calls=%fused_computation.46 | convolution fusion | flops 2150629376 | bytes 2105344 | tf_op jit(solution)/shard_map/dot_general | solution.py:79
  100.0 4.0 %all-to-all-done.3 = f32[4,256,128]{1,2,0:T(8,128)S(1)} async-done(((f32[4,256,128]{1,2,0:T(8,128)}), f32[4,256,128]{1,2,0:T(8,128)S(1)}, u32[]{:S(2)}, u32[]{:S(2)}) %all-to-all-start.3) | async-done | bytes 524320 | tf_op jit(solution)/shard_map/all_to_all | solution.py:122
  104.3 1.4 copy-done.6
  107.7 10.6 %all_to_all.61 = f32[4,264,128]{2,1,0:T(8,128)S(1)} all-to-all(f32[4,264,128]{2,1,0:T(8,128)S(1)} %concatenate.170), channel_id=1, replica_groups=mesh['clique'=8,'shard'=4] {'shard'}, dimensions={0} | all-to-all | bytes 1081344 | tf_op jit(solution)/shard_map/all_to_all | solution.py:98
  119.6 0.8 fusion.11
  120.5 18.8 %all_to_all.62 = f32[8,128,128]{2,1,0:T(8,128)S(1)} all-to-all(f32[8,128,128]{2,1,0:T(8,128)S(1)} %bitcast.177), channel_id=1, replica_groups=mesh['clique'=8,'shard'=4] {'clique'}, dimensions={0} | all-to-all | bytes 1048576 | tf_op jit(solution)/shard_map/all_to_all | solution.py:133
  139.3 1.1 fusion.118
  140.6 0.9 convolution_divide_fusion.1
  142.0 29.7 %all_to_all.63 = f32[8,264,128]{2,1,0:T(8,128)S(1)} all-to-all(f32[8,264,128]{2,1,0:T(8,128)S(1)} %copy.71), channel_id=1, replica_groups=mesh['clique'=8,'shard'=4] {'clique'}, dimensions={0} | all-to-all | bytes 2162688 | tf_op jit(solution)/shard_map/all_to_all | solution.py:140
  173.1 0.8 fusion.8
  174.1 0.8 fusion.13
  175.1 17.4 %all_to_all.64 = f32[4,520,128]{2,1,0:T(8,128)S(1)} all-to-all(f32[4,520,128]{2,1,0:T(8,128)S(1)} %maximum_maximum_fusion), channel_id=1, replica_groups=mesh['clique'=8,'shard'=4] {'shard'}, dimensions={0} | all-to-all | bytes 2129920 | tf_op jit(solution)/shard_map/all_to_all | solution.py:122
  193.8 0.9 fusion.165
  197.8 10.7 %all_to_all.65 = f32[4,264,128]{2,1,0:T(8,128)S(1)} all-to-all(f32[4,264,128]{2,1,0:T(8,128)S(1)} %concatenate.178), channel_id=1, replica_groups=mesh['clique'=8,'shard'=4] {'shard'}, dimensions={0} | all-to-all | bytes 1081344 | tf_op jit(solution)/shard_map/all_to_all | solution.py:98
  210.0 0.8 fusion.15
  210.8 17.9 %all_to_all.66 = f32[8,128,128]{2,1,0:T(8,128)S(1)} all-to-all(f32[8,128,128]{2,1,0:T(8,128)S(1)} %bitcast.178), channel_id=1, replica_groups=mesh['clique'=8,'shard'=4] {'clique'}, dimensions={0} | all-to-all | bytes 1048576 | tf_op jit(solution)/shard_map/all_to_all | solution.py:133
  228.7 0.9 convolution_divide_fusion
  229.6 0.9 copy.73
  230.5 3.5 %all-to-all-start.10 = ((f32[8,128,128]{2,1,0:T(8,128)}), f32[8,128,128]{2,1,0:T(8,128)S(1)}, u32[]{:S(2)}, u32[]{:S(2)}) async-start(f32[8,128,128]{2,1,0:T(8,128)} %copy.73), calls=%async_computation.10 | async-start | bytes 1048576 | tf_op jit(solution)/shard_map/all_to_all | solution.py:140
  234.0 2.3 fusion.2
  236.4 2.2 fusion.5
  238.7 10.6 %all-to-all-done.10 = f32[8,128,128]{2,1,0:T(8,128)S(1)} async-done(((f32[8,128,128]{2,1,0:T(8,128)}), f32[8,128,128]{2,1,0:T(8,128)S(1)}, u32[]{:S(2)}, u32[]{:S(2)}) %all-to-all-start.10) | async-done | bytes 524320 | tf_op jit(solution)/shard_map/all_to_all | solution.py:140
  249.4 0.8 fusion.14
  250.2 0.8 slice_add_fusion.1
  251.1 3.5 %all-to-all-start.11 = ((f32[4,256,128]{2,1,0:T(8,128)}), f32[4,256,128]{2,1,0:T(8,128)S(1)}, u32[]{:S(2)}, u32[]{:S(2)}) async-start(f32[4,256,128]{2,1,0:T(8,128)} %bitcast.57), calls=%async_computation.11 | async-start | bytes 1048576 | tf_op jit(solution)/shard_map/all_to_all | solution.py:122
  254.6 1.3 fusion.62
  255.8 6.7 %all-to-all-done.11 = f32[4,256,128]{2,1,0:T(8,128)S(1)} async-done(((f32[4,256,128]{2,1,0:T(8,128)}), f32[4,256,128]{2,1,0:T(8,128)S(1)}, u32[]{:S(2)}, u32[]{:S(2)}) %all-to-all-start.11) | async-done | bytes 524320 | tf_op jit(solution)/shard_map/all_to_all | solution.py:122
  262.6 1.3 fusion.3
  263.9 1.2 maximum_bitcast_fusion
  (95 shorter events, 19.2 us)
Async XLA Ops:
  36.0 5.9 %copy-start.5 = (s32[2,8]{1,0:T(2,128)S(1)}, s32[2,8]{1,0:T(2,128)}, u32[]{:S(2)}) copy-start(s32[2,8]{1,0:T(2,128)} %param.7) | copy-start | bytes 196
  37.0 31.4 %all-to-all-start.1 = ((f32[8,256,128]{2,1,0:T(8,128)}), f32[8,256,128]{2,1,0:T(8,128)S(1)}, u32[]{:S(2)}, u32[]{:S(2)}) async-start(f32[8,256,128]{2,1,0:T(8,128)} %pad_maximum_fusion.2), calls=%async_computation.1 | async-start | bytes 2097152 | tf_op jit(solution)/shard_map/all_to_all | solution.py:133
  69.4 0.8 copy-start.1
  71.8 18.8 %all-to-all-start.2 = ((f32[8,128,128]{2,1,0:T(8,128)}), f32[8,128,128]{2,1,0:T(8,128)S(1)}, u32[]{:S(2)}, u32[]{:S(2)}) async-start(f32[8,128,128]{2,1,0:T(8,128)} %copy.65), calls=%async_computation.2 | async-start | bytes 1048576 | tf_op jit(solution)/shard_map/all_to_all | solution.py:140
  92.6 11.4 %all-to-all-start.3 = ((f32[4,256,128]{1,2,0:T(8,128)}), f32[4,256,128]{1,2,0:T(8,128)S(1)}, u32[]{:S(2)}, u32[]{:S(2)}) async-start(f32[4,256,128]{1,2,0:T(8,128)} %copy.66), calls=%async_computation.3 | async-start | bytes 1048576 | tf_op jit(solution)/shard_map/all_to_all | solution.py:122
  104.0 1.6 copy-start.6
  120.4 18.9 %copy-start.3 = (f32[8,128,128]{2,1,0:T(8,128)S(1)}, f32[8,128,128]{2,1,0:T(8,128)}, u32[]{:S(2)}) copy-start(f32[8,128,128]{2,1,0:T(8,128)} %get-tuple-element.35) | copy-start | bytes 1572868
  193.8 1.8 copy-start.7
  194.8 1.5 copy-start.4
  210.8 17.9 %copy-start.2 = (f32[8,128,128]{2,1,0:T(8,128)S(1)}, f32[8,128,128]{2,1,0:T(8,128)}, u32[]{:S(2)}) copy-start(f32[8,128,128]{2,1,0:T(8,128)} %copy-done.1) | copy-start | bytes 1572868
  230.5 18.8 %all-to-all-start.10 = ((f32[8,128,128]{2,1,0:T(8,128)}), f32[8,128,128]{2,1,0:T(8,128)S(1)}, u32[]{:S(2)}, u32[]{:S(2)}) async-start(f32[8,128,128]{2,1,0:T(8,128)} %copy.73), calls=%async_computation.10 | async-start | bytes 1048576 | tf_op jit(solution)/shard_map/all_to_all | solution.py:140
  234.0 2.3 copy-start
  251.1 11.4 %all-to-all-start.11 = ((f32[4,256,128]{2,1,0:T(8,128)}), f32[4,256,128]{2,1,0:T(8,128)S(1)}, u32[]{:S(2)}, u32[]{:S(2)}) async-start(f32[4,256,128]{2,1,0:T(8,128)} %bitcast.57), calls=%async_computation.11 | async-start | bytes 1048576 | tf_op jit(solution)/shard_map/all_to_all | solution.py:122

commit v12 on v10

--- a/solution.py
+++ b/solution.py
@@ -106,8 +106,8 @@
             )
         return messages, total
 
-    def fetch(items, partial=None):
-        chunks = []
+    def fetch(items, partial=None, extra=None):
+        chunks = [] if extra is None else [extra.reshape(shard_count, per_peer, lane_count)]
         for owned_rows, which in items:
             owned_rows = jnp.where(jnp.isfinite(owned_rows), owned_rows, 0.0)
             picked = gather_rows(owned_rows, arrived[which])
@@ -115,13 +115,14 @@
         if partial is not None:
             chunks.append(jnp.broadcast_to(partial, (shard_count, PAD, lane_count)))
         back = lax.all_to_all(jnp.concatenate(chunks, axis=1), "shard", 0, 0, tiled=True)
+        count = len(items) + (extra is not None)
         rows = [
             back[:, number * per_peer : (number + 1) * per_peer].reshape(block_count, lane_count)
-            for number in range(len(items))
+            for number in range(count)
         ]
         if partial is None:
             return rows, None
-        return rows, jnp.sum(back[:, len(items) * per_peer, 0])
+        return rows, jnp.sum(back[:, count * per_peer, 0])
 
     def to_middle(arrays):
         pieces = [a.reshape(clique_count, piece_rows, lane_count) for a in arrays]
@@ -151,17 +152,18 @@
     t0, t1, t2 = tables[0, 0], tables[1, 0], tables[2, 0]
 
     t2_up1 = split_dot(sorting[0], t2)
+    (message,), total = send([(t2_up1, 0)], with_slots=True)
+    scaled1 = message * (sep_states / total)
+    (scaled1_mid,) = to_middle([scaled1])
+    (incoming1,), _ = from_middle([jnp.exp(mix(sel[1].T, jnp.log(scaled1_mid)))])
     t0_down0 = split_dot(sorting[2], t0)
-    (message, down0_message), total = send([(t2_up1, 0), (t0_down0, 2)], with_slots=True)
-    scaled1 = message * (sep_states / total)
-    scaled1_mid, down0_mid = to_middle([scaled1, down0_message])
-    (incoming1,), _ = from_middle([jnp.exp(mix(sel[1].T, jnp.log(scaled1_mid)))])
-    (picked,), _ = fetch([(incoming1, 3)])
+    (level0_rows, picked), _ = fetch([(incoming1, 3)], extra=t0_down0)
+    down0_message = segment_rows(level0_rows, arrived[2], per_owner)
     t1_down1 = split_dot(sorting[3], t1) * picked
     t1_up0 = split_dot(down1_to_up0, t1_down1)
     (message,), total = send([(t1_up0, 1)])
     scaled0 = message * (sep_states / total)
-    (scaled0_mid,) = to_middle([scaled0])
+    scaled0_mid, down0_mid = to_middle([scaled0, down0_message])
     incoming0_mid = jnp.exp(mix(sel[0].T, jnp.log(scaled0_mid)))
     incoming0_mid = jnp.where(jnp.isfinite(incoming0_mid), incoming0_mid, 0.0)
     fresh0_mid = down0_mid * incoming0_mid

time: 264 us -> 262 us (level)
  blocking collectives: 125 us -> 119 us
  starting transfers between devices: 19 us -> 22.5 us
    all_to_all x3 -> x2, blocking collectives: 41 us -> 24.8 us  [send(): lax.all_to_all(jnp.concatenate(chunks, axis=1), 'shard', 0, 0, tiled=True)]
    all_to_all x1, waiting for transfers between devices: 26.5 us -> 15.3 us  [to_middle(): lax.all_to_all(jnp.concatenate(pieces, axis=1), 'clique', 0, 0, tiled=True)]
    all_to_all x2, blocking collectives: 36.6 us -> 47.4 us  [to_middle(): lax.all_to_all(jnp.concatenate(pieces, axis=1), 'clique', 0, 0, tiled=True)]
    all_to_all x0 -> x1, waiting for transfers between devices: none -> 6.82 us  [send(): lax.all_to_all(jnp.concatenate(chunks, axis=1), 'shard', 0, 0, tiled=True)]
    all_to_all x2, waiting for transfers between devices: 10.7 us -> 14.3 us  [fetch(): lax.all_to_all(jnp.concatenate(chunks, axis=1), 'shard', 0, 0, tiled=True)]
    all_to_all x0 -> x1, starting transfers between devices: none -> 3.47 us  [send(): lax.all_to_all(jnp.concatenate(chunks, axis=1), 'shard', 0, 0, tiled=True)]
  transfers between devices with their start and end apart: 5 -> 6, of which waited for: 5 -> 6; matrix products, arithmetic and copies ran while one was open for 4% -> 5% of each run, Pallas kernels for 0% -> 0%
where the time goes in v12:
time: 262 us; the launch traced here: 261 us
  blocking collectives  119 us (45%)
  waiting for transfers between devices  61.4 us (23%)
  matrix products  28.8 us (11%)
  starting transfers between devices  22.5 us (9%)
  other arithmetic  15.5 us (6%)
  local copies, waits for them, and re-layouts  9.93 us (4%)
  between operations  3.35 us (1%)
    all_to_all x2, blocking collectives, to_middle(): lax.all_to_all(jnp.concatenate(pieces, axis=1), 'clique', 0, 0, tiled=True)  47.4 us
    all_to_all x1, blocking collectives, from_middle(): lax.all_to_all(jnp.concatenate(chunks, axis=1), 'clique', 0, 0, tiled=True)  29.7 us
    all_to_all x2, waiting for transfers between devices, from_middle(): lax.all_to_all(jnp.concatenate(chunks, axis=1), 'clique', 0, 0, tiled=True)  25 us
    all_to_all x2, blocking collectives, send(): lax.all_to_all(jnp.concatenate(chunks, axis=1), 'shard', 0, 0, tiled=True)  24.8 us
    all_to_all x1, blocking collectives, fetch(): lax.all_to_all(jnp.concatenate(chunks, axis=1), 'shard', 0, 0, tiled=True)  17.4 us
    dot_general x16, matrix products, split_dot(): lax.dot_general(one_hot, parts, (((contract,), (0,)), ((), ())), preferre...  17.3 us
    all_to_all x1, waiting for transfers between devices, to_middle(): lax.all_to_all(jnp.concatenate(pieces, axis=1), 'clique', 0, 0, tiled=True)  15.3 us
    all_to_all x2, waiting for transfers between devices, fetch(): lax.all_to_all(jnp.concatenate(chunks, axis=1), 'shard', 0, 0, tiled=True)  14.3 us
  transfers between devices with their start and end apart: 6, of which 6 were waited for; matrix products, arithmetic and copies ran while one was open for 5% of the time, Pallas kernels for 0%

profile of v12, /device:TPU:0, one launch (start us, length us, event | category | flops | bytes accessed | tf_op | source)
XLA Modules:
  0.0 260.7 jit_solution(16820681378481488872)
XLA Ops:
  1.9 3.3 %fusion = f32[4,1024,2]{1,2,0:T(2,128)S(1)} fusion(s32[4,1024]{1,0:T(4,128)S(1)} %add_add_fusion, bf16[4,1024,1]{1,2,0:T(2,128)(2,1)S(1)} %fusion.120, bf16[4,1024,1]{1,2,0:T(2,128)(2,1)S(1)} %get-tuple-element.11), kind=kOutput, calls=%fused_computation.1 | convolution fusion | flops 21004288 | bytes 65536 | tf_op jit(solution)/shard_map/lbi,lbh->lih/dot_general | solution.py:72
  5.6 0.8 fusion.6
  7.9 14.1 %all_to_all.60 = f32[4,272,128]{2,1,0:T(8,128)S(1)} all-to-all(f32[4,272,128]{2,1,0:T(8,128)S(1)} %pad_maximum_fusion.3), channel_id=1, replica_groups=mesh['clique'=8,'shard'=4] {'shard'}, dimensions={0} | all-to-all | bytes 1114112 | tf_op jit(solution)/shard_map/all_to_all | solution.py:93
  23.5 0.8 fusion.13
  24.3 0.9 fusion.66
  25.2 4.9 %all-to-all-start.1 = ((f32[8,128,128]{2,1,0:T(8,128)}), f32[8,128,128]{2,1,0:T(8,128)S(1)}, u32[]{:S(2)}, u32[]{:S(2)}) async-start(f32[8,128,128]{2,1,0:T(8,128)} %bitcast.32), calls=%async_computation.1 | async-start | bytes 1048576 | tf_op jit(solution)/shard_map/all_to_all | solution.py:129
  30.1 15.3 %all-to-all-done.1 = f32[8,128,128]{2,1,0:T(8,128)S(1)} async-done(((f32[8,128,128]{2,1,0:T(8,128)}), f32[8,128,128]{2,1,0:T(8,128)S(1)}, u32[]{:S(2)}, u32[]{:S(2)}) %all-to-all-start.1) | async-done | bytes 524320 | tf_op jit(solution)/shard_map/all_to_all | solution.py:129
  46.1 0.9 copy.30
  47.0 3.5 %all-to-all-start.2 = ((f32[8,128,128]{2,1,0:T(8,128)}), f32[8,128,128]{2,1,0:T(8,128)S(1)}, u32[]{:S(2)}, u32[]{:S(2)}) async-start(f32[8,128,128]{2,1,0:T(8,128)} %copy.30), calls=%async_computation.2 | async-start | bytes 1048576 | tf_op jit(solution)/shard_map/all_to_all | solution.py:136
  51.4 14.4 %all-to-all-done.2 = f32[8,128,128]{2,1,0:T(8,128)S(1)} async-done(((f32[8,128,128]{2,1,0:T(8,128)}), f32[8,128,128]{2,1,0:T(8,128)S(1)}, u32[]{:S(2)}, u32[]{:S(2)}) %all-to-all-start.2) | async-done | bytes 524320 | tf_op jit(solution)/shard_map/all_to_all | solution.py:136
  65.9 0.8 fusion.12
  66.8 1.0 pad_maximum_fusion.1
  67.8 3.7 %all-to-all-start.3 = ((f32[4,512,128]{2,1,0:T(8,128)}), f32[4,512,128]{2,1,0:T(8,128)S(1)}, u32[]{:S(2)}, u32[]{:S(2)}) async-start(f32[4,512,128]{2,1,0:T(8,128)} %pad_maximum_fusion.1), calls=%async_computation.3 | async-start | bytes 2097152 | tf_op jit(solution)/shard_map/all_to_all | solution.py:117
  71.5 2.0 fusion.2
  73.6 3.7 %fusion.36 = bf16[1024,1024]{1,0:T(8,128)(2,1)} fusion(s32[1024]{0:T(1024)S(1)} %bitcast.185, s32[1024]{0:T(1024)S(1)} %bitcast.174), kind=kOutput, calls=%fused_computation.49 | convolution fusion | flops 2150629376 | bytes 2105344 | tf_op jit(solution)/shard_map/dot_general | solution.py:74
  77.3 7.6 %all-to-all-done.3 = f32[4,512,128]{2,1,0:T(8,128)S(1)} async-done(((f32[4,512,128]{2,1,0:T(8,128)}), f32[4,512,128]{2,1,0:T(8,128)S(1)}, u32[]{:S(2)}, u32[]{:S(2)}) %all-to-all-start.3) | async-done | bytes 1048608 | tf_op jit(solution)/shard_map/all_to_all | solution.py:117
  84.9 0.9 fusion.165
  85.8 1.2 copy.43
  87.1 1.5 reduce-precision_convert_fusion.9
  90.5 1.5 concatenate.141
  91.9 3.5 %all-to-all-start.4 = ((f32[4,264,128]{2,1,0:T(8,128)}), f32[4,264,128]{2,1,0:T(8,128)S(1)}, u32[]{:S(2)}, u32[]{:S(2)}) async-start(f32[4,264,128]{2,1,0:T(8,128)} %concatenate.141), calls=%async_computation.4 | async-start | bytes 1081344 | tf_op jit(solution)/shard_map/all_to_all | solution.py:93
  96.3 6.8 %all-to-all-done.4 = f32[4,264,128]{2,1,0:T(8,128)S(1)} async-done(((f32[4,264,128]{2,1,0:T(8,128)}), f32[4,264,128]{2,1,0:T(8,128)S(1)}, u32[]{:S(2)}, u32[]{:S(2)}) %all-to-all-start.4) | async-done | bytes 540704 | tf_op jit(solution)/shard_map/all_to_all | solution.py:93
  104.5 0.8 fusion.11
  105.4 29.6 %all_to_all.61 = f32[8,256,128]{2,1,0:T(8,128)S(1)} all-to-all(f32[8,256,128]{2,1,0:T(8,128)S(1)} %pad_maximum_fusion.2), channel_id=1, replica_groups=mesh['clique'=8,'shard'=4] {'clique'}, dimensions={0} | all-to-all | bytes 2097152 | tf_op jit(solution)/shard_map/all_to_all | solution.py:129
  135.1 1.1 fusion.117
  136.2 0.9 convolution_divide_fusion.1
  137.7 29.7 %all_to_all.62 = f32[8,264,128]{2,1,0:T(8,128)S(1)} all-to-all(f32[8,264,128]{2,1,0:T(8,128)S(1)} %copy.35), channel_id=1, replica_groups=mesh['clique'=8,'shard'=4] {'clique'}, dimensions={0} | all-to-all | bytes 2162688 | tf_op jit(solution)/shard_map/all_to_all | solution.py:136
  168.8 0.8 fusion.10
  169.9 0.8 fusion.15
  170.9 17.4 %all_to_all.63 = f32[4,520,128]{2,1,0:T(8,128)S(1)} all-to-all(f32[4,520,128]{2,1,0:T(8,128)S(1)} %maximum_maximum_fusion), channel_id=1, replica_groups=mesh['clique'=8,'shard'=4] {'shard'}, dimensions={0} | all-to-all | bytes 2129920 | tf_op jit(solution)/shard_map/all_to_all | solution.py:117
  189.6 0.9 fusion.163
  190.6 0.8 copy-done.7
  193.5 10.7 %all_to_all.64 = f32[4,264,128]{2,1,0:T(8,128)S(1)} all-to-all(f32[4,264,128]{2,1,0:T(8,128)S(1)} %concatenate.151), channel_id=1, replica_groups=mesh['clique'=8,'shard'=4] {'shard'}, dimensions={0} | all-to-all | bytes 1081344 | tf_op jit(solution)/shard_map/all_to_all | solution.py:93
  205.5 0.8 fusion.17
  206.4 17.9 %all_to_all.65 = f32[8,128,128]{2,1,0:T(8,128)S(1)} all-to-all(f32[8,128,128]{2,1,0:T(8,128)S(1)} %bitcast.165), channel_id=1, replica_groups=mesh['clique'=8,'shard'=4] {'clique'}, dimensions={0} | all-to-all | bytes 1048576 | tf_op jit(solution)/shard_map/all_to_all | solution.py:129
  224.3 0.9 convolution_divide_fusion
  225.2 0.9 copy.38
  226.1 3.5 %all-to-all-start.10 = ((f32[8,128,128]{2,1,0:T(8,128)}), f32[8,128,128]{2,1,0:T(8,128)S(1)}, u32[]{:S(2)}, u32[]{:S(2)}) async-start(f32[8,128,128]{2,1,0:T(8,128)} %copy.38), calls=%async_computation.10 | async-start | bytes 1048576 | tf_op jit(solution)/shard_map/all_to_all | solution.py:136
  229.6 2.3 fusion.4
  232.0 2.2 fusion.7
  234.2 10.6 %all-to-all-done.10 = f32[8,128,128]{2,1,0:T(8,128)S(1)} async-done(((f32[8,128,128]{2,1,0:T(8,128)}), f32[8,128,128]{2,1,0:T(8,128)S(1)}, u32[]{:S(2)}, u32[]{:S(2)}) %all-to-all-start.10) | async-done | bytes 524320 | tf_op jit(solution)/shard_map/all_to_all | solution.py:136
  244.9 0.8 fusion.16
  245.8 0.8 slice_add_fusion.1
  246.6 3.5 %all-to-all-start.11 = ((f32[4,256,128]{2,1,0:T(8,128)}), f32[4,256,128]{2,1,0:T(8,128)S(1)}, u32[]{:S(2)}, u32[]{:S(2)}) async-start(f32[4,256,128]{2,1,0:T(8,128)} %bitcast.57), calls=%async_computation.11 | async-start | bytes 1048576 | tf_op jit(solution)/shard_map/all_to_all | solution.py:117
  250.1 1.3 fusion.64
  251.4 6.7 %all-to-all-done.11 = f32[4,256,128]{2,1,0:T(8,128)S(1)} async-done(((f32[4,256,128]{2,1,0:T(8,128)}), f32[4,256,128]{2,1,0:T(8,128)S(1)}, u32[]{:S(2)}, u32[]{:S(2)}) %all-to-all-start.11) | async-done | bytes 524320 | tf_op jit(solution)/shard_map/all_to_all | solution.py:117
  258.2 1.3 fusion.5
  259.5 1.2 maximum_bitcast_fusion
  (88 shorter events, 16.2 us)
Async XLA Ops:
  1.9 3.4 %copy-start.3 = (f32[3,1,1024,128]{3,2,1,0:T(8,128)S(1)}, f32[3,1,1024,128]{3,2,1,0:T(8,128)}, u32[]{:S(2)}) copy-start(f32[3,1,1024,128]{3,2,1,0:T(8,128)} %param.4) | copy-start | bytes 4718596
  24.3 5.7 %copy-start.5 = (s32[2,8]{1,0:T(2,128)S(1)}, s32[2,8]{1,0:T(2,128)}, u32[]{:S(2)}) copy-start(s32[2,8]{1,0:T(2,128)} %param.7) | copy-start | bytes 196
  25.2 20.2 %all-to-all-start.1 = ((f32[8,128,128]{2,1,0:T(8,128)}), f32[8,128,128]{2,1,0:T(8,128)S(1)}, u32[]{:S(2)}, u32[]{:S(2)}) async-start(f32[8,128,128]{2,1,0:T(8,128)} %bitcast.32), calls=%async_computation.1 | async-start | bytes 1048576 | tf_op jit(solution)/shard_map/all_to_all | solution.py:129
  45.4 5.2 %copy-start = (f32[8,128,128]{2,1,0:T(8,128)}, f32[8,128,128]{2,1,0:T(8,128)S(1)}, u32[]{:S(2)}) copy-start(f32[8,128,128]{2,1,0:T(8,128)S(1)} %all-to-all-done.1) | copy-start | bytes 1572868
  47.0 18.8 %all-to-all-start.2 = ((f32[8,128,128]{2,1,0:T(8,128)}), f32[8,128,128]{2,1,0:T(8,128)S(1)}, u32[]{:S(2)}, u32[]{:S(2)}) async-start(f32[8,128,128]{2,1,0:T(8,128)} %copy.30), calls=%async_computation.2 | async-start | bytes 1048576 | tf_op jit(solution)/shard_map/all_to_all | solution.py:136
  67.8 17.1 %all-to-all-start.3 = ((f32[4,512,128]{2,1,0:T(8,128)}), f32[4,512,128]{2,1,0:T(8,128)S(1)}, u32[]{:S(2)}, u32[]{:S(2)}) async-start(f32[4,512,128]{2,1,0:T(8,128)} %pad_maximum_fusion.1), calls=%async_computation.3 | async-start | bytes 2097152 | tf_op jit(solution)/shard_map/all_to_all | solution.py:117
  87.0 1.9 copy-start.6
  91.9 11.2 %all-to-all-start.4 = ((f32[4,264,128]{2,1,0:T(8,128)}), f32[4,264,128]{2,1,0:T(8,128)S(1)}, u32[]{:S(2)}, u32[]{:S(2)}) async-start(f32[4,264,128]{2,1,0:T(8,128)} %concatenate.141), calls=%async_computation.4 | async-start | bytes 1081344 | tf_op jit(solution)/shard_map/all_to_all | solution.py:93
  189.6 1.8 copy-start.7
  190.6 1.5 copy-start.4
  206.3 17.9 %copy-start.1 = (f32[8,128,128]{2,1,0:T(8,128)S(1)}, f32[8,128,128]{2,1,0:T(8,128)}, u32[]{:S(2)}) copy-start(f32[8,128,128]{2,1,0:T(8,128)} %copy-done) | copy-start | bytes 1572868
  226.1 18.8 %all-to-all-start.10 = ((f32[8,128,128]{2,1,0:T(8,128)}), f32[8,128,128]{2,1,0:T(8,128)S(1)}, u32[]{:S(2)}, u32[]{:S(2)}) async-start(f32[8,128,128]{2,1,0:T(8,128)} %copy.38), calls=%async_computation.10 | async-start | bytes 1048576 | tf_op jit(solution)/shard_map/all_to_all | solution.py:136
  229.6 2.3 copy-start.2
  246.6 11.4 %all-to-all-start.11 = ((f32[4,256,128]{2,1,0:T(8,128)}), f32[4,256,128]{2,1,0:T(8,128)S(1)}, u32[]{:S(2)}, u32[]{:S(2)}) async-start(f32[4,256,128]{2,1,0:T(8,128)} %bitcast.57), calls=%async_computation.11 | async-start | bytes 1048576 | tf_op jit(solution)/shard_map/all_to_all | solution.py:117

commit v13 on v12

--- a/solution.py
+++ b/solution.py
@@ -66,21 +66,29 @@
         for which in range(4)
     ]
     halves = jnp.stack([slot // 32, slot % 32], axis=2).astype(jnp.bfloat16)
-    placed = (
-        position[:, :, None] == jnp.arange(block_count, dtype=jnp.int32)[None, None, :]
-    ).astype(jnp.bfloat16)
-    sent_halves = jnp.einsum("lbi,lbh->lih", placed, halves, preferred_element_type=jnp.float32)
-    sent_slots = (sent_halves[:, :, 0] * 32 + sent_halves[:, :, 1]).astype(jnp.int32)
+
+    def slot_chunk_of(which):
+        placed = (
+            position[jnp.array(which), :, None] == jnp.arange(block_count, dtype=jnp.int32)[None, None, :]
+        ).astype(jnp.bfloat16)
+        got = jnp.einsum("lbi,lbh->lih", placed, halves[jnp.array(which)], preferred_element_type=jnp.float32)
+        sent = got[:, :, 0] * 32 + got[:, :, 1]
+        rows = (len(which) * per_peer) // lane_count
+        return (
+            sent.reshape(len(which), shard_count, per_peer)
+            .transpose(1, 0, 2)
+            .reshape(shard_count, rows, lane_count)
+        )
+
+    def take_slots(received, which):
+        got = received.reshape(shard_count, len(which), per_peer).transpose(1, 0, 2)
+        got = got.reshape(len(which), block_count).astype(jnp.int32)
+        for number, list_number in enumerate(which):
+            arrived[list_number] = got[number]
+
     down1_to_up0 = lax.dot_general(
         sorting[1], sorting[3], (((1,), (1,)), ((), ())), preferred_element_type=jnp.float32
     ).astype(jnp.bfloat16)
-    slot_rows = (4 * per_peer) // lane_count
-    slot_chunk = (
-        sent_slots.reshape(4, shard_count, per_peer)
-        .transpose(1, 0, 2)
-        .reshape(shard_count, slot_rows, lane_count)
-        .astype(jnp.float32)
-    )
     arrived = [None] * 4
     piece_rows = per_owner // clique_count
 
@@ -89,15 +97,12 @@
         chunks = [rows.reshape(shard_count, per_peer, lane_count) for rows, _ in items]
         chunks.append(jnp.broadcast_to(partial_sum, (shard_count, PAD, lane_count)))
         if with_slots:
-            chunks.append(slot_chunk)
+            chunks.append(slot_chunk_of([0, 3]))
         arrived_rows = lax.all_to_all(jnp.concatenate(chunks, axis=1), "shard", 0, 0, tiled=True)
         head = len(items) * per_peer
         total = jnp.sum(arrived_rows[:, head, 0])
         if with_slots:
-            got = arrived_rows[:, head + PAD :].reshape(shard_count, 4, per_peer)
-            got = got.transpose(1, 0, 2).reshape(4, block_count).astype(jnp.int32)
-            for which in range(4):
-                arrived[which] = got[which]
+            take_slots(arrived_rows[:, head + PAD :], [0, 3])
         messages = []
         for number, (_, which) in enumerate(items):
             rows = arrived_rows[:, number * per_peer : (number + 1) * per_peer]
@@ -107,7 +112,10 @@
         return messages, total
 
     def fetch(items, partial=None, extra=None):
-        chunks = [] if extra is None else [extra.reshape(shard_count, per_peer, lane_count)]
+        chunks = []
+        if extra is not None:
+            chunks = [extra.reshape(shard_count, per_peer, lane_count), slot_chunk_of([1, 2])]
+        slot_count = 0 if extra is None else chunks[1].shape[1]
         for owned_rows, which in items:
             owned_rows = jnp.where(jnp.isfinite(owned_rows), owned_rows, 0.0)
             picked = gather_rows(owned_rows, arrived[which])
@@ -115,6 +123,9 @@
         if partial is not None:
             chunks.append(jnp.broadcast_to(partial, (shard_count, PAD, lane_count)))
         back = lax.all_to_all(jnp.concatenate(chunks, axis=1), "shard", 0, 0, tiled=True)
+        if extra is not None:
+            take_slots(back[:, per_peer : per_peer + slot_count], [1, 2])
+            back = jnp.concatenate([back[:, :per_peer], back[:, per_peer + slot_count :]], axis=1)
         count = len(items) + (extra is not None)
         rows = [
             back[:, number * per_peer : (number + 1) * per_peer].reshape(block_count, lane_count)

time: 262 us -> 263 us (level)
  waiting for transfers between devices: 61.4 us -> 58.6 us
    all_to_all x2, waiting for transfers between devices: 25 us -> 22.1 us  [from_middle(): lax.all_to_all(jnp.concatenate(chunks, axis=1), 'clique', 0, 0, tiled=True)]
  transfers between devices with their start and end apart: 6 -> 6, of which waited for: 6 -> 6; matrix products, arithmetic and copies ran while one was open for 5% -> 6% of each run, Pallas kernels for 0% -> 0%
where the time goes in v13:
time: 263 us; the launch traced here: 262 us
  blocking collectives  119 us (45%)
  waiting for transfers between devices  58.6 us (22%)
  matrix products  28.8 us (11%)
  starting transfers between devices  22.6 us (9%)
  other arithmetic  16.6 us (6%)
  local copies, waits for them, and re-layouts  12.1 us (5%)
  between operations  3.44 us (1%)
    all_to_all x2, blocking collectives, to_middle(): lax.all_to_all(jnp.concatenate(pieces, axis=1), 'clique', 0, 0, tiled=True)  47.4 us
    all_to_all x1, blocking collectives, from_middle(): lax.all_to_all(jnp.concatenate(chunks, axis=1), 'clique', 0, 0, tiled=True)  29.7 us
    all_to_all x2, blocking collectives, send(): lax.all_to_all(jnp.concatenate(chunks, axis=1), 'shard', 0, 0, tiled=True)  24.8 us
    all_to_all x2, waiting for transfers between devices, from_middle(): lax.all_to_all(jnp.concatenate(chunks, axis=1), 'clique', 0, 0, tiled=True)  22.1 us
    all_to_all x1, blocking collectives, fetch(): lax.all_to_all(jnp.concatenate(chunks, axis=1), 'shard', 0, 0, tiled=True)  17.4 us
    dot_general x16, matrix products, split_dot(): lax.dot_general(one_hot, parts, (((contract,), (0,)), ((), ())), preferre...  17.4 us
    all_to_all x1, waiting for transfers between devices, to_middle(): lax.all_to_all(jnp.concatenate(pieces, axis=1), 'clique', 0, 0, tiled=True)  15.3 us
    all_to_all x2, waiting for transfers between devices, fetch(): lax.all_to_all(jnp.concatenate(chunks, axis=1), 'shard', 0, 0, tiled=True)  14.4 us
  transfers between devices with their start and end apart: 6, of which 6 were waited for; matrix products, arithmetic and copies ran while one was open for 6% of the time, Pallas kernels for 0%

profile of v13, /device:TPU:0, one launch (start us, length us, event | category | flops | bytes accessed | tf_op | source)
XLA Modules:
  0.0 261.5 jit_solution(3483317509645528096)
XLA Ops:
  3.1 1.6 fusion.1
  7.4 14.1 %all_to_all.60 = f32[4,268,128]{2,1,0:T(8,128)S(1)} all-to-all(f32[4,268,128]{2,1,0:T(8,128)S(1)} %pad_maximum_fusion.3), channel_id=1, replica_groups=mesh['clique'=8,'shard'=4] {'shard'}, dimensions={0} | all-to-all | bytes 1097728 | tf_op jit(solution)/shard_map/all_to_all | solution.py:101
  23.8 0.9 fusion.69
  24.6 5.0 %all-to-all-start.1 = ((f32[8,128,128]{2,1,0:T(8,128)}), f32[8,128,128]{2,1,0:T(8,128)S(1)}, u32[]{:S(2)}, u32[]{:S(2)}) async-start(f32[8,128,128]{2,1,0:T(8,128)} %bitcast.26), calls=%async_computation.1 | async-start | bytes 1048576 | tf_op jit(solution)/shard_map/all_to_all | solution.py:140
  29.7 15.3 %all-to-all-done.1 = f32[8,128,128]{2,1,0:T(8,128)S(1)} async-done(((f32[8,128,128]{2,1,0:T(8,128)}), f32[8,128,128]{2,1,0:T(8,128)S(1)}, u32[]{:S(2)}, u32[]{:S(2)}) %all-to-all-start.1) | async-done | bytes 524320 | tf_op jit(solution)/shard_map/all_to_all | solution.py:140
  45.7 0.9 copy.36
  46.6 3.5 %all-to-all-start.2 = ((f32[8,128,128]{2,1,0:T(8,128)}), f32[8,128,128]{2,1,0:T(8,128)S(1)}, u32[]{:S(2)}, u32[]{:S(2)}) async-start(f32[8,128,128]{2,1,0:T(8,128)} %copy.36), calls=%async_computation.2 | async-start | bytes 1048576 | tf_op jit(solution)/shard_map/all_to_all | solution.py:147
  51.3 1.6 fusion
  53.0 0.8 fusion.10
  53.9 11.5 %all-to-all-done.2 = f32[8,128,128]{2,1,0:T(8,128)S(1)} async-done(((f32[8,128,128]{2,1,0:T(8,128)}), f32[8,128,128]{2,1,0:T(8,128)S(1)}, u32[]{:S(2)}, u32[]{:S(2)}) %all-to-all-start.2) | async-done | bytes 524320 | tf_op jit(solution)/shard_map/all_to_all | solution.py:147
  65.5 0.8 fusion.12
  66.4 1.0 pad_maximum_fusion.1
  67.4 3.7 %all-to-all-start.3 = ((f32[4,516,128]{2,1,0:T(8,128)}), f32[4,516,128]{2,1,0:T(8,128)S(1)}, u32[]{:S(2)}, u32[]{:S(2)}) async-start(f32[4,516,128]{2,1,0:T(8,128)} %pad_maximum_fusion.1), calls=%async_computation.3 | async-start | bytes 2129920 | tf_op jit(solution)/shard_map/all_to_all | solution.py:125
  71.1 2.0 fusion.2
  73.2 3.8 %fusion.38 = bf16[1024,1024]{1,0:T(8,128)(2,1)} fusion(s32[1024]{0:T(1024)S(1)} %bitcast.193, s32[1024]{0:T(1024)S(1)} %bitcast.190), kind=kOutput, calls=%fused_computation.56 | convolution fusion | flops 2150629376 | bytes 2105344 | tf_op jit(solution)/shard_map/dot_general | solution.py:89
  76.9 7.8 %all-to-all-done.3 = f32[4,516,128]{2,1,0:T(8,128)S(1)} async-done(((f32[4,516,128]{2,1,0:T(8,128)}), f32[4,516,128]{2,1,0:T(8,128)S(1)}, u32[]{:S(2)}, u32[]{:S(2)}) %all-to-all-start.3) | async-done | bytes 1056800 | tf_op jit(solution)/shard_map/all_to_all | solution.py:125
  84.7 1.0 fusion.161
  85.7 1.2 copy.49
  87.0 1.3 reduce-precision_convert_fusion.7
  88.3 1.3 reduce-precision_convert_fusion.9
  91.1 1.4 concatenate.132
  92.5 3.5 %all-to-all-start.4 = ((f32[4,264,128]{2,1,0:T(8,128)}), f32[4,264,128]{2,1,0:T(8,128)S(1)}, u32[]{:S(2)}, u32[]{:S(2)}) async-start(f32[4,264,128]{2,1,0:T(8,128)} %concatenate.132), calls=%async_computation.4 | async-start | bytes 1081344 | tf_op jit(solution)/shard_map/all_to_all | solution.py:101
  96.0 0.8 fusion.16
  96.9 6.8 %all-to-all-done.4 = f32[4,264,128]{2,1,0:T(8,128)S(1)} async-done(((f32[4,264,128]{2,1,0:T(8,128)}), f32[4,264,128]{2,1,0:T(8,128)S(1)}, u32[]{:S(2)}, u32[]{:S(2)}) %all-to-all-start.4) | async-done | bytes 540704 | tf_op jit(solution)/shard_map/all_to_all | solution.py:101
  105.1 0.8 fusion.15
  106.1 29.6 %all_to_all.61 = f32[8,256,128]{2,1,0:T(8,128)S(1)} all-to-all(f32[8,256,128]{2,1,0:T(8,128)S(1)} %pad_maximum_fusion.2), channel_id=1, replica_groups=mesh['clique'=8,'shard'=4] {'clique'}, dimensions={0} | all-to-all | bytes 2097152 | tf_op jit(solution)/shard_map/all_to_all | solution.py:140
  135.7 1.1 fusion.119
  136.8 0.9 convolution_divide_fusion.1
  138.3 29.7 %all_to_all.62 = f32[8,264,128]{2,1,0:T(8,128)S(1)} all-to-all(f32[8,264,128]{2,1,0:T(8,128)S(1)} %copy.41), channel_id=1, replica_groups=mesh['clique'=8,'shard'=4] {'clique'}, dimensions={0} | all-to-all | bytes 2162688 | tf_op jit(solution)/shard_map/all_to_all | solution.py:147
  169.5 0.8 fusion.14
  170.5 0.8 fusion.17
  171.5 17.4 %all_to_all.63 = f32[4,520,128]{2,1,0:T(8,128)S(1)} all-to-all(f32[4,520,128]{2,1,0:T(8,128)S(1)} %maximum_maximum_fusion), channel_id=1, replica_groups=mesh['clique'=8,'shard'=4] {'shard'}, dimensions={0} | all-to-all | bytes 2129920 | tf_op jit(solution)/shard_map/all_to_all | solution.py:125
  190.2 0.9 fusion.160
  194.1 10.7 %all_to_all.64 = f32[4,264,128]{2,1,0:T(8,128)S(1)} all-to-all(f32[4,264,128]{2,1,0:T(8,128)S(1)} %concatenate.142), channel_id=1, replica_groups=mesh['clique'=8,'shard'=4] {'shard'}, dimensions={0} | all-to-all | bytes 1081344 | tf_op jit(solution)/shard_map/all_to_all | solution.py:101
  207.2 17.9 %all_to_all.65 = f32[8,128,128]{2,1,0:T(8,128)S(1)} all-to-all(f32[8,128,128]{2,1,0:T(8,128)S(1)} %bitcast.171), channel_id=1, replica_groups=mesh['clique'=8,'shard'=4] {'clique'}, dimensions={0} | all-to-all | bytes 1048576 | tf_op jit(solution)/shard_map/all_to_all | solution.py:140
  225.0 0.9 convolution_divide_fusion
  225.9 0.9 copy.44
  226.8 3.5 %all-to-all-start.10 = ((f32[8,128,128]{2,1,0:T(8,128)}), f32[8,128,128]{2,1,0:T(8,128)S(1)}, u32[]{:S(2)}, u32[]{:S(2)}) async-start(f32[8,128,128]{2,1,0:T(8,128)} %copy.44), calls=%async_computation.10 | async-start | bytes 1048576 | tf_op jit(solution)/shard_map/all_to_all | solution.py:147
  230.3 2.3 fusion.4
  232.8 2.2 fusion.9
  235.0 10.6 %all-to-all-done.10 = f32[8,128,128]{2,1,0:T(8,128)S(1)} async-done(((f32[8,128,128]{2,1,0:T(8,128)}), f32[8,128,128]{2,1,0:T(8,128)S(1)}, u32[]{:S(2)}, u32[]{:S(2)}) %all-to-all-start.10) | async-done | bytes 524320 | tf_op jit(solution)/shard_map/all_to_all | solution.py:147
  245.7 0.8 fusion.18
  246.5 0.9 slice_add_fusion.1
  247.4 3.5 %all-to-all-start.11 = ((f32[4,256,128]{2,1,0:T(8,128)}), f32[4,256,128]{2,1,0:T(8,128)S(1)}, u32[]{:S(2)}, u32[]{:S(2)}) async-start(f32[4,256,128]{2,1,0:T(8,128)} %bitcast.59), calls=%async_computation.11 | async-start | bytes 1048576 | tf_op jit(solution)/shard_map/all_to_all | solution.py:125
  250.9 1.3 fusion.66
  252.2 6.7 %all-to-all-done.11 = f32[4,256,128]{2,1,0:T(8,128)S(1)} async-done(((f32[4,256,128]{2,1,0:T(8,128)}), f32[4,256,128]{2,1,0:T(8,128)S(1)}, u32[]{:S(2)}, u32[]{:S(2)}) %all-to-all-start.11) | async-done | bytes 524320 | tf_op jit(solution)/shard_map/all_to_all | solution.py:125
  258.9 1.3 fusion.6
  260.3 1.2 maximum_bitcast_fusion
  (104 shorter events, 19.9 us)
Async XLA Ops:
  2.5 2.3 copy-start.3
  23.8 5.9 %copy-start.5 = (s32[2,8]{1,0:T(2,128)S(1)}, s32[2,8]{1,0:T(2,128)}, u32[]{:S(2)}) copy-start(s32[2,8]{1,0:T(2,128)} %param.11) | copy-start | bytes 196
  24.6 25.5 %copy-start.6 = (s32[2]{0:T(128)S(1)}, s32[2]{0:T(128)}, u32[]{:S(2)}) copy-start(s32[2]{0:T(128)} %constant.79) | copy-start | bytes 28
  24.6 20.3 %all-to-all-start.1 = ((f32[8,128,128]{2,1,0:T(8,128)}), f32[8,128,128]{2,1,0:T(8,128)S(1)}, u32[]{:S(2)}, u32[]{:S(2)}) async-start(f32[8,128,128]{2,1,0:T(8,128)} %bitcast.26), calls=%async_computation.1 | async-start | bytes 1048576 | tf_op jit(solution)/shard_map/all_to_all | solution.py:140
  45.0 5.8 %copy-start = (f32[8,128,128]{2,1,0:T(8,128)}, f32[8,128,128]{2,1,0:T(8,128)S(1)}, u32[]{:S(2)}) copy-start(f32[8,128,128]{2,1,0:T(8,128)S(1)} %all-to-all-done.1) | copy-start | bytes 1572868
  46.6 18.8 %all-to-all-start.2 = ((f32[8,128,128]{2,1,0:T(8,128)}), f32[8,128,128]{2,1,0:T(8,128)S(1)}, u32[]{:S(2)}, u32[]{:S(2)}) async-start(f32[8,128,128]{2,1,0:T(8,128)} %copy.36), calls=%async_computation.2 | async-start | bytes 1048576 | tf_op jit(solution)/shard_map/all_to_all | solution.py:147
  67.4 17.3 %all-to-all-start.3 = ((f32[4,516,128]{2,1,0:T(8,128)}), f32[4,516,128]{2,1,0:T(8,128)S(1)}, u32[]{:S(2)}, u32[]{:S(2)}) async-start(f32[4,516,128]{2,1,0:T(8,128)} %pad_maximum_fusion.1), calls=%async_computation.3 | async-start | bytes 2129920 | tf_op jit(solution)/shard_map/all_to_all | solution.py:125
  87.0 2.7 %copy-start.7 = (bf16[1024,1024]{1,0:T(8,128)(2,1)S(1)}, bf16[1024,1024]{1,0:T(8,128)(2,1)}, u32[]{:S(2)}) copy-start(bf16[1024,1024]{1,0:T(8,128)(2,1)} %fusion.38) | copy-start | bytes 6291460
  92.5 11.2 %all-to-all-start.4 = ((f32[4,264,128]{2,1,0:T(8,128)}), f32[4,264,128]{2,1,0:T(8,128)S(1)}, u32[]{:S(2)}, u32[]{:S(2)}) async-start(f32[4,264,128]{2,1,0:T(8,128)} %concatenate.132), calls=%async_computation.4 | async-start | bytes 1081344 | tf_op jit(solution)/shard_map/all_to_all | solution.py:101
  190.2 1.8 copy-start.8
  191.2 1.5 copy-start.4
  207.1 17.9 %copy-start.1 = (f32[8,128,128]{2,1,0:T(8,128)S(1)}, f32[8,128,128]{2,1,0:T(8,128)}, u32[]{:S(2)}) copy-start(f32[8,128,128]{2,1,0:T(8,128)} %copy-done) | copy-start | bytes 1572868
  226.8 18.8 %all-to-all-start.10 = ((f32[8,128,128]{2,1,0:T(8,128)}), f32[8,128,128]{2,1,0:T(8,128)S(1)}, u32[]{:S(2)}, u32[]{:S(2)}) async-start(f32[8,128,128]{2,1,0:T(8,128)} %copy.44), calls=%async_computation.10 | async-start | bytes 1048576 | tf_op jit(solution)/shard_map/all_to_all | solution.py:147
  230.3 2.3 copy-start.2
  247.4 11.4 %all-to-all-start.11 = ((f32[4,256,128]{2,1,0:T(8,128)}), f32[4,256,128]{2,1,0:T(8,128)S(1)}, u32[]{:S(2)}, u32[]{:S(2)}) async-start(f32[4,256,128]{2,1,0:T(8,128)} %bitcast.59), calls=%async_computation.11 | async-start | bytes 1048576 | tf_op jit(solution)/shard_map/all_to_all | solution.py:125

commit v14 on v12

--- a/solution.py
+++ b/solution.py
@@ -168,7 +168,7 @@
     incoming0_mid = jnp.where(jnp.isfinite(incoming0_mid), incoming0_mid, 0.0)
     fresh0_mid = down0_mid * incoming0_mid
     partial = jnp.dot(sel[0], jnp.sum(fresh0_mid, axis=(1, 2)), precision=lax.Precision.HIGHEST)
-    update0_mid = mix(sel[0], fresh0_mid) / scaled0_mid
+    update0_mid = jnp.take(fresh0_mid, parents[0], axis=0) / scaled0_mid
     (update0, incoming0), range_total = from_middle([update0_mid, incoming0_mid], partial)
     (picked, update0), total = fetch([(incoming0, 2), (update0, 1)], range_total)
     out0 = split_dot(sorting[2], t0_down0 * picked, transposed=True)
@@ -178,7 +178,7 @@
     (message,), total = send([(t1_down1, 3)])
     fresh1 = message * (sep_states / total)
     (fresh1_mid,) = to_middle([fresh1])
-    (update1,), _ = from_middle([mix(sel[1], fresh1_mid) / scaled1_mid])
+    (update1,), _ = from_middle([jnp.take(fresh1_mid, parents[1], axis=0) / scaled1_mid])
     (picked,), _ = fetch([(update1, 0)])
     out2 = split_dot(sorting[0], t2_up1 * picked, transposed=True)
     return jnp.stack([out0, out1, out2])[:, None]

time: 262 us -> 265 us (1.011)
  blocking collectives: 119 us -> 71.9 us
  waiting for transfers between devices: 61.4 us -> 102 us
  starting transfers between devices: 22.5 us -> 29.6 us
  other arithmetic: 15.5 us -> 19.1 us
    all_to_all x2 -> x0, blocking collectives: 47.4 us -> none  [to_middle(): lax.all_to_all(jnp.concatenate(pieces, axis=1), 'clique', 0, 0, tiled=True)]
    all_to_all x1 -> x3, waiting for transfers between devices: 15.3 us -> 57 us  [to_middle(): lax.all_to_all(jnp.concatenate(pieces, axis=1), 'clique', 0, 0, tiled=True)]
    all_to_all x1 -> x3, starting transfers between devices: 4.87 us -> 11.9 us  [to_middle(): lax.all_to_all(jnp.concatenate(pieces, axis=1), 'clique', 0, 0, tiled=True)]
  transfers between devices with their start and end apart: 6 -> 8, of which waited for: 6 -> 8; matrix products, arithmetic and copies ran while one was open for 5% -> 5% of each run, Pallas kernels for 0% -> 0%
where the time goes in v14:
time: 265 us; the launch traced here: 264 us
  waiting for transfers between devices  102 us (38%)
  blocking collectives  71.9 us (27%)
  starting transfers between devices  29.6 us (11%)
  matrix products  27.7 us (10%)
  other arithmetic  19.1 us (7%)
  local copies, waits for them, and re-layouts  10.2 us (4%)
  between operations  3.46 us (1%)
    all_to_all x3, waiting for transfers between devices, to_middle(): lax.all_to_all(jnp.concatenate(pieces, axis=1), 'clique', 0, 0, tiled=True)  57 us
    all_to_all x1, blocking collectives, from_middle(): lax.all_to_all(jnp.concatenate(chunks, axis=1), 'clique', 0, 0, tiled=True)  29.7 us
    all_to_all x2, blocking collectives, send(): lax.all_to_all(jnp.concatenate(chunks, axis=1), 'shard', 0, 0, tiled=True)  24.9 us
    all_to_all x2, waiting for transfers between devices, from_middle(): lax.all_to_all(jnp.concatenate(chunks, axis=1), 'clique', 0, 0, tiled=True)  24 us
    dot_general x16, matrix products, split_dot(): lax.dot_general(one_hot, parts, (((contract,), (0,)), ((), ())), preferre...  17.4 us
    all_to_all x1, blocking collectives, fetch(): lax.all_to_all(jnp.concatenate(chunks, axis=1), 'shard', 0, 0, tiled=True)  17.4 us
    all_to_all x2, waiting for transfers between devices, fetch(): lax.all_to_all(jnp.concatenate(chunks, axis=1), 'shard', 0, 0, tiled=True)  14.2 us
    all_to_all x3, starting transfers between devices, to_middle(): lax.all_to_all(jnp.concatenate(pieces, axis=1), 'clique', 0, 0, tiled=True)  11.9 us
  transfers between devices with their start and end apart: 8, of which 8 were waited for; matrix products, arithmetic and copies ran while one was open for 5% of the time, Pallas kernels for 0%

profile of v14, /device:TPU:0, one launch (start us, length us, event | category | flops | bytes accessed | tf_op | source)
XLA Modules:
  0.0 263.9 jit_solution(11516691934426078681)
XLA Ops:
  1.9 3.3 %fusion = f32[4,1024,2]{1,2,0:T(2,128)S(1)} fusion(s32[4,1024]{1,0:T(4,128)S(1)} %add_add_fusion, bf16[4,1024,1]{1,2,0:T(2,128)(2,1)S(1)} %fusion.117, bf16[4,1024,1]{1,2,0:T(2,128)(2,1)S(1)} %get-tuple-element.18), kind=kOutput, calls=%fused_computation.3 | convolution fusion | flops 21004288 | bytes 65536 | tf_op jit(solution)/shard_map/lbi,lbh->lih/dot_general | solution.py:72
  7.9 14.1 %all_to_all.60 = f32[4,272,128]{2,1,0:T(8,128)S(1)} all-to-all(f32[4,272,128]{2,1,0:T(8,128)S(1)} %pad_maximum_fusion.3), channel_id=1, replica_groups=mesh['clique'=8,'shard'=4] {'shard'}, dimensions={0} | all-to-all | bytes 1114112 | tf_op jit(solution)/shard_map/all_to_all | solution.py:93
  24.3 0.9 fusion.66
  25.2 4.9 %all-to-all-start.1 = ((f32[8,128,128]{2,1,0:T(8,128)}), f32[8,128,128]{2,1,0:T(8,128)S(1)}, u32[]{:S(2)}, u32[]{:S(2)}) async-start(f32[8,128,128]{2,1,0:T(8,128)} %bitcast.31), calls=%async_computation.1 | async-start | bytes 1048576 | tf_op jit(solution)/shard_map/all_to_all | solution.py:129
  30.1 15.3 %all-to-all-done.1 = f32[8,128,128]{2,1,0:T(8,128)S(1)} async-done(((f32[8,128,128]{2,1,0:T(8,128)}), f32[8,128,128]{2,1,0:T(8,128)S(1)}, u32[]{:S(2)}, u32[]{:S(2)}) %all-to-all-start.1) | async-done | bytes 524320 | tf_op jit(solution)/shard_map/all_to_all | solution.py:129
  46.1 0.9 copy.26
  47.0 3.5 %all-to-all-start.2 = ((f32[8,128,128]{2,1,0:T(8,128)}), f32[8,128,128]{2,1,0:T(8,128)S(1)}, u32[]{:S(2)}, u32[]{:S(2)}) async-start(f32[8,128,128]{2,1,0:T(8,128)} %copy.26), calls=%async_computation.2 | async-start | bytes 1048576 | tf_op jit(solution)/shard_map/all_to_all | solution.py:136
  51.3 1.0 copy-done
  52.3 13.4 %all-to-all-done.2 = f32[8,128,128]{2,1,0:T(8,128)S(1)} async-done(((f32[8,128,128]{2,1,0:T(8,128)}), f32[8,128,128]{2,1,0:T(8,128)S(1)}, u32[]{:S(2)}, u32[]{:S(2)}) %all-to-all-start.2) | async-done | bytes 524320 | tf_op jit(solution)/shard_map/all_to_all | solution.py:136
  65.8 0.8 fusion.12
  66.7 1.0 pad_maximum_fusion.1
  67.8 3.7 %all-to-all-start.3 = ((f32[4,512,128]{2,1,0:T(8,128)}), f32[4,512,128]{2,1,0:T(8,128)S(1)}, u32[]{:S(2)}, u32[]{:S(2)}) async-start(f32[4,512,128]{2,1,0:T(8,128)} %pad_maximum_fusion.1), calls=%async_computation.3 | async-start | bytes 2097152 | tf_op jit(solution)/shard_map/all_to_all | solution.py:117
  71.5 2.1 fusion.2
  73.5 3.8 %fusion.36 = bf16[1024,1024]{1,0:T(8,128)(2,1)} fusion(s32[1024]{0:T(1024)S(1)} %bitcast.186, s32[1024]{0:T(1024)S(1)} %bitcast.175), kind=kOutput, calls=%fused_computation.51 | convolution fusion | flops 2150629376 | bytes 2105344 | tf_op jit(solution)/shard_map/dot_general | solution.py:74
  77.3 7.6 %all-to-all-done.3 = f32[4,512,128]{2,1,0:T(8,128)S(1)} async-done(((f32[4,512,128]{2,1,0:T(8,128)}), f32[4,512,128]{2,1,0:T(8,128)S(1)}, u32[]{:S(2)}, u32[]{:S(2)}) %all-to-all-start.3) | async-done | bytes 1048608 | tf_op jit(solution)/shard_map/all_to_all | solution.py:117
  85.3 1.5 reduce-precision_convert_fusion.9
  87.8 0.8 fusion.154
  88.6 1.5 concatenate.141
  90.1 3.5 %all-to-all-start.4 = ((f32[4,264,128]{2,1,0:T(8,128)}), f32[4,264,128]{2,1,0:T(8,128)S(1)}, u32[]{:S(2)}, u32[]{:S(2)}) async-start(f32[4,264,128]{2,1,0:T(8,128)} %concatenate.141), calls=%async_computation.4 | async-start | bytes 1081344 | tf_op jit(solution)/shard_map/all_to_all | solution.py:93
  93.6 0.8 fusion.14
  94.5 6.8 %all-to-all-done.4 = f32[4,264,128]{2,1,0:T(8,128)S(1)} async-done(((f32[4,264,128]{2,1,0:T(8,128)}), f32[4,264,128]{2,1,0:T(8,128)S(1)}, u32[]{:S(2)}, u32[]{:S(2)}) %all-to-all-start.4) | async-done | bytes 540704 | tf_op jit(solution)/shard_map/all_to_all | solution.py:93
  102.7 0.8 fusion.11
  103.6 1.0 pad_maximum_fusion.2
  104.6 3.6 %all-to-all-start.5 = ((f32[8,256,128]{2,1,0:T(8,128)}), f32[8,256,128]{2,1,0:T(8,128)S(1)}, u32[]{:S(2)}, u32[]{:S(2)}) async-start(f32[8,256,128]{2,1,0:T(8,128)} %pad_maximum_fusion.2), calls=%async_computation.5 | async-start | bytes 2097152 | tf_op jit(solution)/shard_map/all_to_all | solution.py:129
  108.2 26.5 %all-to-all-done.5 = f32[8,256,128]{2,1,0:T(8,128)S(1)} async-done(((f32[8,256,128]{2,1,0:T(8,128)}), f32[8,256,128]{2,1,0:T(8,128)S(1)}, u32[]{:S(2)}, u32[]{:S(2)}) %all-to-all-start.5) | async-done | bytes 1048608 | tf_op jit(solution)/shard_map/all_to_all | solution.py:129
  134.8 1.9 fusion.153
  138.1 1.1 pad_maximum_fusion
  139.5 29.7 %all_to_all.61 = f32[8,264,128]{2,1,0:T(8,128)S(1)} all-to-all(f32[8,264,128]{2,1,0:T(8,128)S(1)} %copy.32), channel_id=1, replica_groups=mesh['clique'=8,'shard'=4] {'clique'}, dimensions={0} | all-to-all | bytes 2162688 | tf_op jit(solution)/shard_map/all_to_all | solution.py:136
  170.6 0.8 fusion.10
  171.6 0.8 fusion.15
  172.6 17.4 %all_to_all.62 = f32[4,520,128]{2,1,0:T(8,128)S(1)} all-to-all(f32[4,520,128]{2,1,0:T(8,128)S(1)} %maximum_maximum_fusion), channel_id=1, replica_groups=mesh['clique'=8,'shard'=4] {'shard'}, dimensions={0} | all-to-all | bytes 2129920 | tf_op jit(solution)/shard_map/all_to_all | solution.py:117
  191.5 1.5 copy-done.6
  195.2 10.7 %all_to_all.63 = f32[4,264,128]{2,1,0:T(8,128)S(1)} all-to-all(f32[4,264,128]{2,1,0:T(8,128)S(1)} %concatenate.151), channel_id=1, replica_groups=mesh['clique'=8,'shard'=4] {'shard'}, dimensions={0} | all-to-all | bytes 1081344 | tf_op jit(solution)/shard_map/all_to_all | solution.py:93
  208.1 0.9 fusion.62
  209.0 3.5 %all-to-all-start.9 = ((f32[8,128,128]{2,1,0:T(8,128)}), f32[8,128,128]{2,1,0:T(8,128)S(1)}, u32[]{:S(2)}, u32[]{:S(2)}) async-start(f32[8,128,128]{2,1,0:T(8,128)} %bitcast.53), calls=%async_computation.9 | async-start | bytes 1048576 | tf_op jit(solution)/shard_map/all_to_all | solution.py:129
  212.5 15.2 %all-to-all-done.9 = f32[8,128,128]{2,1,0:T(8,128)S(1)} async-done(((f32[8,128,128]{2,1,0:T(8,128)}), f32[8,128,128]{2,1,0:T(8,128)S(1)}, u32[]{:S(2)}, u32[]{:S(2)}) %all-to-all-start.9) | async-done | bytes 524320 | tf_op jit(solution)/shard_map/all_to_all | solution.py:129
  228.3 0.9 select_divide_fusion
  229.2 3.5 %all-to-all-start.10 = ((f32[8,128,128]{2,1,0:T(8,128)}), f32[8,128,128]{2,1,0:T(8,128)S(1)}, u32[]{:S(2)}, u32[]{:S(2)}) async-start(f32[8,128,128]{2,1,0:T(8,128)} %select_divide_fusion), calls=%async_computation.10 | async-start | bytes 1048576 | tf_op jit(solution)/shard_map/all_to_all | solution.py:136
  232.8 2.3 fusion.4
  235.2 2.2 fusion.7
  237.5 10.5 %all-to-all-done.10 = f32[8,128,128]{2,1,0:T(8,128)S(1)} async-done(((f32[8,128,128]{2,1,0:T(8,128)}), f32[8,128,128]{2,1,0:T(8,128)S(1)}, u32[]{:S(2)}, u32[]{:S(2)}) %all-to-all-start.10) | async-done | bytes 524320 | tf_op jit(solution)/shard_map/all_to_all | solution.py:136
  248.1 0.8 fusion.16
  248.9 0.8 slice_add_fusion.1
  249.8 3.5 %all-to-all-start.11 = ((f32[4,256,128]{2,1,0:T(8,128)}), f32[4,256,128]{2,1,0:T(8,128)S(1)}, u32[]{:S(2)}, u32[]{:S(2)}) async-start(f32[4,256,128]{2,1,0:T(8,128)} %bitcast.55), calls=%async_computation.11 | async-start | bytes 1048576 | tf_op jit(solution)/shard_map/all_to_all | solution.py:117
  253.3 1.3 fusion.64
  254.6 6.7 %all-to-all-done.11 = f32[4,256,128]{2,1,0:T(8,128)S(1)} async-done(((f32[4,256,128]{2,1,0:T(8,128)}), f32[4,256,128]{2,1,0:T(8,128)S(1)}, u32[]{:S(2)}, u32[]{:S(2)}) %all-to-all-start.11) | async-done | bytes 524320 | tf_op jit(solution)/shard_map/all_to_all | solution.py:117
  261.3 1.3 fusion.5
  262.7 1.2 maximum_bitcast_fusion
  (93 shorter events, 19.0 us)
Async XLA Ops:
  1.9 3.4 %copy-start.2 = (f32[3,1,1024,128]{3,2,1,0:T(8,128)S(1)}, f32[3,1,1024,128]{3,2,1,0:T(8,128)}, u32[]{:S(2)}) copy-start(f32[3,1,1024,128]{3,2,1,0:T(8,128)} %param.6) | copy-start | bytes 4718596
  24.3 5.7 %copy-start.4 = (s32[2,8]{1,0:T(2,128)S(1)}, s32[2,8]{1,0:T(2,128)}, u32[]{:S(2)}) copy-start(s32[2,8]{1,0:T(2,128)} %param.9) | copy-start | bytes 196
  25.2 20.2 %all-to-all-start.1 = ((f32[8,128,128]{2,1,0:T(8,128)}), f32[8,128,128]{2,1,0:T(8,128)S(1)}, u32[]{:S(2)}, u32[]{:S(2)}) async-start(f32[8,128,128]{2,1,0:T(8,128)} %bitcast.31), calls=%async_computation.1 | async-start | bytes 1048576 | tf_op jit(solution)/shard_map/all_to_all | solution.py:129
  47.0 18.8 %all-to-all-start.2 = ((f32[8,128,128]{2,1,0:T(8,128)}), f32[8,128,128]{2,1,0:T(8,128)S(1)}, u32[]{:S(2)}, u32[]{:S(2)}) async-start(f32[8,128,128]{2,1,0:T(8,128)} %copy.26), calls=%async_computation.2 | async-start | bytes 1048576 | tf_op jit(solution)/shard_map/all_to_all | solution.py:136
  51.3 1.0 copy-start
  67.8 17.1 %all-to-all-start.3 = ((f32[4,512,128]{2,1,0:T(8,128)}), f32[4,512,128]{2,1,0:T(8,128)S(1)}, u32[]{:S(2)}, u32[]{:S(2)}) async-start(f32[4,512,128]{2,1,0:T(8,128)} %pad_maximum_fusion.1), calls=%async_computation.3 | async-start | bytes 2097152 | tf_op jit(solution)/shard_map/all_to_all | solution.py:117
  85.1 1.9 copy-start.5
  90.1 11.2 %all-to-all-start.4 = ((f32[4,264,128]{2,1,0:T(8,128)}), f32[4,264,128]{2,1,0:T(8,128)S(1)}, u32[]{:S(2)}, u32[]{:S(2)}) async-start(f32[4,264,128]{2,1,0:T(8,128)} %concatenate.141), calls=%async_computation.4 | async-start | bytes 1081344 | tf_op jit(solution)/shard_map/all_to_all | solution.py:93
  104.6 30.1 %all-to-all-start.5 = ((f32[8,256,128]{2,1,0:T(8,128)}), f32[8,256,128]{2,1,0:T(8,128)S(1)}, u32[]{:S(2)}, u32[]{:S(2)}) async-start(f32[8,256,128]{2,1,0:T(8,128)} %pad_maximum_fusion.2), calls=%async_computation.5 | async-start | bytes 2097152 | tf_op jit(solution)/shard_map/all_to_all | solution.py:129
  191.3 1.7 copy-start.6
  191.5 2.2 copy-start.3
  209.0 18.8 %all-to-all-start.9 = ((f32[8,128,128]{2,1,0:T(8,128)}), f32[8,128,128]{2,1,0:T(8,128)S(1)}, u32[]{:S(2)}, u32[]{:S(2)}) async-start(f32[8,128,128]{2,1,0:T(8,128)} %bitcast.53), calls=%async_computation.9 | async-start | bytes 1048576 | tf_op jit(solution)/shard_map/all_to_all | solution.py:129
  229.2 18.8 %all-to-all-start.10 = ((f32[8,128,128]{2,1,0:T(8,128)}), f32[8,128,128]{2,1,0:T(8,128)S(1)}, u32[]{:S(2)}, u32[]{:S(2)}) async-start(f32[8,128,128]{2,1,0:T(8,128)} %select_divide_fusion), calls=%async_computation.10 | async-start | bytes 1048576 | tf_op jit(solution)/shard_map/all_to_all | solution.py:136
  232.7 2.3 copy-start.1
  249.8 11.4 %all-to-all-start.11 = ((f32[4,256,128]{2,1,0:T(8,128)}), f32[4,256,128]{2,1,0:T(8,128)S(1)}, u32[]{:S(2)}, u32[]{:S(2)}) async-start(f32[4,256,128]{2,1,0:T(8,128)} %bitcast.55), calls=%async_computation.11 | async-start | bytes 1048576 | tf_op jit(solution)/shard_map/all_to_all | solution.py:117

commit v15 on v12

--- a/solution.py
+++ b/solution.py
@@ -84,8 +84,8 @@
     arrived = [None] * 4
     piece_rows = per_owner // clique_count
 
-    def send(items, with_slots=False):
-        partial_sum = jnp.sum(items[0][0])
+    def send(items, with_slots=False, unsorted=None):
+        partial_sum = jnp.sum(items[0][0] if unsorted is None else unsorted)
         chunks = [rows.reshape(shard_count, per_peer, lane_count) for rows, _ in items]
         chunks.append(jnp.broadcast_to(partial_sum, (shard_count, PAD, lane_count)))
         if with_slots:
@@ -152,7 +152,7 @@
     t0, t1, t2 = tables[0, 0], tables[1, 0], tables[2, 0]
 
     t2_up1 = split_dot(sorting[0], t2)
-    (message,), total = send([(t2_up1, 0)], with_slots=True)
+    (message,), total = send([(t2_up1, 0)], with_slots=True, unsorted=t2)
     scaled1 = message * (sep_states / total)
     (scaled1_mid,) = to_middle([scaled1])
     (incoming1,), _ = from_middle([jnp.exp(mix(sel[1].T, jnp.log(scaled1_mid)))])
@@ -161,7 +161,7 @@
     down0_message = segment_rows(level0_rows, arrived[2], per_owner)
     t1_down1 = split_dot(sorting[3], t1) * picked
     t1_up0 = split_dot(down1_to_up0, t1_down1)
-    (message,), total = send([(t1_up0, 1)])
+    (message,), total = send([(t1_up0, 1)], unsorted=t1_down1)
     scaled0 = message * (sep_states / total)
     scaled0_mid, down0_mid = to_middle([scaled0, down0_message])
     incoming0_mid = jnp.exp(mix(sel[0].T, jnp.log(scaled0_mid)))
@@ -175,7 +175,7 @@
     t1_up0 = t1_up0 * (update0 * (sep_states / total))
     out1 = split_dot(sorting[1], t1_up0, transposed=True)
     t1_down1 = split_dot(down1_to_up0, t1_up0, transposed=True)
-    (message,), total = send([(t1_down1, 3)])
+    (message,), total = send([(t1_down1, 3)], unsorted=t1_up0)
     fresh1 = message * (sep_states / total)
     (fresh1_mid,) = to_middle([fresh1])
     (update1,), _ = from_middle([mix(sel[1], fresh1_mid) / scaled1_mid])

time: 262 us -> 263 us (level)
  other arithmetic: 15.5 us -> 20 us
  transfers between devices with their start and end apart: 6 -> 6, of which waited for: 6 -> 6; matrix products, arithmetic and copies ran while one was open for 5% -> 6% of each run, Pallas kernels for 0% -> 0%
where the time goes in v15:
time: 263 us; the launch traced here: 261 us
  blocking collectives  119 us (45%)
  waiting for transfers between devices  59.2 us (23%)
  matrix products  28.8 us (11%)
  starting transfers between devices  22.5 us (9%)
  other arithmetic  20 us (8%)
  local copies, waits for them, and re-layouts  8.27 us (3%)
  between operations  3.41 us (1%)
    all_to_all x2, blocking collectives, to_middle(): lax.all_to_all(jnp.concatenate(pieces, axis=1), 'clique', 0, 0, tiled=True)  47.4 us
    all_to_all x1, blocking collectives, from_middle(): lax.all_to_all(jnp.concatenate(chunks, axis=1), 'clique', 0, 0, tiled=True)  29.7 us
    all_to_all x2, blocking collectives, send(): lax.all_to_all(jnp.concatenate(chunks, axis=1), 'shard', 0, 0, tiled=True)  24.9 us
    all_to_all x2, waiting for transfers between devices, from_middle(): lax.all_to_all(jnp.concatenate(chunks, axis=1), 'clique', 0, 0, tiled=True)  24 us
    all_to_all x1, blocking collectives, fetch(): lax.all_to_all(jnp.concatenate(chunks, axis=1), 'shard', 0, 0, tiled=True)  17.4 us
    dot_general x16, matrix products, split_dot(): lax.dot_general(one_hot, parts, (((contract,), (0,)), ((), ())), preferre...  17.3 us
    all_to_all x1, waiting for transfers between devices, to_middle(): lax.all_to_all(jnp.concatenate(pieces, axis=1), 'clique', 0, 0, tiled=True)  15.3 us
    all_to_all x2, waiting for transfers between devices, fetch(): lax.all_to_all(jnp.concatenate(chunks, axis=1), 'shard', 0, 0, tiled=True)  13 us
  transfers between devices with their start and end apart: 6, of which 6 were waited for; matrix products, arithmetic and copies ran while one was open for 6% of the time, Pallas kernels for 0%

profile of v15, /device:TPU:0, one launch (start us, length us, event | category | flops | bytes accessed | tf_op | source)
XLA Modules:
  0.0 261.5 jit_solution(879615248780631368)
XLA Ops:
  0.9 1.8 slice_reduce_fusion
  2.6 1.6 reduce-precision_convert_fusion.12
  5.3 3.3 %fusion = f32[4,1024,2]{1,2,0:T(2,128)S(1)} fusion(s32[4,1024]{1,0:T(4,128)S(1)} %add_add_fusion, bf16[4,1024,1]{1,2,0:T(2,128)(2,1)S(1)} %fusion.120, bf16[4,1024,1]{1,2,0:T(2,128)(2,1)S(1)} %get-tuple-element.7), kind=kOutput, calls=%fused_computation.1 | convolution fusion | flops 21004288 | bytes 65536 | tf_op jit(solution)/shard_map/lbi,lbh->lih/dot_general | solution.py:72
  8.7 0.8 fusion.6
  10.4 14.1 %all_to_all.60 = f32[4,272,128]{2,1,0:T(8,128)S(1)} all-to-all(f32[4,272,128]{2,1,0:T(8,128)S(1)} %pad_maximum_fusion.3), channel_id=1, replica_groups=mesh['clique'=8,'shard'=4] {'shard'}, dimensions={0} | all-to-all | bytes 1114112 | tf_op jit(solution)/shard_map/all_to_all | solution.py:93
  26.0 0.8 fusion.13
  26.8 0.9 fusion.66
  27.6 4.9 %all-to-all-start.1 = ((f32[8,128,128]{2,1,0:T(8,128)}), f32[8,128,128]{2,1,0:T(8,128)S(1)}, u32[]{:S(2)}, u32[]{:S(2)}) async-start(f32[8,128,128]{2,1,0:T(8,128)} %bitcast.32), calls=%async_computation.1 | async-start | bytes 1048576 | tf_op jit(solution)/shard_map/all_to_all | solution.py:129
  32.5 15.3 %all-to-all-done.1 = f32[8,128,128]{2,1,0:T(8,128)S(1)} async-done(((f32[8,128,128]{2,1,0:T(8,128)}), f32[8,128,128]{2,1,0:T(8,128)S(1)}, u32[]{:S(2)}, u32[]{:S(2)}) %all-to-all-start.1) | async-done | bytes 524320 | tf_op jit(solution)/shard_map/all_to_all | solution.py:129
  48.6 0.9 copy.30
  49.5 3.5 %all-to-all-start.2 = ((f32[8,128,128]{2,1,0:T(8,128)}), f32[8,128,128]{2,1,0:T(8,128)S(1)}, u32[]{:S(2)}, u32[]{:S(2)}) async-start(f32[8,128,128]{2,1,0:T(8,128)} %copy.30), calls=%async_computation.2 | async-start | bytes 1048576 | tf_op jit(solution)/shard_map/all_to_all | solution.py:136
  53.8 1.0 copy-done
  54.8 13.4 %all-to-all-done.2 = f32[8,128,128]{2,1,0:T(8,128)S(1)} async-done(((f32[8,128,128]{2,1,0:T(8,128)}), f32[8,128,128]{2,1,0:T(8,128)S(1)}, u32[]{:S(2)}, u32[]{:S(2)}) %all-to-all-start.2) | async-done | bytes 524320 | tf_op jit(solution)/shard_map/all_to_all | solution.py:136
  68.3 0.8 fusion.12
  69.2 1.0 pad_maximum_fusion.1
  70.3 3.7 %all-to-all-start.3 = ((f32[4,512,128]{2,1,0:T(8,128)}), f32[4,512,128]{2,1,0:T(8,128)S(1)}, u32[]{:S(2)}, u32[]{:S(2)}) async-start(f32[4,512,128]{2,1,0:T(8,128)} %pad_maximum_fusion.1), calls=%async_computation.3 | async-start | bytes 2097152 | tf_op jit(solution)/shard_map/all_to_all | solution.py:117
  74.0 2.1 fusion.2
  76.0 3.8 %fusion.36 = bf16[1024,1024]{1,0:T(8,128)(2,1)} fusion(s32[1024]{0:T(1024)S(1)} %bitcast.187, s32[1024]{0:T(1024)S(1)} %bitcast.176), kind=kOutput, calls=%fused_computation.49 | convolution fusion | flops 2150629376 | bytes 2105344 | tf_op jit(solution)/shard_map/dot_general | solution.py:74
  79.8 7.6 %all-to-all-done.3 = f32[4,512,128]{2,1,0:T(8,128)S(1)} async-done(((f32[4,512,128]{2,1,0:T(8,128)}), f32[4,512,128]{2,1,0:T(8,128)S(1)}, u32[]{:S(2)}, u32[]{:S(2)}) %all-to-all-start.3) | async-done | bytes 1048608 | tf_op jit(solution)/shard_map/all_to_all | solution.py:117
  87.7 2.2 fusion.160
  89.9 0.8 reduce-precision_convert_fusion.7
  91.6 1.6 concatenate.141
  93.1 3.5 %all-to-all-start.4 = ((f32[4,264,128]{2,1,0:T(8,128)}), f32[4,264,128]{2,1,0:T(8,128)S(1)}, u32[]{:S(2)}, u32[]{:S(2)}) async-start(f32[4,264,128]{2,1,0:T(8,128)} %concatenate.141), calls=%async_computation.4 | async-start | bytes 1081344 | tf_op jit(solution)/shard_map/all_to_all | solution.py:93
  97.5 6.8 %all-to-all-done.4 = f32[4,264,128]{2,1,0:T(8,128)S(1)} async-done(((f32[4,264,128]{2,1,0:T(8,128)}), f32[4,264,128]{2,1,0:T(8,128)S(1)}, u32[]{:S(2)}, u32[]{:S(2)}) %all-to-all-start.4) | async-done | bytes 540704 | tf_op jit(solution)/shard_map/all_to_all | solution.py:93
  106.6 29.6 %all_to_all.61 = f32[8,256,128]{2,1,0:T(8,128)S(1)} all-to-all(f32[8,256,128]{2,1,0:T(8,128)S(1)} %pad_maximum_fusion.2), channel_id=1, replica_groups=mesh['clique'=8,'shard'=4] {'clique'}, dimensions={0} | all-to-all | bytes 2097152 | tf_op jit(solution)/shard_map/all_to_all | solution.py:129
  136.3 1.1 fusion.117
  137.4 0.9 convolution_divide_fusion.1
  138.9 29.7 %all_to_all.62 = f32[8,264,128]{2,1,0:T(8,128)S(1)} all-to-all(f32[8,264,128]{2,1,0:T(8,128)S(1)} %copy.35), channel_id=1, replica_groups=mesh['clique'=8,'shard'=4] {'clique'}, dimensions={0} | all-to-all | bytes 2162688 | tf_op jit(solution)/shard_map/all_to_all | solution.py:136
  170.0 0.8 fusion.10
  171.0 0.8 fusion.15
  172.1 17.4 %all_to_all.63 = f32[4,520,128]{2,1,0:T(8,128)S(1)} all-to-all(f32[4,520,128]{2,1,0:T(8,128)S(1)} %maximum_maximum_fusion), channel_id=1, replica_groups=mesh['clique'=8,'shard'=4] {'shard'}, dimensions={0} | all-to-all | bytes 2129920 | tf_op jit(solution)/shard_map/all_to_all | solution.py:117
  190.8 0.9 fusion.163
  194.1 10.7 %all_to_all.64 = f32[4,264,128]{2,1,0:T(8,128)S(1)} all-to-all(f32[4,264,128]{2,1,0:T(8,128)S(1)} %concatenate.151), channel_id=1, replica_groups=mesh['clique'=8,'shard'=4] {'shard'}, dimensions={0} | all-to-all | bytes 1081344 | tf_op jit(solution)/shard_map/all_to_all | solution.py:93
  207.1 17.9 %all_to_all.65 = f32[8,128,128]{2,1,0:T(8,128)S(1)} all-to-all(f32[8,128,128]{2,1,0:T(8,128)S(1)} %bitcast.167), channel_id=1, replica_groups=mesh['clique'=8,'shard'=4] {'clique'}, dimensions={0} | all-to-all | bytes 1048576 | tf_op jit(solution)/shard_map/all_to_all | solution.py:129
  224.9 0.9 convolution_divide_fusion
  225.9 0.9 copy.38
  226.8 3.5 %all-to-all-start.10 = ((f32[8,128,128]{2,1,0:T(8,128)}), f32[8,128,128]{2,1,0:T(8,128)S(1)}, u32[]{:S(2)}, u32[]{:S(2)}) async-start(f32[8,128,128]{2,1,0:T(8,128)} %copy.38), calls=%async_computation.10 | async-start | bytes 1048576 | tf_op jit(solution)/shard_map/all_to_all | solution.py:136
  230.3 2.2 fusion.4
  232.7 2.2 fusion.7
  234.9 10.6 %all-to-all-done.10 = f32[8,128,128]{2,1,0:T(8,128)S(1)} async-done(((f32[8,128,128]{2,1,0:T(8,128)}), f32[8,128,128]{2,1,0:T(8,128)S(1)}, u32[]{:S(2)}, u32[]{:S(2)}) %all-to-all-start.10) | async-done | bytes 524320 | tf_op jit(solution)/shard_map/all_to_all | solution.py:136
  245.6 0.8 fusion.16
  246.5 0.9 slice_add_fusion.1
  247.3 3.5 %all-to-all-start.11 = ((f32[4,256,128]{2,1,0:T(8,128)}), f32[4,256,128]{2,1,0:T(8,128)S(1)}, u32[]{:S(2)}, u32[]{:S(2)}) async-start(f32[4,256,128]{2,1,0:T(8,128)} %bitcast.57), calls=%async_computation.11 | async-start | bytes 1048576 | tf_op jit(solution)/shard_map/all_to_all | solution.py:117
  250.8 1.3 fusion.64
  252.1 1.3 fusion.63
  253.3 5.5 %all-to-all-done.11 = f32[4,256,128]{2,1,0:T(8,128)S(1)} async-done(((f32[4,256,128]{2,1,0:T(8,128)}), f32[4,256,128]{2,1,0:T(8,128)S(1)}, u32[]{:S(2)}, u32[]{:S(2)}) %all-to-all-start.11) | async-done | bytes 524320 | tf_op jit(solution)/shard_map/all_to_all | solution.py:117
  258.9 1.3 fusion.5
  260.2 1.2 maximum_bitcast_fusion
  (92 shorter events, 16.3 us)
Async XLA Ops:
  26.8 5.7 %copy-start.6 = (s32[2,8]{1,0:T(2,128)S(1)}, s32[2,8]{1,0:T(2,128)}, u32[]{:S(2)}) copy-start(s32[2,8]{1,0:T(2,128)} %param.7) | copy-start | bytes 196
  27.6 20.2 %all-to-all-start.1 = ((f32[8,128,128]{2,1,0:T(8,128)}), f32[8,128,128]{2,1,0:T(8,128)S(1)}, u32[]{:S(2)}, u32[]{:S(2)}) async-start(f32[8,128,128]{2,1,0:T(8,128)} %bitcast.32), calls=%async_computation.1 | async-start | bytes 1048576 | tf_op jit(solution)/shard_map/all_to_all | solution.py:129
  47.8 5.9 %copy-start.2 = (f32[8,128,128]{2,1,0:T(8,128)}, f32[8,128,128]{2,1,0:T(8,128)S(1)}, u32[]{:S(2)}) copy-start(f32[8,128,128]{2,1,0:T(8,128)S(1)} %all-to-all-done.1) | copy-start | bytes 1572868
  49.5 18.8 %all-to-all-start.2 = ((f32[8,128,128]{2,1,0:T(8,128)}), f32[8,128,128]{2,1,0:T(8,128)S(1)}, u32[]{:S(2)}, u32[]{:S(2)}) async-start(f32[8,128,128]{2,1,0:T(8,128)} %copy.30), calls=%async_computation.2 | async-start | bytes 1048576 | tf_op jit(solution)/shard_map/all_to_all | solution.py:136
  53.8 1.0 copy-start
  70.3 17.1 %all-to-all-start.3 = ((f32[4,512,128]{2,1,0:T(8,128)}), f32[4,512,128]{2,1,0:T(8,128)S(1)}, u32[]{:S(2)}, u32[]{:S(2)}) async-start(f32[4,512,128]{2,1,0:T(8,128)} %pad_maximum_fusion.1), calls=%async_computation.3 | async-start | bytes 2097152 | tf_op jit(solution)/shard_map/all_to_all | solution.py:117
  87.7 3.1 %copy-start.7 = (bf16[1024,1024]{1,0:T(8,128)(2,1)S(1)}, bf16[1024,1024]{1,0:T(8,128)(2,1)}, u32[]{:S(2)}) copy-start(bf16[1024,1024]{1,0:T(8,128)(2,1)} %fusion.36) | copy-start | bytes 6291460
  91.5 5.1 %copy-start.5 = (bf16[1024,128]{1,0:T(8,128)(2,1)S(1)}, bf16[1024,128]{1,0:T(8,128)(2,1)}, u32[]{:S(2)}) copy-start(bf16[1024,128]{1,0:T(8,128)(2,1)} %get-tuple-element.41) | copy-start | bytes 786436
  93.1 11.2 %all-to-all-start.4 = ((f32[4,264,128]{2,1,0:T(8,128)}), f32[4,264,128]{2,1,0:T(8,128)S(1)}, u32[]{:S(2)}, u32[]{:S(2)}) async-start(f32[4,264,128]{2,1,0:T(8,128)} %concatenate.141), calls=%async_computation.4 | async-start | bytes 1081344 | tf_op jit(solution)/shard_map/all_to_all | solution.py:93
  190.8 1.8 copy-start.8
  207.0 17.9 %copy-start.3 = (f32[8,128,128]{2,1,0:T(8,128)S(1)}, f32[8,128,128]{2,1,0:T(8,128)}, u32[]{:S(2)}) copy-start(f32[8,128,128]{2,1,0:T(8,128)} %copy-done.2) | copy-start | bytes 1572868
  226.8 18.8 %all-to-all-start.10 = ((f32[8,128,128]{2,1,0:T(8,128)}), f32[8,128,128]{2,1,0:T(8,128)S(1)}, u32[]{:S(2)}, u32[]{:S(2)}) async-start(f32[8,128,128]{2,1,0:T(8,128)} %copy.38), calls=%async_computation.10 | async-start | bytes 1048576 | tf_op jit(solution)/shard_map/all_to_all | solution.py:136
  230.3 2.3 copy-start.1
  230.3 2.3 copy-start.4
  247.3 11.4 %all-to-all-start.11 = ((f32[4,256,128]{2,1,0:T(8,128)}), f32[4,256,128]{2,1,0:T(8,128)S(1)}, u32[]{:S(2)}, u32[]{:S(2)}) async-start(f32[4,256,128]{2,1,0:T(8,128)} %bitcast.57), calls=%async_computation.11 | async-start | bytes 1048576 | tf_op jit(solution)/shard_map/all_to_all | solution.py:117

commit v16 on v12

--- a/solution.py
+++ b/solution.py
@@ -109,7 +109,8 @@
     def fetch(items, partial=None, extra=None):
         chunks = [] if extra is None else [extra.reshape(shard_count, per_peer, lane_count)]
         for owned_rows, which in items:
-            owned_rows = jnp.where(jnp.isfinite(owned_rows), owned_rows, 0.0)
+            if which != 2:
+                owned_rows = jnp.where(jnp.isfinite(owned_rows), owned_rows, 0.0)
             picked = gather_rows(owned_rows, arrived[which])
             chunks.append(picked.reshape(shard_count, per_peer, lane_count))
         if partial is not None:

time: 262 us -> 262 us (level)
  no operation moved by 1% of the time
where the time goes in v16:
time: 262 us; the launch traced here: 261 us
  blocking collectives  119 us (45%)
  waiting for transfers between devices  61.4 us (23%)
  matrix products  28.8 us (11%)
  starting transfers between devices  22.5 us (9%)
  other arithmetic  15.5 us (6%)
  local copies, waits for them, and re-layouts  9.93 us (4%)
  between operations  3.35 us (1%)
    all_to_all x2, blocking collectives, to_middle(): lax.all_to_all(jnp.concatenate(pieces, axis=1), 'clique', 0, 0, tiled=True)  47.4 us
    all_to_all x1, blocking collectives, from_middle(): lax.all_to_all(jnp.concatenate(chunks, axis=1), 'clique', 0, 0, tiled=True)  29.7 us
    all_to_all x2, waiting for transfers between devices, from_middle(): lax.all_to_all(jnp.concatenate(chunks, axis=1), 'clique', 0, 0, tiled=True)  25 us
    all_to_all x2, blocking collectives, send(): lax.all_to_all(jnp.concatenate(chunks, axis=1), 'shard', 0, 0, tiled=True)  24.9 us
    all_to_all x1, blocking collectives, fetch(): lax.all_to_all(jnp.concatenate(chunks, axis=1), 'shard', 0, 0, tiled=True)  17.4 us
    dot_general x16, matrix products, split_dot(): lax.dot_general(one_hot, parts, (((contract,), (0,)), ((), ())), preferre...  17.3 us
    all_to_all x1, waiting for transfers between devices, to_middle(): lax.all_to_all(jnp.concatenate(pieces, axis=1), 'clique', 0, 0, tiled=True)  15.3 us
    all_to_all x2, waiting for transfers between devices, fetch(): lax.all_to_all(jnp.concatenate(chunks, axis=1), 'shard', 0, 0, tiled=True)  14.3 us
  transfers between devices with their start and end apart: 6, of which 6 were waited for; matrix products, arithmetic and copies ran while one was open for 5% of the time, Pallas kernels for 0%

profile of v16, /device:TPU:0, one launch (start us, length us, event | category | flops | bytes accessed | tf_op | source)
XLA Modules:
  0.0 260.7 jit_solution(7648280120858998971)
XLA Ops:
  1.9 3.3 %fusion = f32[4,1024,2]{1,2,0:T(2,128)S(1)} fusion(s32[4,1024]{1,0:T(4,128)S(1)} %add_add_fusion, bf16[4,1024,1]{1,2,0:T(2,128)(2,1)S(1)} %fusion.120, bf16[4,1024,1]{1,2,0:T(2,128)(2,1)S(1)} %get-tuple-element.11), kind=kOutput, calls=%fused_computation.1 | convolution fusion | flops 21004288 | bytes 65536 | tf_op jit(solution)/shard_map/lbi,lbh->lih/dot_general | solution.py:72
  7.9 14.1 %all_to_all.60 = f32[4,272,128]{2,1,0:T(8,128)S(1)} all-to-all(f32[4,272,128]{2,1,0:T(8,128)S(1)} %pad_maximum_fusion.3), channel_id=1, replica_groups=mesh['clique'=8,'shard'=4] {'shard'}, dimensions={0} | all-to-all | bytes 1114112 | tf_op jit(solution)/shard_map/all_to_all | solution.py:93
  23.5 0.8 fusion.13
  24.3 0.9 fusion.66
  25.2 4.9 %all-to-all-start.1 = ((f32[8,128,128]{2,1,0:T(8,128)}), f32[8,128,128]{2,1,0:T(8,128)S(1)}, u32[]{:S(2)}, u32[]{:S(2)}) async-start(f32[8,128,128]{2,1,0:T(8,128)} %bitcast.32), calls=%async_computation.1 | async-start | bytes 1048576 | tf_op jit(solution)/shard_map/all_to_all | solution.py:130
  30.1 15.3 %all-to-all-done.1 = f32[8,128,128]{2,1,0:T(8,128)S(1)} async-done(((f32[8,128,128]{2,1,0:T(8,128)}), f32[8,128,128]{2,1,0:T(8,128)S(1)}, u32[]{:S(2)}, u32[]{:S(2)}) %all-to-all-start.1) | async-done | bytes 524320 | tf_op jit(solution)/shard_map/all_to_all | solution.py:130
  46.1 0.9 copy.30
  47.0 3.5 %all-to-all-start.2 = ((f32[8,128,128]{2,1,0:T(8,128)}), f32[8,128,128]{2,1,0:T(8,128)S(1)}, u32[]{:S(2)}, u32[]{:S(2)}) async-start(f32[8,128,128]{2,1,0:T(8,128)} %copy.30), calls=%async_computation.2 | async-start | bytes 1048576 | tf_op jit(solution)/shard_map/all_to_all | solution.py:137
  51.4 14.4 %all-to-all-done.2 = f32[8,128,128]{2,1,0:T(8,128)S(1)} async-done(((f32[8,128,128]{2,1,0:T(8,128)}), f32[8,128,128]{2,1,0:T(8,128)S(1)}, u32[]{:S(2)}, u32[]{:S(2)}) %all-to-all-start.2) | async-done | bytes 524320 | tf_op jit(solution)/shard_map/all_to_all | solution.py:137
  65.9 0.8 fusion.12
  66.8 1.0 pad_maximum_fusion.1
  67.8 3.7 %all-to-all-start.3 = ((f32[4,512,128]{2,1,0:T(8,128)}), f32[4,512,128]{2,1,0:T(8,128)S(1)}, u32[]{:S(2)}, u32[]{:S(2)}) async-start(f32[4,512,128]{2,1,0:T(8,128)} %pad_maximum_fusion.1), calls=%async_computation.3 | async-start | bytes 2097152 | tf_op jit(solution)/shard_map/all_to_all | solution.py:118
  71.5 2.0 fusion.2
  73.6 3.7 %fusion.36 = bf16[1024,1024]{1,0:T(8,128)(2,1)} fusion(s32[1024]{0:T(1024)S(1)} %bitcast.182, s32[1024]{0:T(1024)S(1)} %bitcast.171), kind=kOutput, calls=%fused_computation.49 | convolution fusion | flops 2150629376 | bytes 2105344 | tf_op jit(solution)/shard_map/dot_general | solution.py:74
  77.3 7.6 %all-to-all-done.3 = f32[4,512,128]{2,1,0:T(8,128)S(1)} async-done(((f32[4,512,128]{2,1,0:T(8,128)}), f32[4,512,128]{2,1,0:T(8,128)S(1)}, u32[]{:S(2)}, u32[]{:S(2)}) %all-to-all-start.3) | async-done | bytes 1048608 | tf_op jit(solution)/shard_map/all_to_all | solution.py:118
  84.9 0.9 fusion.165
  85.8 1.2 copy.43
  87.1 1.5 reduce-precision_convert_fusion.9
  90.5 1.5 concatenate.141
  91.9 3.5 %all-to-all-start.4 = ((f32[4,264,128]{2,1,0:T(8,128)}), f32[4,264,128]{2,1,0:T(8,128)S(1)}, u32[]{:S(2)}, u32[]{:S(2)}) async-start(f32[4,264,128]{2,1,0:T(8,128)} %concatenate.141), calls=%async_computation.4 | async-start | bytes 1081344 | tf_op jit(solution)/shard_map/all_to_all | solution.py:93
  95.4 0.8 fusion.14
  96.3 6.8 %all-to-all-done.4 = f32[4,264,128]{2,1,0:T(8,128)S(1)} async-done(((f32[4,264,128]{2,1,0:T(8,128)}), f32[4,264,128]{2,1,0:T(8,128)S(1)}, u32[]{:S(2)}, u32[]{:S(2)}) %all-to-all-start.4) | async-done | bytes 540704 | tf_op jit(solution)/shard_map/all_to_all | solution.py:93
  104.5 0.8 fusion.11
  105.4 29.6 %all_to_all.61 = f32[8,256,128]{2,1,0:T(8,128)S(1)} all-to-all(f32[8,256,128]{2,1,0:T(8,128)S(1)} %pad_maximum_fusion.2), channel_id=1, replica_groups=mesh['clique'=8,'shard'=4] {'clique'}, dimensions={0} | all-to-all | bytes 2097152 | tf_op jit(solution)/shard_map/all_to_all | solution.py:130
  135.1 1.1 fusion.117
  136.2 0.9 convolution_divide_fusion.1
  137.7 29.7 %all_to_all.62 = f32[8,264,128]{2,1,0:T(8,128)S(1)} all-to-all(f32[8,264,128]{2,1,0:T(8,128)S(1)} %copy.35), channel_id=1, replica_groups=mesh['clique'=8,'shard'=4] {'clique'}, dimensions={0} | all-to-all | bytes 2162688 | tf_op jit(solution)/shard_map/all_to_all | solution.py:137
  168.8 0.8 fusion.10
  169.8 0.8 fusion.15
  170.9 17.4 %all_to_all.63 = f32[4,520,128]{2,1,0:T(8,128)S(1)} all-to-all(f32[4,520,128]{2,1,0:T(8,128)S(1)} %maximum_maximum_fusion), channel_id=1, replica_groups=mesh['clique'=8,'shard'=4] {'shard'}, dimensions={0} | all-to-all | bytes 2129920 | tf_op jit(solution)/shard_map/all_to_all | solution.py:118
  189.6 0.9 fusion.163
  190.6 0.8 copy-done.7
  193.4 10.7 %all_to_all.64 = f32[4,264,128]{2,1,0:T(8,128)S(1)} all-to-all(f32[4,264,128]{2,1,0:T(8,128)S(1)} %concatenate.151), channel_id=1, replica_groups=mesh['clique'=8,'shard'=4] {'shard'}, dimensions={0} | all-to-all | bytes 1081344 | tf_op jit(solution)/shard_map/all_to_all | solution.py:93
  205.5 0.8 fusion.17
  206.4 17.9 %all_to_all.65 = f32[8,128,128]{2,1,0:T(8,128)S(1)} all-to-all(f32[8,128,128]{2,1,0:T(8,128)S(1)} %bitcast.162), channel_id=1, replica_groups=mesh['clique'=8,'shard'=4] {'clique'}, dimensions={0} | all-to-all | bytes 1048576 | tf_op jit(solution)/shard_map/all_to_all | solution.py:130
  224.3 0.9 convolution_divide_fusion
  225.2 0.9 copy.38
  226.0 3.5 %all-to-all-start.10 = ((f32[8,128,128]{2,1,0:T(8,128)}), f32[8,128,128]{2,1,0:T(8,128)S(1)}, u32[]{:S(2)}, u32[]{:S(2)}) async-start(f32[8,128,128]{2,1,0:T(8,128)} %copy.38), calls=%async_computation.10 | async-start | bytes 1048576 | tf_op jit(solution)/shard_map/all_to_all | solution.py:137
  229.6 2.3 fusion.4
  232.0 2.2 fusion.7
  234.2 10.6 %all-to-all-done.10 = f32[8,128,128]{2,1,0:T(8,128)S(1)} async-done(((f32[8,128,128]{2,1,0:T(8,128)}), f32[8,128,128]{2,1,0:T(8,128)S(1)}, u32[]{:S(2)}, u32[]{:S(2)}) %all-to-all-start.10) | async-done | bytes 524320 | tf_op jit(solution)/shard_map/all_to_all | solution.py:137
  244.9 0.8 fusion.16
  245.7 0.8 slice_add_fusion.1
  246.6 3.5 %all-to-all-start.11 = ((f32[4,256,128]{2,1,0:T(8,128)}), f32[4,256,128]{2,1,0:T(8,128)S(1)}, u32[]{:S(2)}, u32[]{:S(2)}) async-start(f32[4,256,128]{2,1,0:T(8,128)} %bitcast.57), calls=%async_computation.11 | async-start | bytes 1048576 | tf_op jit(solution)/shard_map/all_to_all | solution.py:118
  250.1 1.3 fusion.64
  251.4 6.7 %all-to-all-done.11 = f32[4,256,128]{2,1,0:T(8,128)S(1)} async-done(((f32[4,256,128]{2,1,0:T(8,128)}), f32[4,256,128]{2,1,0:T(8,128)S(1)}, u32[]{:S(2)}, u32[]{:S(2)}) %all-to-all-start.11) | async-done | bytes 524320 | tf_op jit(solution)/shard_map/all_to_all | solution.py:118
  258.1 1.3 fusion.5
  259.5 1.2 maximum_bitcast_fusion
  (88 shorter events, 16.2 us)
Async XLA Ops:
  1.9 3.4 %copy-start.3 = (f32[3,1,1024,128]{3,2,1,0:T(8,128)S(1)}, f32[3,1,1024,128]{3,2,1,0:T(8,128)}, u32[]{:S(2)}) copy-start(f32[3,1,1024,128]{3,2,1,0:T(8,128)} %param.4) | copy-start | bytes 4718596
  24.3 5.7 %copy-start.5 = (s32[2,8]{1,0:T(2,128)S(1)}, s32[2,8]{1,0:T(2,128)}, u32[]{:S(2)}) copy-start(s32[2,8]{1,0:T(2,128)} %param.7) | copy-start | bytes 196
  25.2 20.2 %all-to-all-start.1 = ((f32[8,128,128]{2,1,0:T(8,128)}), f32[8,128,128]{2,1,0:T(8,128)S(1)}, u32[]{:S(2)}, u32[]{:S(2)}) async-start(f32[8,128,128]{2,1,0:T(8,128)} %bitcast.32), calls=%async_computation.1 | async-start | bytes 1048576 | tf_op jit(solution)/shard_map/all_to_all | solution.py:130
  45.4 5.2 %copy-start = (f32[8,128,128]{2,1,0:T(8,128)}, f32[8,128,128]{2,1,0:T(8,128)S(1)}, u32[]{:S(2)}) copy-start(f32[8,128,128]{2,1,0:T(8,128)S(1)} %all-to-all-done.1) | copy-start | bytes 1572868
  47.0 18.8 %all-to-all-start.2 = ((f32[8,128,128]{2,1,0:T(8,128)}), f32[8,128,128]{2,1,0:T(8,128)S(1)}, u32[]{:S(2)}, u32[]{:S(2)}) async-start(f32[8,128,128]{2,1,0:T(8,128)} %copy.30), calls=%async_computation.2 | async-start | bytes 1048576 | tf_op jit(solution)/shard_map/all_to_all | solution.py:137
  67.8 17.1 %all-to-all-start.3 = ((f32[4,512,128]{2,1,0:T(8,128)}), f32[4,512,128]{2,1,0:T(8,128)S(1)}, u32[]{:S(2)}, u32[]{:S(2)}) async-start(f32[4,512,128]{2,1,0:T(8,128)} %pad_maximum_fusion.1), calls=%async_computation.3 | async-start | bytes 2097152 | tf_op jit(solution)/shard_map/all_to_all | solution.py:118
  87.0 1.9 copy-start.6
  91.9 11.2 %all-to-all-start.4 = ((f32[4,264,128]{2,1,0:T(8,128)}), f32[4,264,128]{2,1,0:T(8,128)S(1)}, u32[]{:S(2)}, u32[]{:S(2)}) async-start(f32[4,264,128]{2,1,0:T(8,128)} %concatenate.141), calls=%async_computation.4 | async-start | bytes 1081344 | tf_op jit(solution)/shard_map/all_to_all | solution.py:93
  189.6 1.8 copy-start.7
  190.6 1.5 copy-start.4
  206.3 17.9 %copy-start.1 = (f32[8,128,128]{2,1,0:T(8,128)S(1)}, f32[8,128,128]{2,1,0:T(8,128)}, u32[]{:S(2)}) copy-start(f32[8,128,128]{2,1,0:T(8,128)} %copy-done) | copy-start | bytes 1572868
  226.0 18.8 %all-to-all-start.10 = ((f32[8,128,128]{2,1,0:T(8,128)}), f32[8,128,128]{2,1,0:T(8,128)S(1)}, u32[]{:S(2)}, u32[]{:S(2)}) async-start(f32[8,128,128]{2,1,0:T(8,128)} %copy.38), calls=%async_computation.10 | async-start | bytes 1048576 | tf_op jit(solution)/shard_map/all_to_all | solution.py:137
  229.5 2.3 copy-start.2
  246.6 11.4 %all-to-all-start.11 = ((f32[4,256,128]{2,1,0:T(8,128)}), f32[4,256,128]{2,1,0:T(8,128)S(1)}, u32[]{:S(2)}, u32[]{:S(2)}) async-start(f32[4,256,128]{2,1,0:T(8,128)} %bitcast.57), calls=%async_computation.11 | async-start | bytes 1048576 | tf_op jit(solution)/shard_map/all_to_all | solution.py:118
